TPU v7x, 768 devices: a whole 4x8x12 slice. The times are simulated.
768 devices in a mesh: sect: 8 (over x, core), tile: 96 (over z, y).
Axes of the slice: x: 4, y: 8, z: 12, core: 2. Of those that a mesh axis runs over, the one named last changes fastest.
Arguments:
- spectrum: float32 [1296, 768, 128], P('sect', 'tile'), may hold values from 0.05 to 1
- courant: float32 [36], replicated, may hold values from 0.1 to 0.45
- group_ratio: float32 [36], replicated, may hold values from 0.5 to 1
- ocean_currents: float32 [2, 196608], P(None, 'tile'), may hold values from -0.15 to 0.15
- elevation: float32 [196608], P('tile'), may hold values from -0.5 to 0.5
- sea_mask: int32 [768, 128], P('tile'), may hold values 0 or 1
- owner_tile: int32 [98304, 1], P('tile'), may hold values from 0 to 95; in each aligned block of 1024 rows (0 to 1023, 1024 to 2047, ...) at most 22 rows name the same one
- ocean_slot: int32 [98304], P('tile'), may hold values from 0 to 2047
Outputs:
- new_spectrum: float32 [1296, 768, 128], P('sect', 'tile')
- ocean_stress: float32 [3, 196608], P(None, 'tile')
Inputs may be any that keep to these rules, and one draw needn't show every extreme that they name: `owner_tile`: among the wave cells of one tile at most 22 name the same owner tile, a bound that some block reaches of them.
All inputs are finite; a program needn't handle non-finite values. No bound on the sum of `sea_mask` on one device may be relied on, other than what follows from the above.
Results may differ from a plain program's by a relative error of at most 0.00011.
Values sent between devices are 32-bit elements; how exact they have to be, the bound alone decides.
No kernel may reach another device: no remote copies, remote signals or barrier semaphores. Data moves between devices by JAX's collectives and lax.ppermute only.
A program may use at most 32 MiB of HBM per device.

v0:
```python
import math

import jax
import jax.numpy as jnp
from jax import lax
from jax.sharding import PartitionSpec as P

NDIR = 36
NFREQ = 36
STEPS = 4


def with_halo(x, sides, width):
    for axis, dim in sides:
        size, length = (lax.axis_size(axis), x.shape[dim])
        up = [(i, (i + 1) % size) for i in range(size - 1)]
        down = [(j, i) for i, j in up]
        last = lax.slice_in_dim(x, length - width, length, axis=dim)
        leading = lax.slice_in_dim(x, 0, width, axis=dim)
        before = lax.ppermute(last, axis, up)
        after = lax.ppermute(leading, axis, down)
        x = jnp.concatenate([before, x, after], axis=dim)
    return x


def advance(energy, flow_fields, speed_x, speed_y):
    vel_x = speed_x + flow_fields[0]
    vel_y = speed_y + flow_fields[1]
    middle = energy[:, 1:-1]
    mid_vel = vel_x[:, 1:-1]
    face_x = 0.5 * (mid_vel + jnp.roll(mid_vel, -1, axis=2))
    east_side = jnp.roll(middle, -1, axis=2)
    flux_x = jnp.maximum(face_x, 0.0) * middle + jnp.minimum(face_x, 0.0) * east_side
    div_x = flux_x - jnp.roll(flux_x, 1, axis=2)
    face_y = 0.5 * (vel_y[:, :-1] + vel_y[:, 1:])
    flux_y = jnp.maximum(face_y, 0.0) * energy[:, :-1] + jnp.minimum(face_y, 0.0) * energy[:, 1:]
    div_y = flux_y[:, 1:] - flux_y[:, :-1]
    return flow_fields[2, 1:-1] * (middle - div_x - div_y)


def local(
    spectrum, courant, group_ratio, ocean_currents, elevation, sea_mask, owner_tile, ocean_slot
):
    bin_count, row_count, columns = spectrum.shape
    cell_count = row_count * columns
    tile_count = lax.axis_size("tile")
    capacity = 2 * ((cell_count + tile_count - 1) // tile_count)
    ocean_cells = elevation.shape[0]
    first_bin = lax.axis_index("sect") * bin_count
    bin_ids = first_bin + jnp.arange(bin_count, dtype=jnp.int32)
    dir_ids = bin_ids // NFREQ
    freq_ids = bin_ids % NFREQ
    freq_pick = (freq_ids[:, None] == jnp.arange(NFREQ, dtype=jnp.int32)[None, :]).astype(
        jnp.float32
    )
    group_speed = jnp.sum(freq_pick * courant[None, :], 1)
    ratio_bin = jnp.sum(freq_pick * group_ratio[None, :], 1)
    angles = (dir_ids.astype(jnp.float32) + 0.5) * (2.0 * math.pi / NDIR)
    cos_dir = jnp.cos(angles)
    sin_dir = jnp.sin(angles)
    speed_x = (group_speed * cos_dir)[:, None, None]
    speed_y = (group_speed * sin_dir)[:, None, None]
    owners = owner_tile[:, 0]
    one_hot = (owners[:, None] == jnp.arange(tile_count, dtype=jnp.int32)[None, :]).astype(
        jnp.int32
    )
    earlier = jnp.cumsum(one_hot, 0) - one_hot
    rank_in = jnp.sum(earlier * one_hot, 1)
    position = owners * capacity + rank_in
    requests = jnp.full((tile_count * capacity,), -1, jnp.int32).at[position].set(ocean_slot)
    asked_slots = lax.all_to_all(
        requests.reshape(tile_count, capacity), "tile", split_axis=0, concat_axis=0, tiled=True
    )
    is_valid = asked_slots >= 0
    slot_index = jnp.where(is_valid, asked_slots, 0)
    surface = jnp.concatenate([ocean_currents, elevation[None]], 0)
    answer = jnp.where(is_valid[None], surface[:, slot_index], 0.0)
    returned = lax.all_to_all(answer, "tile", split_axis=1, concat_axis=1, tiled=True)
    at_cells = returned.reshape(3, tile_count * capacity)[:, position]
    sea_float = sea_mask.astype(jnp.float32)
    flow_fields = jnp.concatenate([at_cells[:2].reshape(2, row_count, columns), sea_float[None]], 0)
    energy = spectrum
    for sub_step in range(STEPS):
        extended = with_halo(jnp.concatenate([energy, flow_fields], 0), (("tile", 1),), 1)
        energy = advance(extended[:bin_count], extended[bin_count:], speed_x, speed_y)
    weights = jnp.stack(
        [
            ratio_bin * (1.0 + cos_dir * cos_dir) - 0.5,
            ratio_bin * cos_dir * sin_dir,
            ratio_bin * (1.0 + sin_dir * sin_dir) - 0.5,
        ],
        0,
    ) * (4.0 / (NDIR * NFREQ))
    partial_value = jnp.dot(
        weights, energy.reshape(bin_count, cell_count), precision=lax.Precision.HIGHEST
    )
    partial_value = partial_value * ((1.0 + at_cells[2]) * sea_float.reshape(-1))
    partial_value = lax.psum(partial_value, "sect")
    packed = jnp.zeros((3, tile_count * capacity), jnp.float32).at[:, position].set(partial_value)
    arrived = lax.all_to_all(
        packed.reshape(3, tile_count, capacity), "tile", split_axis=1, concat_axis=1, tiled=True
    )
    flat_index = slot_index.reshape(-1)
    weight = is_valid.reshape(-1).astype(jnp.float32)
    totals = (
        jnp.zeros((3, ocean_cells), jnp.float32)
        .at[:, flat_index]
        .add(arrived.reshape(3, -1) * weight[None])
    )
    counts = jnp.zeros((ocean_cells,), jnp.float32).at[flat_index].add(weight)
    return (energy, totals / jnp.maximum(counts, 1.0)[None])


def solution(mesh):
    in_specs = (
        P("sect", "tile", None),
        P(),
        P(),
        P(None, "tile"),
        P("tile"),
        P("tile", None),
        P("tile", None),
        P("tile"),
    )
    out_specs = (P("sect", "tile", None), P(None, "tile"))
    return jax.shard_map(local, mesh=mesh, in_specs=in_specs, out_specs=out_specs, check_vma=False)
```

profile of v0, /device:TPU:8, one launch (start us, length us, event | category | flops | bytes accessed | tf_op | source)
XLA Modules:
  0.0 240.1 jit_solution(13609012161803773219)
XLA Ops:
  0.6 0.7 fusion.61
  1.4 27.0 %reduce-window.6 = s32[96,8,128]{2,1,0:T(8,128)S(1)} reduce-window(s32[96,8,128]{2,1,0:T(8,128)S(1)} %fusion.61, s32[]{:T(128)} %constant.22.clone.1), window={size=1x1x128 pad=0_0x0_0x127_0}, to_apply=%region_1.2 | reduce-window | flops 12484608 | bytes 786436 | tf_op jit(solution)/shard_map/reduce-window
  29.2 4.5 %scatter_custom_fusion = s32[2112]{0:T(1024)S(1)} fusion(s32[1024]{0:T(1024)S(1)} %bitcast.94, s32[1024]{0:T(1024)} %param.15, s32[]{:T(128)} %constant.25.clone.1), kind=kCustom, calls=%fused_computation.157 | custom fusion | bytes 8960 | tf_op jit(solution)/shard_map/scatter | solution.py:70
  33.7 0.8 all_to_all.16
  34.4 21.8 %all-to-all-start = ((s32[96,1,22]{2,1,0:T(1,128)}), s32[96,1,22]{2,1,0:T(1,128)S(1)}, u32[]{:S(2)}, u32[]{:S(2)}) async-start(s32[96,1,22]{2,1,0:T(1,128)} %bitcast.6), calls=%async_computation | async-start | bytes 98304 | tf_op jit(solution)/shard_map/all_to_all | solution.py:71
  56.7 13.1 %all-to-all-done = s32[96,1,22]{2,1,0:T(1,128)S(1)} async-done(((s32[96,1,22]{2,1,0:T(1,128)}), s32[96,1,22]{2,1,0:T(1,128)S(1)}, u32[]{:S(2)}, u32[]{:S(2)}) %all-to-all-start) | async-done | bytes 8480 | tf_op jit(solution)/shard_map/all_to_all | solution.py:71
  70.2 4.0 %gather_fusion = f32[2112,3]{1,0:T(8,128)S(1)} fusion(f32[3,2048]{0,1:T(8,128)S(1)} %copy.112, s32[3072]{0:T(1024)S(1)} %pad_clamp_fusion), kind=kCustom, calls=%fused_computation | custom fusion | bytes 59136 | tf_op jit(solution)/shard_map/gather | solution.py:77
  74.7 0.8 copy.114
  75.5 6.5 %all-to-all-start.1 = ((f32[3,96,22]{2,0,1:T(4,128)}), f32[3,96,22]{2,0,1:T(4,128)S(1)}, u32[]{:S(2)}, u32[]{:S(2)}) async-start(f32[3,96,22]{2,0,1:T(4,128)} %copy.114), calls=%async_computation.1 | async-start | bytes 393216 | tf_op jit(solution)/shard_map/all_to_all | solution.py:78
  82.1 16.1 %all-to-all-done.1 = f32[3,96,22]{2,0,1:T(4,128)S(1)} async-done(((f32[3,96,22]{2,0,1:T(4,128)}), f32[3,96,22]{2,0,1:T(4,128)S(1)}, u32[]{:S(2)}, u32[]{:S(2)}) %all-to-all-start.1) | async-done | bytes 25376 | tf_op jit(solution)/shard_map/all_to_all | solution.py:78
  98.8 2.8 %gather_fusion.1 = f32[1024,3]{1,0:T(8,128)S(1)} fusion(f32[3,2112]{0,1:T(8,128)S(1)} %copy.116, s32[1024]{0:T(1024)S(1)} %broadcast_clamp_fusion), kind=kCustom, calls=%fused_computation.1 | custom fusion | bytes 28672 | tf_op jit(solution)/shard_map/gather | solution.py:79
  102.0 3.1 %collective-permute-start.1 = (f32[165,1,128]{2,0,1:T(8,128)S(1)}, f32[165,1,128]{2,0,1:T(8,128)S(1)}, u32[]{:S(2)}, u32[]{:S(2)}) collective-permute-start(f32[165,1,128]{2,0,1:T(8,128)S(1)} %copy.119), channel_id=1, source_target_pairs={{1,0},{2,1},{3,2},{4,3},{5,4},{6,5},{7,6},{8,7},{9,8},{10,9},{11,1... | collective-permute-start | bytes 253448 | tf_op jit(solution)/shard_map/ppermute | solution.py:21
  105.1 2.7 %collective-permute-start = (f32[165,1,128]{2,0,1:T(8,128)S(1)}, f32[165,1,128]{2,0,1:T(8,128)S(1)}, u32[]{:S(2)}, u32[]{:S(2)}) collective-permute-start(f32[165,1,128]{2,0,1:T(8,128)S(1)} %copy.118), channel_id=1, source_target_pairs={{0,1},{1,2},{2,3},{3,4},{4,5},{5,6},{6,7},{7,8},{8,9},{9,10},{10,1... | collective-permute-start | bytes 253448 | tf_op jit(solution)/shard_map/ppermute | solution.py:20
  108.5 3.0 %collective-permute-done = f32[165,1,128]{2,0,1:T(8,128)S(1)} collective-permute-done((f32[165,1,128]{2,0,1:T(8,128)S(1)}, f32[165,1,128]{2,0,1:T(8,128)S(1)}, u32[]{:S(2)}, u32[]{:S(2)}) %collective-permute-start) | collective-permute-done | bytes 84512 | tf_op jit(solution)/shard_map/ppermute | solution.py:20
  114.5 1.9 collective-permute-start.3
  116.4 4.1 %collective-permute-start.2 = (f32[165,1,128]{2,0,1:T(8,128)S(1)}, f32[165,1,128]{2,0,1:T(8,128)S(1)}, u32[]{:S(2)}, u32[]{:S(2)}) collective-permute-start(f32[165,1,128]{2,0,1:T(8,128)S(1)} %copy.125), channel_id=1, source_target_pairs={{0,1},{1,2},{2,3},{3,4},{4,5},{5,6},{6,7},{7,8},{8,9},{9,10},{10,1... | collective-permute-start | bytes 253448 | tf_op jit(solution)/shard_map/ppermute | solution.py:20
  121.6 0.8 reduce.7
  125.9 1.9 collective-permute-start.5
  127.8 3.9 %collective-permute-start.4 = (f32[165,1,128]{2,0,1:T(8,128)S(1)}, f32[165,1,128]{2,0,1:T(8,128)S(1)}, u32[]{:S(2)}, u32[]{:S(2)}) collective-permute-start(f32[165,1,128]{2,0,1:T(8,128)S(1)} %copy.132), channel_id=1, source_target_pairs={{0,1},{1,2},{2,3},{3,4},{4,5},{5,6},{6,7},{7,8},{8,9},{9,10},{10,1... | collective-permute-start | bytes 253448 | tf_op jit(solution)/shard_map/ppermute | solution.py:20
  131.8 12.9 %scatter_custom_fusion.3 = f32[2048]{0:T(1024)S(1)} fusion(s32[2112]{0:T(1024)S(1)} %fusion.62, f32[2112]{0:T(1024)S(1)} %reshape.305, f32[]{:T(128)} %constant.23.clone.1), kind=kCustom, calls=%fused_computation.165 | custom fusion | flops 2112 | bytes 8196 | tf_op jit(solution)/shard_map/scatter-add | solution.py:110
  148.0 2.1 collective-permute-start.7
  150.1 6.0 %collective-permute-start.6 = (f32[165,1,128]{2,0,1:T(8,128)S(1)}, f32[165,1,128]{2,0,1:T(8,128)S(1)}, u32[]{:S(2)}, u32[]{:S(2)}) collective-permute-start(f32[165,1,128]{2,0,1:T(8,128)S(1)} %copy.139), channel_id=1, source_target_pairs={{0,1},{1,2},{2,3},{3,4},{4,5},{5,6},{6,7},{7,8},{8,9},{9,10},{10,1... | collective-permute-start | bytes 253448 | tf_op jit(solution)/shard_map/ppermute | solution.py:20
  156.8 1.1 collective-permute-done.6
  159.8 0.6 fusion.19
  161.0 0.6 copy-done.1
  162.1 23.6 %psum.7 = f32[3,1024]{1,0:T(4,128)S(1)} all-reduce(f32[3,1024]{1,0:T(4,128)S(1)} %convolution_multiply_fusion), channel_id=1, replica_groups=mesh['sect'=8,'tile'=96] {'sect'}, use_global_device_ids=true, to_apply=%region_6.7 | all-reduce | flops 3072 | bytes 24576 | tf_op jit(solution)/shard_map/psum | solution.py:98
  185.8 3.4 %scatter_custom_fusion.1 = f32[3,2112]{0,1:T(8,128)S(1)} fusion(s32[1024]{0:T(1024)S(1)} %bitcast.96, f32[1024,3]{1,0:T(8,128)S(1)} %copy.146, f32[]{:T(128)} %constant.23.clone.1), kind=kCustom, calls=%fused_computation.119 | custom fusion | bytes 25348 | tf_op jit(solution)/shard_map/scatter | solution.py:99
  189.8 0.8 copy.148
  190.5 17.8 %all-to-all-start.2 = ((f32[3,96,22]{2,0,1:T(4,128)}), f32[3,96,22]{2,0,1:T(4,128)S(1)}, u32[]{:S(2)}, u32[]{:S(2)}) async-start(f32[3,96,22]{2,0,1:T(4,128)} %copy.148), calls=%async_computation.2 | async-start | bytes 393216 | tf_op jit(solution)/shard_map/all_to_all | solution.py:100
  208.3 15.4 %all-to-all-done.2 = f32[3,96,22]{2,0,1:T(4,128)S(1)} async-done(((f32[3,96,22]{2,0,1:T(4,128)}), f32[3,96,22]{2,0,1:T(4,128)S(1)}, u32[]{:S(2)}, u32[]{:S(2)}) %all-to-all-start.2) | async-done | bytes 25376 | tf_op jit(solution)/shard_map/all_to_all | solution.py:100
  224.3 14.5 %scatter_custom_fusion.2 = f32[3,2048]{0,1:T(8,128)S(1)} fusion(s32[2112]{0:T(1024)S(1)} %fusion.62, f32[2112,3]{1,0:T(8,128)S(1)} %copy.151, f32[]{:T(128)} %constant.23.clone.1), kind=kCustom, calls=%fused_computation.125 | custom fusion | flops 6336 | bytes 24580 | tf_op jit(solution)/shard_map/scatter-add | solution.py:108
  239.2 0.9 copy.152
  (135 shorter events, 19.5 us)
Async XLA Ops:
  1.3 27.7 %copy-start.2 = (s32[1024,1]{0,1:T(1,128)S(1)}, s32[1024,1]{0,1:T(1,128)}, u32[]{:S(2)}) copy-start(s32[1024,1]{0,1:T(1,128)} %param.14) | copy-start | bytes 12292
  28.4 27.9 %copy-start.5 = (s32[8,128]{1,0:T(8,128)S(1)}, s32[8,128]{1,0:T(8,128)}, u32[]{:S(2)}) copy-start(s32[8,128]{1,0:T(8,128)} %param.13) | copy-start | bytes 12292
  28.4 27.9 %copy-start.3 = (f32[2,2048]{1,0:T(2,128)S(1)}, f32[2,2048]{1,0:T(2,128)}, u32[]{:S(2)}) copy-start(f32[2,2048]{1,0:T(2,128)} %param.11) | copy-start | bytes 49156
  28.4 27.9 %copy-start.4 = (f32[2048]{0:T(1024)S(1)}, f32[2048]{0:T(1024)}, u32[]{:S(2)}) copy-start(f32[2048]{0:T(1024)} %param.12) | copy-start | bytes 24580
  34.4 35.4 %all-to-all-start = ((s32[96,1,22]{2,1,0:T(1,128)}), s32[96,1,22]{2,1,0:T(1,128)S(1)}, u32[]{:S(2)}, u32[]{:S(2)}) async-start(s32[96,1,22]{2,1,0:T(1,128)} %bitcast.6), calls=%async_computation | async-start | bytes 98304 | tf_op jit(solution)/shard_map/all_to_all | solution.py:71
  74.1 7.9 %copy-start.6 = (f32[36]{0:T(128)S(1)}, f32[36]{0:T(128)}, u32[]{:S(2)}) copy-start(f32[36]{0:T(128)} %param.10) | copy-start | bytes 436
  74.2 7.9 %copy-start.7 = (f32[36]{0:T(128)S(1)}, f32[36]{0:T(128)}, u32[]{:S(2)}) copy-start(f32[36]{0:T(128)} %param.9) | copy-start | bytes 436
  75.5 26.3 %copy-start = (f32[162,8,128]{2,1,0:T(8,128)S(1)}, f32[162,8,128]{2,1,0:T(8,128)}, u32[]{:S(2)}) copy-start(f32[162,8,128]{2,1,0:T(8,128)} %param.8) | copy-start | bytes 1990660
  75.5 22.7 %all-to-all-start.1 = ((f32[3,96,22]{2,0,1:T(4,128)}), f32[3,96,22]{2,0,1:T(4,128)S(1)}, u32[]{:S(2)}, u32[]{:S(2)}) async-start(f32[3,96,22]{2,0,1:T(4,128)} %copy.114), calls=%async_computation.1 | async-start | bytes 393216 | tf_op jit(solution)/shard_map/all_to_all | solution.py:78
  102.0 6.4 %collective-permute-start.1 = (f32[165,1,128]{2,0,1:T(8,128)S(1)}, f32[165,1,128]{2,0,1:T(8,128)S(1)}, u32[]{:S(2)}, u32[]{:S(2)}) collective-permute-start(f32[165,1,128]{2,0,1:T(8,128)S(1)} %copy.119), channel_id=1, source_target_pairs={{1,0},{2,1},{3,2},{4,3},{5,4},{6,5},{7,6},{8,7},{9,8},{10,9},{11,1... | collective-permute-start | bytes 253448 | tf_op jit(solution)/shard_map/ppermute | solution.py:21
  105.1 6.4 %collective-permute-start = (f32[165,1,128]{2,0,1:T(8,128)S(1)}, f32[165,1,128]{2,0,1:T(8,128)S(1)}, u32[]{:S(2)}, u32[]{:S(2)}) collective-permute-start(f32[165,1,128]{2,0,1:T(8,128)S(1)} %copy.118), channel_id=1, source_target_pairs={{0,1},{1,2},{2,3},{3,4},{4,5},{5,6},{6,7},{7,8},{8,9},{9,10},{10,1... | collective-permute-start | bytes 253448 | tf_op jit(solution)/shard_map/ppermute | solution.py:20
  114.5 8.3 %collective-permute-start.3 = (f32[165,1,128]{2,0,1:T(8,128)S(1)}, f32[165,1,128]{2,0,1:T(8,128)S(1)}, u32[]{:S(2)}, u32[]{:S(2)}) collective-permute-start(f32[165,1,128]{2,0,1:T(8,128)S(1)} %copy.126), channel_id=1, source_target_pairs={{1,0},{2,1},{3,2},{4,3},{5,4},{6,5},{7,6},{8,7},{9,8},{10,9},{11,1... | collective-permute-start | bytes 253448 | tf_op jit(solution)/shard_map/ppermute | solution.py:21
  116.4 6.4 %collective-permute-start.2 = (f32[165,1,128]{2,0,1:T(8,128)S(1)}, f32[165,1,128]{2,0,1:T(8,128)S(1)}, u32[]{:S(2)}, u32[]{:S(2)}) collective-permute-start(f32[165,1,128]{2,0,1:T(8,128)S(1)} %copy.125), channel_id=1, source_target_pairs={{0,1},{1,2},{2,3},{3,4},{4,5},{5,6},{6,7},{7,8},{8,9},{9,10},{10,1... | collective-permute-start | bytes 253448 | tf_op jit(solution)/shard_map/ppermute | solution.py:20
  125.9 19.0 %collective-permute-start.5 = (f32[165,1,128]{2,0,1:T(8,128)S(1)}, f32[165,1,128]{2,0,1:T(8,128)S(1)}, u32[]{:S(2)}, u32[]{:S(2)}) collective-permute-start(f32[165,1,128]{2,0,1:T(8,128)S(1)} %copy.133), channel_id=1, source_target_pairs={{1,0},{2,1},{3,2},{4,3},{5,4},{6,5},{7,6},{8,7},{9,8},{10,9},{11,1... | collective-permute-start | bytes 253448 | tf_op jit(solution)/shard_map/ppermute | solution.py:21
  127.8 17.2 %collective-permute-start.4 = (f32[165,1,128]{2,0,1:T(8,128)S(1)}, f32[165,1,128]{2,0,1:T(8,128)S(1)}, u32[]{:S(2)}, u32[]{:S(2)}) collective-permute-start(f32[165,1,128]{2,0,1:T(8,128)S(1)} %copy.132), channel_id=1, source_target_pairs={{0,1},{1,2},{2,3},{3,4},{4,5},{5,6},{6,7},{7,8},{8,9},{9,10},{10,1... | collective-permute-start | bytes 253448 | tf_op jit(solution)/shard_map/ppermute | solution.py:20
  148.0 8.7 %collective-permute-start.7 = (f32[165,1,128]{2,0,1:T(8,128)S(1)}, f32[165,1,128]{2,0,1:T(8,128)S(1)}, u32[]{:S(2)}, u32[]{:S(2)}) collective-permute-start(f32[165,1,128]{2,0,1:T(8,128)S(1)} %copy.140), channel_id=1, source_target_pairs={{1,0},{2,1},{3,2},{4,3},{5,4},{6,5},{7,6},{8,7},{9,8},{10,9},{11,1... | collective-permute-start | bytes 253448 | tf_op jit(solution)/shard_map/ppermute | solution.py:21
  150.1 7.8 %collective-permute-start.6 = (f32[165,1,128]{2,0,1:T(8,128)S(1)}, f32[165,1,128]{2,0,1:T(8,128)S(1)}, u32[]{:S(2)}, u32[]{:S(2)}) collective-permute-start(f32[165,1,128]{2,0,1:T(8,128)S(1)} %copy.139), channel_id=1, source_target_pairs={{0,1},{1,2},{2,3},{3,4},{4,5},{5,6},{6,7},{7,8},{8,9},{9,10},{10,1... | collective-permute-start | bytes 253448 | tf_op jit(solution)/shard_map/ppermute | solution.py:20
  160.8 0.8 copy-start.1
  190.5 33.2 %all-to-all-start.2 = ((f32[3,96,22]{2,0,1:T(4,128)}), f32[3,96,22]{2,0,1:T(4,128)S(1)}, u32[]{:S(2)}, u32[]{:S(2)}) async-start(f32[3,96,22]{2,0,1:T(4,128)} %copy.148), calls=%async_computation.2 | async-start | bytes 393216 | tf_op jit(solution)/shard_map/all_to_all | solution.py:100
where the time goes:
time: 241 us; the launch traced here: 240 us
  starting transfers between devices  71.8 us (30%)
  other arithmetic  65.9 us (27%)
  waiting for transfers between devices  49 us (20%)
  local copies, waits for them, and re-layouts  27.8 us (12%)
  blocking collectives  23.6 us (10%)
    another operation x3, other arithmetic  27.2 us
    psum x1, blocking collectives, local(): partial_value = lax.psum(partial_value, 'sect')  23.6 us
    all_to_all x1, starting transfers between devices, local(): lax.all_to_all(requests.reshape(tile_count, capacity), 'tile', split_axis...  21.8 us
    all_to_all x1, starting transfers between devices, local(): lax.all_to_all(packed.reshape(3, tile_count, capacity), 'tile', split_axi...  17.8 us
    ppermute x4, starting transfers between devices, with_halo(): before = lax.ppermute(last, axis, up)  16.7 us
    all_to_all x1, waiting for transfers between devices, local(): lax.all_to_all(answer, 'tile', split_axis=1, concat_axis=1, tiled=True)  16.1 us
    all_to_all x1, waiting for transfers between devices, local(): lax.all_to_all(packed.reshape(3, tile_count, capacity), 'tile', split_axi...  15.4 us
    scatter-add x1, other arithmetic, local(): totals = jnp.zeros((3, ocean_cells), jnp.float32).at[:, flat_index].add(a...  14.5 us
  transfers between devices with their start and end apart: 11, of which 6 were waited for; matrix products, arithmetic and copies ran while one was open for 7% of the time, Pallas kernels for 0%

commit v1 on v0

--- a/solution.py
+++ b/solution.py
@@ -61,11 +61,9 @@
     speed_x = (group_speed * cos_dir)[:, None, None]
     speed_y = (group_speed * sin_dir)[:, None, None]
     owners = owner_tile[:, 0]
-    one_hot = (owners[:, None] == jnp.arange(tile_count, dtype=jnp.int32)[None, :]).astype(
-        jnp.int32
-    )
-    earlier = jnp.cumsum(one_hot, 0) - one_hot
-    rank_in = jnp.sum(earlier * one_hot, 1)
+    cell_ids = jnp.arange(owners.shape[0], dtype=jnp.int32)
+    same_before = (owners[None, :] == owners[:, None]) & (cell_ids[None, :] < cell_ids[:, None])
+    rank_in = jnp.sum(same_before.astype(jnp.int32), 1)
     position = owners * capacity + rank_in
     requests = jnp.full((tile_count * capacity,), -1, jnp.int32).at[position].set(ocean_slot)
     asked_slots = lax.all_to_all(
@@ -79,10 +77,11 @@
     at_cells = returned.reshape(3, tile_count * capacity)[:, position]
     sea_float = sea_mask.astype(jnp.float32)
     flow_fields = jnp.concatenate([at_cells[:2].reshape(2, row_count, columns), sea_float[None]], 0)
-    energy = spectrum
+    extended = with_halo(jnp.concatenate([spectrum, flow_fields], 0), (("tile", 1),), STEPS)
+    energy = extended[:bin_count]
     for sub_step in range(STEPS):
-        extended = with_halo(jnp.concatenate([energy, flow_fields], 0), (("tile", 1),), 1)
-        energy = advance(extended[:bin_count], extended[bin_count:], speed_x, speed_y)
+        flows_now = extended[bin_count:, sub_step : extended.shape[1] - sub_step]
+        energy = advance(energy, flows_now, speed_x, speed_y)
     weights = jnp.stack(
         [
             ratio_bin * (1.0 + cos_dir * cos_dir) - 0.5,

time: 241 us -> 185 us (0.77)
  starting transfers between devices: 71.8 us -> 42.9 us
  other arithmetic: 65.9 us -> 45.2 us
  waiting for transfers between devices: 49 us -> 42.6 us
    another operation x3 -> x0, other arithmetic: 27.2 us -> none
    ppermute x4 -> x1, starting transfers between devices: 16.7 us -> 2.73 us  [with_halo(): before = lax.ppermute(last, axis, up)]
    all_to_all x1, starting transfers between devices: 17.8 us -> 8.84 us  [local(): lax.all_to_all(packed.reshape(3, tile_count, capacity), 'tile', split_axi...]
    ppermute x4 -> x1, starting transfers between devices: 9.02 us -> 3.11 us  [with_halo(): after = lax.ppermute(leading, axis, down)]
    ppermute x4 -> x1, waiting for transfers between devices: 4.18 us -> 0.01 us  [with_halo(): before = lax.ppermute(last, axis, up)]
  transfers between devices with their start and end apart: 11 -> 5, of which waited for: 6 -> 3; matrix products, arithmetic and copies ran while one was open for 7% -> 11% of each run, Pallas kernels for 0% -> 0%
where the time goes in v1:
time: 185 us
  other arithmetic  45.2 us (24%)
  starting transfers between devices  42.9 us (23%)
  waiting for transfers between devices  42.6 us (23%)
  local copies, waits for them, and re-layouts  28.8 us (16%)
  blocking collectives  23.6 us (13%)
    psum x1, blocking collectives, local(): partial_value = lax.psum(partial_value, 'sect')  23.6 us
    all_to_all x1, starting transfers between devices, local(): lax.all_to_all(requests.reshape(tile_count, capacity), 'tile', split_axis...  21.8 us
    all_to_all x1, waiting for transfers between devices, local(): lax.all_to_all(answer, 'tile', split_axis=1, concat_axis=1, tiled=True)  16.2 us
    all_to_all x1, waiting for transfers between devices, local(): lax.all_to_all(packed.reshape(3, tile_count, capacity), 'tile', split_axi...  15.4 us
    scatter-add x1, other arithmetic, local(): counts = jnp.zeros((ocean_cells,), jnp.float32).at[flat_index].add(weight)  14.6 us
    scatter-add x1, other arithmetic, local(): totals = jnp.zeros((3, ocean_cells), jnp.float32).at[:, flat_index].add(a...  14.6 us
    all_to_all x1, waiting for transfers between devices, local(): lax.all_to_all(requests.reshape(tile_count, capacity), 'tile', split_axis...  11 us
    all_to_all x1, starting transfers between devices, local(): lax.all_to_all(packed.reshape(3, tile_count, capacity), 'tile', split_axi...  8.84 us
  transfers between devices with their start and end apart: 5, of which 3 were waited for; matrix products, arithmetic and copies ran while one was open for 11% of the time, Pallas kernels for 0%

profile of v1, /device:TPU:8, one launch (start us, length us, event | category | flops | bytes accessed | tf_op | source)
XLA Modules:
  0.0 184.7 jit_solution(2406811676478598066)
XLA Ops:
  0.6 1.3 convert_reduce_fusion
  1.9 0.7 compare_select_fusion.4
  2.6 4.5 %scatter_custom_fusion = s32[2112]{0:T(1024)S(1)} fusion(s32[1024]{0:T(1024)S(1)} %bitcast.66, s32[1024]{0:T(1024)} %param.15, s32[]{:T(128)} %constant.16.clone.1), kind=kCustom, calls=%fused_computation.109 | custom fusion | bytes 8960 | tf_op jit(solution)/shard_map/scatter | solution.py:68
  7.1 0.8 all_to_all.16
  7.9 21.8 %all-to-all-start = ((s32[96,1,22]{2,1,0:T(1,128)}), s32[96,1,22]{2,1,0:T(1,128)S(1)}, u32[]{:S(2)}, u32[]{:S(2)}) async-start(s32[96,1,22]{2,1,0:T(1,128)} %bitcast.3), calls=%async_computation | async-start | bytes 98304 | tf_op jit(solution)/shard_map/all_to_all | solution.py:69
  29.7 0.7 fusion.53
  30.4 0.8 pad_maximum_fusion.2
  31.1 0.8 select_reduce_fusion
  32.2 11.0 %all-to-all-done = s32[96,1,22]{2,1,0:T(1,128)S(1)} async-done(((s32[96,1,22]{2,1,0:T(1,128)}), s32[96,1,22]{2,1,0:T(1,128)S(1)}, u32[]{:S(2)}, u32[]{:S(2)}) %all-to-all-start) | async-done | bytes 8480 | tf_op jit(solution)/shard_map/all_to_all | solution.py:69
  43.4 4.0 %gather_fusion = f32[2112,3]{1,0:T(8,128)S(1)} fusion(f32[3,2048]{0,1:T(8,128)S(1)} %copy.65, s32[3072]{0:T(1024)S(1)} %pad_clamp_fusion), kind=kCustom, calls=%fused_computation | custom fusion | bytes 59136 | tf_op jit(solution)/shard_map/gather | solution.py:75
  48.1 0.8 copy.67
  48.9 6.5 %all-to-all-start.1 = ((f32[3,96,22]{2,0,1:T(4,128)}), f32[3,96,22]{2,0,1:T(4,128)S(1)}, u32[]{:S(2)}, u32[]{:S(2)}) async-start(f32[3,96,22]{2,0,1:T(4,128)} %copy.67), calls=%async_computation.1 | async-start | bytes 393216 | tf_op jit(solution)/shard_map/all_to_all | solution.py:76
  55.5 16.2 %all-to-all-done.1 = f32[3,96,22]{2,0,1:T(4,128)S(1)} async-done(((f32[3,96,22]{2,0,1:T(4,128)}), f32[3,96,22]{2,0,1:T(4,128)S(1)}, u32[]{:S(2)}, u32[]{:S(2)}) %all-to-all-start.1) | async-done | bytes 25376 | tf_op jit(solution)/shard_map/all_to_all | solution.py:76
  72.2 2.8 %gather_fusion.1 = f32[1024,3]{1,0:T(8,128)S(1)} fusion(f32[3,2112]{0,1:T(8,128)S(1)} %copy.69, s32[1024]{0:T(1024)S(1)} %broadcast_clamp_fusion), kind=kCustom, calls=%fused_computation.1 | custom fusion | bytes 28672 | tf_op jit(solution)/shard_map/gather | solution.py:77
  75.4 3.1 %collective-permute-start.1 = (f32[165,4,128]{2,0,1:T(8,128)S(1)}, f32[165,4,128]{2,0,1:T(8,128)S(1)}, u32[]{:S(2)}, u32[]{:S(2)}) collective-permute-start(f32[165,4,128]{2,0,1:T(8,128)S(1)} %copy.72), channel_id=1, source_target_pairs={{1,0},{2,1},{3,2},{4,3},{5,4},{6,5},{7,6},{8,7},{9,8},{10,9},{11,1... | collective-permute-start | bytes 1013768 | tf_op jit(solution)/shard_map/ppermute | solution.py:21
  78.6 2.7 %collective-permute-start = (f32[165,4,128]{2,0,1:T(8,128)S(1)}, f32[165,4,128]{2,0,1:T(8,128)S(1)}, u32[]{:S(2)}, u32[]{:S(2)}) collective-permute-start(f32[165,4,128]{2,0,1:T(8,128)S(1)} %copy.71), channel_id=1, source_target_pairs={{0,1},{1,2},{2,3},{3,4},{4,5},{5,6},{6,7},{7,8},{8,9},{9,10},{10,1... | collective-permute-start | bytes 1013768 | tf_op jit(solution)/shard_map/ppermute | solution.py:20
  82.1 0.8 reduce.7
  83.3 14.6 %scatter_custom_fusion.3 = f32[2048]{0:T(1024)S(1)} fusion(s32[2112]{0:T(1024)S(1)} %fusion.35, f32[2112]{0:T(1024)S(1)} %reshape.286, f32[]{:T(128)} %constant.21.clone.1), kind=kCustom, calls=%fused_computation.117 | custom fusion | flops 2112 | bytes 8196 | tf_op jit(solution)/shard_map/scatter-add | solution.py:109
  100.8 1.0 fusion.18
  102.2 0.8 fusion.14
  105.0 1.0 fusion.20
  106.4 0.7 fusion.9
  109.0 1.0 fusion.22
  110.7 0.7 fusion.4
  114.4 0.6 copy-done.1
  115.5 23.6 %psum.7 = f32[3,1024]{1,0:T(4,128)S(1)} all-reduce(f32[3,1024]{1,0:T(4,128)S(1)} %convolution_multiply_fusion), channel_id=1, replica_groups=mesh['sect'=8,'tile'=96] {'sect'}, use_global_device_ids=true, to_apply=%region_4.5 | all-reduce | flops 3072 | bytes 24576 | tf_op jit(solution)/shard_map/psum | solution.py:97
  139.3 3.4 %scatter_custom_fusion.1 = f32[3,2112]{0,1:T(8,128)S(1)} fusion(s32[1024]{0:T(1024)S(1)} %bitcast.68, f32[1024,3]{1,0:T(8,128)S(1)} %copy.76, f32[]{:T(128)} %constant.21.clone.1), kind=kCustom, calls=%fused_computation.76 | custom fusion | bytes 25348 | tf_op jit(solution)/shard_map/scatter | solution.py:98
  143.2 0.8 copy.78
  144.0 8.8 %all-to-all-start.2 = ((f32[3,96,22]{2,0,1:T(4,128)}), f32[3,96,22]{2,0,1:T(4,128)S(1)}, u32[]{:S(2)}, u32[]{:S(2)}) async-start(f32[3,96,22]{2,0,1:T(4,128)} %copy.78), calls=%async_computation.2 | async-start | bytes 393216 | tf_op jit(solution)/shard_map/all_to_all | solution.py:99
  152.8 15.4 %all-to-all-done.2 = f32[3,96,22]{2,0,1:T(4,128)S(1)} async-done(((f32[3,96,22]{2,0,1:T(4,128)}), f32[3,96,22]{2,0,1:T(4,128)S(1)}, u32[]{:S(2)}, u32[]{:S(2)}) %all-to-all-start.2) | async-done | bytes 25376 | tf_op jit(solution)/shard_map/all_to_all | solution.py:99
  168.8 14.6 %scatter_custom_fusion.2 = f32[3,2048]{0,1:T(8,128)S(1)} fusion(s32[2112]{0:T(1024)S(1)} %fusion.35, f32[2112,3]{1,0:T(8,128)S(1)} %copy.81, f32[]{:T(128)} %constant.21.clone.1), kind=kCustom, calls=%fused_computation.82 | custom fusion | flops 6336 | bytes 24580 | tf_op jit(solution)/shard_map/scatter-add | solution.py:107
  183.7 0.9 copy.82
  (83 shorter events, 16.6 us)
Async XLA Ops:
  7.9 35.4 %all-to-all-start = ((s32[96,1,22]{2,1,0:T(1,128)}), s32[96,1,22]{2,1,0:T(1,128)S(1)}, u32[]{:S(2)}, u32[]{:S(2)}) async-start(s32[96,1,22]{2,1,0:T(1,128)} %bitcast.3), calls=%async_computation | async-start | bytes 98304 | tf_op jit(solution)/shard_map/all_to_all | solution.py:69
  48.9 26.3 %copy-start = (f32[162,8,128]{2,1,0:T(8,128)S(1)}, f32[162,8,128]{2,1,0:T(8,128)}, u32[]{:S(2)}) copy-start(f32[162,8,128]{2,1,0:T(8,128)} %param.8) | copy-start | bytes 1990660
  48.9 22.7 %all-to-all-start.1 = ((f32[3,96,22]{2,0,1:T(4,128)}), f32[3,96,22]{2,0,1:T(4,128)S(1)}, u32[]{:S(2)}, u32[]{:S(2)}) async-start(f32[3,96,22]{2,0,1:T(4,128)} %copy.67), calls=%async_computation.1 | async-start | bytes 393216 | tf_op jit(solution)/shard_map/all_to_all | solution.py:76
  75.4 22.9 %collective-permute-start.1 = (f32[165,4,128]{2,0,1:T(8,128)S(1)}, f32[165,4,128]{2,0,1:T(8,128)S(1)}, u32[]{:S(2)}, u32[]{:S(2)}) collective-permute-start(f32[165,4,128]{2,0,1:T(8,128)S(1)} %copy.72), channel_id=1, source_target_pairs={{1,0},{2,1},{3,2},{4,3},{5,4},{6,5},{7,6},{8,7},{9,8},{10,9},{11,1... | collective-permute-start | bytes 1013768 | tf_op jit(solution)/shard_map/ppermute | solution.py:21
  78.6 19.8 %collective-permute-start = (f32[165,4,128]{2,0,1:T(8,128)S(1)}, f32[165,4,128]{2,0,1:T(8,128)S(1)}, u32[]{:S(2)}, u32[]{:S(2)}) collective-permute-start(f32[165,4,128]{2,0,1:T(8,128)S(1)} %copy.71), channel_id=1, source_target_pairs={{0,1},{1,2},{2,3},{3,4},{4,5},{5,6},{6,7},{7,8},{8,9},{9,10},{10,1... | collective-permute-start | bytes 1013768 | tf_op jit(solution)/shard_map/ppermute | solution.py:20
  114.2 0.8 copy-start.1
  144.0 24.3 %all-to-all-start.2 = ((f32[3,96,22]{2,0,1:T(4,128)}), f32[3,96,22]{2,0,1:T(4,128)S(1)}, u32[]{:S(2)}, u32[]{:S(2)}) async-start(f32[3,96,22]{2,0,1:T(4,128)} %copy.78), calls=%async_computation.2 | async-start | bytes 393216 | tf_op jit(solution)/shard_map/all_to_all | solution.py:99

commit v2 on v1

--- a/solution.py
+++ b/solution.py
@@ -43,8 +43,6 @@
 ):
     bin_count, row_count, columns = spectrum.shape
     cell_count = row_count * columns
-    tile_count = lax.axis_size("tile")
-    capacity = 2 * ((cell_count + tile_count - 1) // tile_count)
     ocean_cells = elevation.shape[0]
     first_bin = lax.axis_index("sect") * bin_count
     bin_ids = first_bin + jnp.arange(bin_count, dtype=jnp.int32)
@@ -60,21 +58,11 @@
     sin_dir = jnp.sin(angles)
     speed_x = (group_speed * cos_dir)[:, None, None]
     speed_y = (group_speed * sin_dir)[:, None, None]
-    owners = owner_tile[:, 0]
-    cell_ids = jnp.arange(owners.shape[0], dtype=jnp.int32)
-    same_before = (owners[None, :] == owners[:, None]) & (cell_ids[None, :] < cell_ids[:, None])
-    rank_in = jnp.sum(same_before.astype(jnp.int32), 1)
-    position = owners * capacity + rank_in
-    requests = jnp.full((tile_count * capacity,), -1, jnp.int32).at[position].set(ocean_slot)
-    asked_slots = lax.all_to_all(
-        requests.reshape(tile_count, capacity), "tile", split_axis=0, concat_axis=0, tiled=True
-    )
-    is_valid = asked_slots >= 0
-    slot_index = jnp.where(is_valid, asked_slots, 0)
+    target = owner_tile[:, 0] * ocean_cells + ocean_slot
     surface = jnp.concatenate([ocean_currents, elevation[None]], 0)
-    answer = jnp.where(is_valid[None], surface[:, slot_index], 0.0)
-    returned = lax.all_to_all(answer, "tile", split_axis=1, concat_axis=1, tiled=True)
-    at_cells = returned.reshape(3, tile_count * capacity)[:, position]
+    tile_count = lax.axis_size("tile")
+    surface_all = lax.all_gather(surface.reshape(1, 3, -1, columns), "tile", axis=0, tiled=True)
+    at_cells = jnp.stack([surface_all[:, k].reshape(-1)[target] for k in range(3)], 0)
     sea_float = sea_mask.astype(jnp.float32)
     flow_fields = jnp.concatenate([at_cells[:2].reshape(2, row_count, columns), sea_float[None]], 0)
     extended = with_halo(jnp.concatenate([spectrum, flow_fields], 0), (("tile", 1),), STEPS)
@@ -95,19 +83,14 @@
     )
     partial_value = partial_value * ((1.0 + at_cells[2]) * sea_float.reshape(-1))
     partial_value = lax.psum(partial_value, "sect")
-    packed = jnp.zeros((3, tile_count * capacity), jnp.float32).at[:, position].set(partial_value)
-    arrived = lax.all_to_all(
-        packed.reshape(3, tile_count, capacity), "tile", split_axis=1, concat_axis=1, tiled=True
+    contributions = jnp.concatenate([partial_value, jnp.ones((1, cell_count), jnp.float32)], 0)
+    blank = jnp.zeros((tile_count * ocean_cells,), jnp.float32)
+    spread = jnp.stack(
+        [blank.at[target].add(contributions[k]).reshape(tile_count, -1, columns) for k in range(4)],
+        1,
     )
-    flat_index = slot_index.reshape(-1)
-    weight = is_valid.reshape(-1).astype(jnp.float32)
-    totals = (
-        jnp.zeros((3, ocean_cells), jnp.float32)
-        .at[:, flat_index]
-        .add(arrived.reshape(3, -1) * weight[None])
-    )
-    counts = jnp.zeros((ocean_cells,), jnp.float32).at[flat_index].add(weight)
-    return (energy, totals / jnp.maximum(counts, 1.0)[None])
+    gathered = lax.psum_scatter(spread, "tile", scatter_dimension=0, tiled=True).reshape(4, -1)
+    return (energy, gathered[:3] / jnp.maximum(gathered[3], 1.0)[None])
 
 
 def solution(mesh):

time: 185 us -> 917 us (4.96)
  the two profiles are of different devices: /device:TPU:8 before, /device:TPU:2 now
where the time goes in v2:
time: 917 us; the launch traced here: 916 us
  waiting for transfers between devices  803 us (88%)
  other arithmetic  42.2 us (5%)
  local copies, waits for them, and re-layouts  29.4 us (3%)
  blocking collectives  20.6 us (2%)
  between operations  14.5 us (2%)
    reduce_scatter x1, waiting for transfers between devices, local(): lax.psum_scatter(spread, 'tile', scatter_dimension=0, tiled=True)  678 us
    all_gather x1, waiting for transfers between devices, local(): lax.all_gather(surface.reshape(1, 3, -1, columns), 'tile', axis=0, tiled=...  124 us
    scatter-add x4, other arithmetic, local(): blank.at[target].add(contributions[k]).reshape(tile_count, -1, columns)  24.5 us
    psum x1, blocking collectives, local(): partial_value = lax.psum(partial_value, 'sect')  20.6 us
    gather x3, local copies, waits for them, and re-layouts, local(): surface_all[:, k].reshape(-1)[target]  18.6 us
  transfers between devices with their start and end apart: 4, of which 2 were waited for; matrix products, arithmetic and copies ran while one was open for 2% of the time, Pallas kernels for 0%

profile of v2, /device:TPU:2, one launch (start us, length us, event | category | flops | bytes accessed | tf_op | source)
XLA Modules:
  0.0 916.3 jit_solution(13046932595437385379)
XLA Ops:
  7.2 0.7 copy.25
  7.9 1.3 pad_maximum_fusion.3
  9.3 0.7 broadcast_multiply_fusion
  10.0 0.7 broadcast_clamp_fusion
  10.7 6.1 scatter_custom_fusion.3
  16.8 0.8 select_reduce_fusion
  17.7 0.7 fusion.51
  18.4 124.2 %all-gather.2.cloned.1.call-done = f32[96,3,16,128]{3,2,1,0:T(8,128)} async-done(((f32[1,3,16,128]{3,2,1,0:T(8,128)}), f32[96,3,16,128]{3,2,1,0:T(8,128)}) %all-gather.2.cloned.1.call-update) | async-done | bytes 2359312 | tf_op jit(solution)/shard_map/all_gather | solution.py:64
  142.6 1.8 fusion.48
  144.3 6.2 gather_fusion.1
  150.5 6.2 gather_fusion
  156.9 1.3 collective-permute-start.1
  158.2 5.3 collective-permute-start
  163.6 6.3 gather_fusion.2
  170.0 1.1 copy.18
  173.4 1.0 fusion.17
  174.8 0.8 fusion.13
  177.6 1.0 fusion.19
  179.0 0.7 fusion.8
  181.7 1.0 fusion.21
  183.3 0.7 fusion.3
  185.5 0.6 fusion.26
  187.0 0.6 copy-done.1
  188.1 20.6 %psum.7 = f32[3,1024]{1,0:T(4,128)S(1)} all-reduce(f32[3,1024]{1,0:T(4,128)S(1)} %convolution_multiply_fusion), channel_id=1, replica_groups=mesh['sect'=8,'tile'=96] {'sect'}, use_global_device_ids=true, to_apply=%region_2.3 | all-reduce | flops 3072 | bytes 24576 | tf_op jit(solution)/shard_map/psum | solution.py:85
  208.8 6.1 scatter_custom_fusion.2
  214.9 6.1 scatter_custom_fusion.1
  221.0 6.1 scatter_custom_fusion
  227.1 1.9 pad_maximum_fusion
  229.1 678.3 %reduce-scatter.2.cloned.1.call-done = f32[1,4,16,128]{3,2,1,0:T(8,128)} async-done(((f32[96,4,16,128]{3,2,1,0:T(8,128)}), f32[1,4,16,128]{3,2,1,0:T(8,128)}) %reduce-scatter.2.cloned.1.call-update) | async-done | bytes 32784 | tf_op jit(solution)/shard_map/reduce_scatter | solution.py:92
  907.4 0.7 slice_bitcast_fusion
  908.1 0.7 fusion.36
  908.8 0.6 bitcast_divide_fusion
  (59 shorter events, 10.9 us)
Async XLA Ops:
  7.2 135.4 %all-gather.2.cloned.1.call-start = ((), (), s32[]{:S(2)}) async-start(), calls=%async_computation.1 | async-start | bytes 2383872 | tf_op jit(solution)/shard_map/all_gather | solution.py:64
  9.3 898.1 %reduce-scatter.2.cloned.1.call-start = ((), (), s32[]{:S(2)}) async-start(), calls=%async_computation.2 | async-start | bytes 3178496 | tf_op jit(solution)/shard_map/reduce_scatter | solution.py:92
  150.5 6.2 copy-start
  156.9 13.0 %collective-permute-start.1 = (f32[165,4,128]{2,0,1:T(8,128)S(1)}, f32[165,4,128]{2,0,1:T(8,128)S(1)}, u32[]{:S(2)}, u32[]{:S(2)}) collective-permute-start(f32[165,4,128]{2,0,1:T(8,128)S(1)} %copy.17), channel_id=1, source_target_pairs={{1,0},{2,1},{3,2},{4,3},{5,4},{6,5},{7,6},{8,7},{9,8},{10,9},{11,1... | collective-permute-start | bytes 1013768 | tf_op jit(solution)/shard_map/ppermute | solution.py:21
  158.2 11.8 %collective-permute-start = (f32[165,4,128]{2,0,1:T(8,128)S(1)}, f32[165,4,128]{2,0,1:T(8,128)}, u32[]{:S(2)}, u32[]{:S(2)}) collective-permute-start(f32[165,4,128]{2,0,1:T(8,128)S(1)} %copy.16), channel_id=1, source_target_pairs={{0,1},{1,2},{2,3},{3,4},{4,5},{5,6},{6,7},{7,8},{8,9},{9,10},{10,1... | collective-permute-start | bytes 1013768 | tf_op jit(solution)/shard_map/ppermute | solution.py:20
  163.5 6.4 copy-start.2
  186.8 0.8 copy-start.1
Sparse Core Ops, SparseCore 0:
  12.3 130.1 all-gather.1
  229.2 678.1 reduce-scatter.1

commit v3 on v1

--- a/solution.py
+++ b/solution.py
@@ -94,20 +94,32 @@
         weights, energy.reshape(bin_count, cell_count), precision=lax.Precision.HIGHEST
     )
     partial_value = partial_value * ((1.0 + at_cells[2]) * sea_float.reshape(-1))
-    partial_value = lax.psum(partial_value, "sect")
+    sect_count = lax.axis_size("sect")
+    every_part = lax.all_to_all(
+        jnp.broadcast_to(partial_value[None], (sect_count,) + partial_value.shape),
+        "sect",
+        0,
+        0,
+        tiled=True,
+    )
+    partial_value = every_part[0]
+    for part in range(1, sect_count):
+        partial_value = partial_value + every_part[part]
     packed = jnp.zeros((3, tile_count * capacity), jnp.float32).at[:, position].set(partial_value)
     arrived = lax.all_to_all(
         packed.reshape(3, tile_count, capacity), "tile", split_axis=1, concat_axis=1, tiled=True
     )
-    flat_index = slot_index.reshape(-1)
+    flat_slots = asked_slots.reshape(-1)
     weight = is_valid.reshape(-1).astype(jnp.float32)
-    totals = (
-        jnp.zeros((3, ocean_cells), jnp.float32)
-        .at[:, flat_index]
-        .add(arrived.reshape(3, -1) * weight[None])
+    slot_pick = (flat_slots[:, None] == jnp.arange(ocean_cells, dtype=jnp.int32)[None, :]).astype(
+        jnp.float32
     )
-    counts = jnp.zeros((ocean_cells,), jnp.float32).at[flat_index].add(weight)
-    return (energy, totals / jnp.maximum(counts, 1.0)[None])
+    summed = jnp.dot(
+        jnp.concatenate([arrived.reshape(3, -1) * weight[None], weight[None]], 0),
+        slot_pick,
+        precision=lax.Precision.HIGHEST,
+    )
+    return (energy, summed[:3] / jnp.maximum(summed[3], 1.0)[None])
 
 
 def solution(mesh):

time: 185 us -> 154 us (0.83)
  other arithmetic: 45.2 us -> 16.5 us
  blocking collectives: 23.6 us -> 0 us
  waiting for transfers between devices: 42.6 us -> 54.2 us
  matrix products: 0.44 us -> 5.95 us
  starting transfers between devices: 42.9 us -> 47.3 us
    scatter-add x2 -> x0, other arithmetic: 29.1 us -> none  [the longest x1 14.6 us: local(): counts = jnp.zeros((ocean_cells,), jnp.float32).at[flat_index].add(weight)]
    psum x1 -> x0, blocking collectives: 23.6 us -> none  [local(): partial_value = lax.psum(partial_value, 'sect')]
    dot_general x0 -> x1, matrix products: none -> 5.51 us  [local(): jnp.dot(jnp.concatenate([arrived.reshape(3, -1) * weight[None], weight[No...]
    all_to_all x0 -> x1, waiting for transfers between devices: none -> 4.72 us  [local(): lax.all_to_all(jnp.broadcast_to(partial_value[None], (sect_count,) + part...]
    all_to_all x0 -> x1, starting transfers between devices: none -> 4.3 us  [local(): lax.all_to_all(jnp.broadcast_to(partial_value[None], (sect_count,) + part...]
    ppermute x1, waiting for transfers between devices: 0.01 us -> 3.06 us  [with_halo(): before = lax.ppermute(last, axis, up)]
    ppermute x1, waiting for transfers between devices: 0.01 us -> 2.64 us  [with_halo(): after = lax.ppermute(leading, axis, down)]
  transfers between devices with their start and end apart: 5 -> 6, of which waited for: 3 -> 6; matrix products, arithmetic and copies ran while one was open for 11% -> 3% of each run, Pallas kernels for 0% -> 0%
where the time goes in v3:
time: 154 us; the launch traced here: 153 us
  waiting for transfers between devices  54.2 us (35%)
  starting transfers between devices  47.3 us (31%)
  local copies, waits for them, and re-layouts  27.9 us (18%)
  other arithmetic  16.5 us (11%)
  matrix products  5.95 us (4%)
    all_to_all x1, starting transfers between devices, local(): lax.all_to_all(requests.reshape(tile_count, capacity), 'tile', split_axis...  21.8 us
    all_to_all x1, waiting for transfers between devices, local(): lax.all_to_all(packed.reshape(3, tile_count, capacity), 'tile', split_axi...  16.9 us
    all_to_all x1, waiting for transfers between devices, local(): lax.all_to_all(answer, 'tile', split_axis=1, concat_axis=1, tiled=True)  15.9 us
    all_to_all x1, waiting for transfers between devices, local(): lax.all_to_all(requests.reshape(tile_count, capacity), 'tile', split_axis...  11 us
    all_to_all x1, starting transfers between devices, local(): lax.all_to_all(packed.reshape(3, tile_count, capacity), 'tile', split_axi...  8.83 us
    all_to_all x1, starting transfers between devices, local(): lax.all_to_all(answer, 'tile', split_axis=1, concat_axis=1, tiled=True)  6.35 us
    dot_general x1, matrix products, local(): jnp.dot(jnp.concatenate([arrived.reshape(3, -1) * weight[None], weight[No...  5.51 us
    all_to_all x1, waiting for transfers between devices, local(): lax.all_to_all(jnp.broadcast_to(partial_value[None], (sect_count,) + part...  4.72 us
  transfers between devices with their start and end apart: 6, of which 6 were waited for; matrix products, arithmetic and copies ran while one was open for 3% of the time, Pallas kernels for 0%

profile of v3, /device:TPU:8, one launch (start us, length us, event | category | flops | bytes accessed | tf_op | source)
XLA Modules:
  0.0 153.0 jit_solution(14003182779691545759)
XLA Ops:
  0.6 1.3 convert_reduce_fusion
  1.9 0.7 compare_select_fusion.2
  2.6 4.5 %scatter_custom_fusion = s32[2112]{0:T(1024)S(1)} fusion(s32[1024]{0:T(1024)S(1)} %bitcast.68, s32[1024]{0:T(1024)} %param.15, s32[]{:T(128)} %constant.16.clone.1), kind=kCustom, calls=%fused_computation.118 | custom fusion | bytes 8960 | tf_op jit(solution)/shard_map/scatter | solution.py:68
  7.1 0.8 all_to_all.19
  7.9 21.8 %all-to-all-start = ((s32[96,1,22]{2,1,0:T(1,128)}), s32[96,1,22]{2,1,0:T(1,128)S(1)}, u32[]{:S(2)}, u32[]{:S(2)}) async-start(s32[96,1,22]{2,1,0:T(1,128)} %bitcast.3), calls=%async_computation | async-start | bytes 98304 | tf_op jit(solution)/shard_map/all_to_all | solution.py:69
  29.7 0.7 fusion.55
  30.4 0.8 pad_maximum_fusion.2
  31.1 0.8 select_reduce_fusion
  32.2 11.0 %all-to-all-done = s32[96,1,22]{2,1,0:T(1,128)S(1)} async-done(((s32[96,1,22]{2,1,0:T(1,128)}), s32[96,1,22]{2,1,0:T(1,128)S(1)}, u32[]{:S(2)}, u32[]{:S(2)}) %all-to-all-start) | async-done | bytes 8480 | tf_op jit(solution)/shard_map/all_to_all | solution.py:69
  43.4 4.0 %gather_fusion = f32[2112,3]{1,0:T(8,128)S(1)} fusion(f32[3,2048]{0,1:T(8,128)S(1)} %copy.59, s32[3072]{0:T(1024)S(1)} %pad_clamp_fusion), kind=kCustom, calls=%fused_computation | custom fusion | bytes 59136 | tf_op jit(solution)/shard_map/gather | solution.py:75
  48.1 0.8 copy.61
  48.9 6.3 %all-to-all-start.1 = ((f32[3,96,22]{2,0,1:T(4,128)}), f32[3,96,22]{2,0,1:T(4,128)S(1)}, u32[]{:S(2)}, u32[]{:S(2)}) async-start(f32[3,96,22]{2,0,1:T(4,128)} %copy.61), calls=%async_computation.1 | async-start | bytes 393216 | tf_op jit(solution)/shard_map/all_to_all | solution.py:76
  55.6 15.9 %all-to-all-done.1 = f32[3,96,22]{2,0,1:T(4,128)S(1)} async-done(((f32[3,96,22]{2,0,1:T(4,128)}), f32[3,96,22]{2,0,1:T(4,128)S(1)}, u32[]{:S(2)}, u32[]{:S(2)}) %all-to-all-start.1) | async-done | bytes 25376 | tf_op jit(solution)/shard_map/all_to_all | solution.py:76
  72.1 2.8 %gather_fusion.1 = f32[1024,3]{1,0:T(8,128)S(1)} fusion(f32[3,2112]{0,1:T(8,128)S(1)} %copy.63, s32[1024]{0:T(1024)S(1)} %broadcast_clamp_fusion), kind=kCustom, calls=%fused_computation.1 | custom fusion | bytes 28672 | tf_op jit(solution)/shard_map/gather | solution.py:77
  75.3 3.1 %collective-permute-start.1 = (f32[165,4,128]{2,0,1:T(8,128)S(1)}, f32[165,4,128]{2,0,1:T(8,128)S(1)}, u32[]{:S(2)}, u32[]{:S(2)}) collective-permute-start(f32[165,4,128]{2,0,1:T(8,128)S(1)} %copy.66), channel_id=1, source_target_pairs={{1,0},{2,1},{3,2},{4,3},{5,4},{6,5},{7,6},{8,7},{9,8},{10,9},{11,1... | collective-permute-start | bytes 1013768 | tf_op jit(solution)/shard_map/ppermute | solution.py:21
  78.4 2.9 %collective-permute-start = (f32[165,4,128]{2,0,1:T(8,128)S(1)}, f32[165,4,128]{2,0,1:T(8,128)S(1)}, u32[]{:S(2)}, u32[]{:S(2)}) collective-permute-start(f32[165,4,128]{2,0,1:T(8,128)S(1)} %copy.65), channel_id=1, source_target_pairs={{0,1},{1,2},{2,3},{3,4},{4,5},{5,6},{6,7},{7,8},{8,9},{9,10},{10,1... | collective-permute-start | bytes 1013768 | tf_op jit(solution)/shard_map/ppermute | solution.py:20
  81.8 2.6 %collective-permute-done.1 = f32[165,4,128]{2,0,1:T(8,128)S(1)} collective-permute-done((f32[165,4,128]{2,0,1:T(8,128)S(1)}, f32[165,4,128]{2,0,1:T(8,128)S(1)}, u32[]{:S(2)}, u32[]{:S(2)}) %collective-permute-start.1) | collective-permute-done | bytes 337952 | tf_op jit(solution)/shard_map/ppermute | solution.py:21
  84.5 3.1 %collective-permute-done = f32[165,4,128]{2,0,1:T(8,128)S(1)} collective-permute-done((f32[165,4,128]{2,0,1:T(8,128)S(1)}, f32[165,4,128]{2,0,1:T(8,128)S(1)}, u32[]{:S(2)}, u32[]{:S(2)}) %collective-permute-start) | collective-permute-done | bytes 337952 | tf_op jit(solution)/shard_map/ppermute | solution.py:20
  89.9 1.0 fusion.20
  91.4 0.8 fusion.16
  94.2 1.0 fusion.22
  98.2 1.2 fusion.24
  99.9 0.7 fusion.6
  104.7 0.7 broadcast_in_dim.30
  105.3 4.3 %all-to-all-start.2 = ((f32[8,3,1024]{2,1,0:T(4,128)}), f32[8,3,1024]{2,1,0:T(4,128)S(1)}, u32[]{:S(2)}, u32[]{:S(2)}) async-start(f32[8,3,1024]{2,1,0:T(4,128)} %broadcast_in_dim.30), calls=%async_computation.2 | async-start | bytes 262144 | tf_op jit(solution)/shard_map/all_to_all | solution.py:98
  110.2 0.8 reduce.5
  111.1 4.7 %all-to-all-done.2 = f32[8,3,1024]{2,1,0:T(4,128)S(1)} async-done(((f32[8,3,1024]{2,1,0:T(4,128)}), f32[8,3,1024]{2,1,0:T(4,128)S(1)}, u32[]{:S(2)}, u32[]{:S(2)}) %all-to-all-start.2) | async-done | bytes 98336 | tf_op jit(solution)/shard_map/all_to_all | solution.py:98
  116.0 3.4 %scatter_custom_fusion.1 = f32[3,2112]{0,1:T(8,128)S(1)} fusion(s32[1024]{0:T(1024)S(1)} %bitcast.70, f32[1024,3]{1,0:T(8,128)S(1)} %copy.70, f32[]{:T(128)} %constant.21.clone.1), kind=kCustom, calls=%fused_computation.77 | custom fusion | bytes 25348 | tf_op jit(solution)/shard_map/scatter | solution.py:108
  119.9 0.8 copy.72
  120.7 8.8 %all-to-all-start.3 = ((f32[3,96,22]{2,0,1:T(4,128)}), f32[3,96,22]{2,0,1:T(4,128)S(1)}, u32[]{:S(2)}, u32[]{:S(2)}) async-start(f32[3,96,22]{2,0,1:T(4,128)} %copy.72), calls=%async_computation.3 | async-start | bytes 393216 | tf_op jit(solution)/shard_map/all_to_all | solution.py:109
  129.8 16.9 %all-to-all-done.3 = f32[3,96,22]{2,0,1:T(4,128)S(1)} async-done(((f32[3,96,22]{2,0,1:T(4,128)}), f32[3,96,22]{2,0,1:T(4,128)S(1)}, u32[]{:S(2)}, u32[]{:S(2)}) %all-to-all-start.3) | async-done | bytes 25376 | tf_op jit(solution)/shard_map/all_to_all | solution.py:109
  146.9 5.5 %fusion = f32[4,2048]{1,0:T(4,128)S(1)} fusion(s32[2112]{0:T(1024)S(1)} %all_to_all.25, f32[1,2112]{1,0:T(1,128)S(1)} %reshape.226, f32[3,2112]{1,0:T(4,128)S(1)} %broadcast_multiply_fusion), kind=kOutput, calls=%fused_computation.5 | convolution fusion | flops 211951872 | bytes 75008 | tf_op jit(solution)/shard_map/dot_general | solution.py:117
  (83 shorter events, 17.6 us)
Async XLA Ops:
  7.9 35.4 %all-to-all-start = ((s32[96,1,22]{2,1,0:T(1,128)}), s32[96,1,22]{2,1,0:T(1,128)S(1)}, u32[]{:S(2)}, u32[]{:S(2)}) async-start(s32[96,1,22]{2,1,0:T(1,128)} %bitcast.3), calls=%async_computation | async-start | bytes 98304 | tf_op jit(solution)/shard_map/all_to_all | solution.py:69
  48.9 22.6 %all-to-all-start.1 = ((f32[3,96,22]{2,0,1:T(4,128)}), f32[3,96,22]{2,0,1:T(4,128)S(1)}, u32[]{:S(2)}, u32[]{:S(2)}) async-start(f32[3,96,22]{2,0,1:T(4,128)} %copy.61), calls=%async_computation.1 | async-start | bytes 393216 | tf_op jit(solution)/shard_map/all_to_all | solution.py:76
  55.4 19.7 %copy-start = (f32[162,8,128]{2,1,0:T(8,128)S(1)}, f32[162,8,128]{2,1,0:T(8,128)}, u32[]{:S(2)}) copy-start(f32[162,8,128]{2,1,0:T(8,128)} %param.8) | copy-start | bytes 1990660
  75.3 9.1 %collective-permute-start.1 = (f32[165,4,128]{2,0,1:T(8,128)S(1)}, f32[165,4,128]{2,0,1:T(8,128)S(1)}, u32[]{:S(2)}, u32[]{:S(2)}) collective-permute-start(f32[165,4,128]{2,0,1:T(8,128)S(1)} %copy.66), channel_id=1, source_target_pairs={{1,0},{2,1},{3,2},{4,3},{5,4},{6,5},{7,6},{8,7},{9,8},{10,9},{11,1... | collective-permute-start | bytes 1013768 | tf_op jit(solution)/shard_map/ppermute | solution.py:21
  78.4 9.1 %collective-permute-start = (f32[165,4,128]{2,0,1:T(8,128)S(1)}, f32[165,4,128]{2,0,1:T(8,128)S(1)}, u32[]{:S(2)}, u32[]{:S(2)}) collective-permute-start(f32[165,4,128]{2,0,1:T(8,128)S(1)} %copy.65), channel_id=1, source_target_pairs={{0,1},{1,2},{2,3},{3,4},{4,5},{5,6},{6,7},{7,8},{8,9},{9,10},{10,1... | collective-permute-start | bytes 1013768 | tf_op jit(solution)/shard_map/ppermute | solution.py:20
  103.4 0.8 copy-start.1
  105.3 10.4 %all-to-all-start.2 = ((f32[8,3,1024]{2,1,0:T(4,128)}), f32[8,3,1024]{2,1,0:T(4,128)S(1)}, u32[]{:S(2)}, u32[]{:S(2)}) async-start(f32[8,3,1024]{2,1,0:T(4,128)} %broadcast_in_dim.30), calls=%async_computation.2 | async-start | bytes 262144 | tf_op jit(solution)/shard_map/all_to_all | solution.py:98
  120.7 26.0 %all-to-all-start.3 = ((f32[3,96,22]{2,0,1:T(4,128)}), f32[3,96,22]{2,0,1:T(4,128)S(1)}, u32[]{:S(2)}, u32[]{:S(2)}) async-start(f32[3,96,22]{2,0,1:T(4,128)} %copy.72), calls=%async_computation.3 | async-start | bytes 393216 | tf_op jit(solution)/shard_map/all_to_all | solution.py:109

commit v4 on v3

--- a/solution.py
+++ b/solution.py
@@ -65,7 +65,11 @@
     same_before = (owners[None, :] == owners[:, None]) & (cell_ids[None, :] < cell_ids[:, None])
     rank_in = jnp.sum(same_before.astype(jnp.int32), 1)
     position = owners * capacity + rank_in
-    requests = jnp.full((tile_count * capacity,), -1, jnp.int32).at[position].set(ocean_slot)
+    spectrum_ext = with_halo(spectrum, (("tile", 1),), STEPS)
+    slot_ids = jnp.arange(tile_count * capacity, dtype=jnp.int32)
+    requests = (
+        jnp.sum(jnp.where(position[:, None] == slot_ids[None, :], ocean_slot[:, None] + 1, 0), 0) - 1
+    )
     asked_slots = lax.all_to_all(
         requests.reshape(tile_count, capacity), "tile", split_axis=0, concat_axis=0, tiled=True
     )
@@ -77,10 +81,10 @@
     at_cells = returned.reshape(3, tile_count * capacity)[:, position]
     sea_float = sea_mask.astype(jnp.float32)
     flow_fields = jnp.concatenate([at_cells[:2].reshape(2, row_count, columns), sea_float[None]], 0)
-    extended = with_halo(jnp.concatenate([spectrum, flow_fields], 0), (("tile", 1),), STEPS)
-    energy = extended[:bin_count]
+    flows_ext = with_halo(flow_fields, (("tile", 1),), STEPS)
+    energy = spectrum_ext
     for sub_step in range(STEPS):
-        flows_now = extended[bin_count:, sub_step : extended.shape[1] - sub_step]
+        flows_now = flows_ext[:, sub_step : flows_ext.shape[1] - sub_step]
         energy = advance(energy, flows_now, speed_x, speed_y)
     weights = jnp.stack(
         [

time: 154 us -> 157 us (1.019)
  starting transfers between devices: 47.3 us -> 53.7 us
  waiting for transfers between devices: 54.2 us -> 49.5 us
  other arithmetic: 16.5 us -> 18.7 us
    ppermute x1 -> x2, starting transfers between devices: 3.12 us -> 14.7 us  [with_halo(): after = lax.ppermute(leading, axis, down)]
    all_to_all x1, starting transfers between devices: 21.8 us -> 15.3 us  [local(): lax.all_to_all(requests.reshape(tile_count, capacity), 'tile', split_axis...]
    scatter x1 -> x0, local copies, waits for them, and re-layouts: 4.49 us -> none  [local(): jnp.full((tile_count * capacity,), -1, jnp.int32).at[position]]
    ppermute x1 -> x2, waiting for transfers between devices: 2.64 us -> 0.01 us  [with_halo(): after = lax.ppermute(leading, axis, down)]
    ppermute x1 -> x2, starting transfers between devices: 2.91 us -> 4.61 us  [with_halo(): before = lax.ppermute(last, axis, up)]
  transfers between devices with their start and end apart: 6 -> 8, of which waited for: 6 -> 5; matrix products, arithmetic and copies ran while one was open for 3% -> 15% of each run, Pallas kernels for 0% -> 0%
where the time goes in v4:
time: 157 us; the launch traced here: 156 us
  starting transfers between devices  53.7 us (34%)
  waiting for transfers between devices  49.5 us (32%)
  local copies, waits for them, and re-layouts  27.2 us (17%)
  other arithmetic  18.7 us (12%)
  matrix products  5.95 us (4%)
    all_to_all x1, waiting for transfers between devices, local(): lax.all_to_all(packed.reshape(3, tile_count, capacity), 'tile', split_axi...  16.8 us
    all_to_all x1, starting transfers between devices, local(): lax.all_to_all(requests.reshape(tile_count, capacity), 'tile', split_axis...  15.3 us
    all_to_all x1, waiting for transfers between devices, local(): lax.all_to_all(answer, 'tile', split_axis=1, concat_axis=1, tiled=True)  15 us
    ppermute x2, starting transfers between devices, with_halo(): after = lax.ppermute(leading, axis, down)  14.7 us
    all_to_all x1, waiting for transfers between devices, local(): lax.all_to_all(requests.reshape(tile_count, capacity), 'tile', split_axis...  10.6 us
    all_to_all x1, starting transfers between devices, local(): lax.all_to_all(packed.reshape(3, tile_count, capacity), 'tile', split_axi...  8.49 us
    all_to_all x1, starting transfers between devices, local(): lax.all_to_all(answer, 'tile', split_axis=1, concat_axis=1, tiled=True)  6.29 us
    dot_general x1, matrix products, local(): jnp.dot(jnp.concatenate([arrived.reshape(3, -1) * weight[None], weight[No...  5.51 us
  transfers between devices with their start and end apart: 8, of which 5 were waited for; matrix products, arithmetic and copies ran while one was open for 15% of the time, Pallas kernels for 0%

profile of v4, /device:TPU:8, one launch (start us, length us, event | category | flops | bytes accessed | tf_op | source)
XLA Modules:
  0.0 156.4 jit_solution(813405248044512474)
XLA Ops:
  0.7 1.4 fusion.53
  2.2 11.4 %collective-permute-start.3 = (f32[162,4,128]{2,0,1:T(8,128)S(1)}, f32[162,4,128]{2,0,1:T(8,128)S(1)}, u32[]{:S(2)}, u32[]{:S(2)}) collective-permute-start(f32[162,4,128]{2,0,1:T(8,128)S(1)} %copy.77), channel_id=1, source_target_pairs={{1,0},{2,1},{3,2},{4,3},{5,4},{6,5},{7,6},{8,7},{9,8},{10,9},{11,1... | collective-permute-start | bytes 995336 | tf_op jit(solution)/shard_map/ppermute | solution.py:21
  13.6 1.9 %collective-permute-start.2 = (f32[162,4,128]{2,0,1:T(8,128)S(1)}, f32[162,4,128]{2,0,1:T(8,128)S(1)}, u32[]{:S(2)}, u32[]{:S(2)}) collective-permute-start(f32[162,4,128]{2,0,1:T(8,128)S(1)} %copy.76), channel_id=1, source_target_pairs={{0,1},{1,2},{2,3},{3,4},{4,5},{5,6},{6,7},{7,8},{8,9},{9,10},{10,1... | collective-permute-start | bytes 995336 | tf_op jit(solution)/shard_map/ppermute | solution.py:20
  16.1 1.0 select_reduce_fusion
  17.1 0.8 sub.69
  17.8 15.3 %all-to-all-start = ((s32[96,1,22]{2,1,0:T(1,128)}), s32[96,1,22]{2,1,0:T(1,128)S(1)}, u32[]{:S(2)}, u32[]{:S(2)}) async-start(s32[96,1,22]{2,1,0:T(1,128)} %bitcast.3), calls=%async_computation | async-start | bytes 98304 | tf_op jit(solution)/shard_map/all_to_all | solution.py:73
  34.4 0.7 select_reduce_fusion.1
  35.1 0.7 multiply_add_fusion.2
  36.1 10.6 %all-to-all-done = s32[96,1,22]{2,1,0:T(1,128)S(1)} async-done(((s32[96,1,22]{2,1,0:T(1,128)}), s32[96,1,22]{2,1,0:T(1,128)S(1)}, u32[]{:S(2)}, u32[]{:S(2)}) %all-to-all-start) | async-done | bytes 8480 | tf_op jit(solution)/shard_map/all_to_all | solution.py:73
  47.5 4.6 %gather_fusion = f32[2112,3]{1,0:T(8,128)S(1)} fusion(f32[3,2048]{0,1:T(8,128)S(1)} %copy.60, s32[3072]{0:T(1024)} %pad_clamp_fusion), kind=kCustom, calls=%fused_computation | custom fusion | bytes 59136 | tf_op jit(solution)/shard_map/gather | solution.py:79
  53.6 0.8 copy.62
  54.3 6.3 %all-to-all-start.1 = ((f32[3,96,22]{2,0,1:T(4,128)}), f32[3,96,22]{2,0,1:T(4,128)S(1)}, u32[]{:S(2)}, u32[]{:S(2)}) async-start(f32[3,96,22]{2,0,1:T(4,128)} %copy.62), calls=%async_computation.1 | async-start | bytes 393216 | tf_op jit(solution)/shard_map/all_to_all | solution.py:80
  61.5 15.0 %all-to-all-done.1 = f32[3,96,22]{2,0,1:T(4,128)S(1)} async-done(((f32[3,96,22]{2,0,1:T(4,128)}), f32[3,96,22]{2,0,1:T(4,128)S(1)}, u32[]{:S(2)}, u32[]{:S(2)}) %all-to-all-start.1) | async-done | bytes 25376 | tf_op jit(solution)/shard_map/all_to_all | solution.py:80
  77.0 3.3 %gather_fusion.1 = f32[1024,3]{1,0:T(8,128)S(1)} fusion(f32[3,2112]{0,1:T(8,128)S(1)} %copy.64, s32[1024]{0:T(1024)} %broadcast_clamp_fusion), kind=kCustom, calls=%fused_computation.1 | custom fusion | bytes 28672 | tf_op jit(solution)/shard_map/gather | solution.py:81
  80.5 0.8 fusion.39
  81.3 3.3 %collective-permute-start.1 = (f32[3,4,128]{2,1,0:T(4,128)S(1)}, f32[3,4,128]{2,1,0:T(4,128)S(1)}, u32[]{:S(2)}, u32[]{:S(2)}) collective-permute-start(f32[3,4,128]{2,1,0:T(4,128)S(1)} %get-tuple-element.22), channel_id=1, source_target_pairs={{1,0},{2,1},{3,2},{4,3},{5,4},{6,5},{7,6},{8,7},{9,8},{10,9},{11,1... | collective-permute-start | bytes 18440 | tf_op jit(solution)/shard_map/ppermute | solution.py:21
  84.6 2.7 %collective-permute-start = (f32[3,4,128]{2,1,0:T(4,128)S(1)}, f32[3,4,128]{2,1,0:T(4,128)S(1)}, u32[]{:S(2)}, u32[]{:S(2)}) collective-permute-start(f32[3,4,128]{2,1,0:T(4,128)S(1)} %get-tuple-element.21), channel_id=1, source_target_pairs={{0,1},{1,2},{2,3},{3,4},{4,5},{5,6},{6,7},{7,8},{8,9},{9,10},{10,1... | collective-permute-start | bytes 18440 | tf_op jit(solution)/shard_map/ppermute | solution.py:20
  87.7 2.4 %collective-permute-done = f32[3,4,128]{2,1,0:T(4,128)S(1)} collective-permute-done((f32[3,4,128]{2,1,0:T(4,128)S(1)}, f32[3,4,128]{2,1,0:T(4,128)S(1)}, u32[]{:S(2)}, u32[]{:S(2)}) %collective-permute-start) | collective-permute-done | bytes 6176 | tf_op jit(solution)/shard_map/ppermute | solution.py:20
  96.0 1.0 fusion.20
  97.4 0.7 fusion.16
  99.1 1.0 fusion.22
  100.5 0.7 fusion.11
  102.2 1.2 fusion.24
  108.3 0.7 broadcast_in_dim.41
  109.0 4.3 %all-to-all-start.2 = ((f32[8,3,1024]{2,1,0:T(4,128)}), f32[8,3,1024]{2,1,0:T(4,128)S(1)}, u32[]{:S(2)}, u32[]{:S(2)}) async-start(f32[8,3,1024]{2,1,0:T(4,128)} %broadcast_in_dim.41), calls=%async_computation.2 | async-start | bytes 262144 | tf_op jit(solution)/shard_map/all_to_all | solution.py:102
  113.8 0.8 reduce.5
  114.8 4.6 %all-to-all-done.2 = f32[8,3,1024]{2,1,0:T(4,128)S(1)} async-done(((f32[8,3,1024]{2,1,0:T(4,128)}), f32[8,3,1024]{2,1,0:T(4,128)S(1)}, u32[]{:S(2)}, u32[]{:S(2)}) %all-to-all-start.2) | async-done | bytes 98336 | tf_op jit(solution)/shard_map/all_to_all | solution.py:102
  119.7 3.5 %scatter_custom_fusion = f32[3,2112]{0,1:T(8,128)S(1)} fusion(s32[1024]{0:T(1024)} %bitcast.70, f32[1024,3]{1,0:T(8,128)S(1)} %copy.71, f32[]{:T(128)} %constant.21.clone.1), kind=kCustom, calls=%fused_computation.77 | custom fusion | bytes 25856 | tf_op jit(solution)/shard_map/scatter | solution.py:112
  123.7 0.8 copy.73
  124.5 8.5 %all-to-all-start.3 = ((f32[3,96,22]{2,0,1:T(4,128)}), f32[3,96,22]{2,0,1:T(4,128)S(1)}, u32[]{:S(2)}, u32[]{:S(2)}) async-start(f32[3,96,22]{2,0,1:T(4,128)} %copy.73), calls=%async_computation.3 | async-start | bytes 393216 | tf_op jit(solution)/shard_map/all_to_all | solution.py:113
  133.2 16.8 %all-to-all-done.3 = f32[3,96,22]{2,0,1:T(4,128)S(1)} async-done(((f32[3,96,22]{2,0,1:T(4,128)}), f32[3,96,22]{2,0,1:T(4,128)S(1)}, u32[]{:S(2)}, u32[]{:S(2)}) %all-to-all-start.3) | async-done | bytes 25376 | tf_op jit(solution)/shard_map/all_to_all | solution.py:113
  150.3 5.5 %fusion = f32[4,2048]{1,0:T(4,128)S(1)} fusion(s32[2112]{0:T(1024)S(1)} %all_to_all.22, f32[1,2112]{1,0:T(1,128)S(1)} %reshape.241, f32[3,2112]{1,0:T(4,128)S(1)} %broadcast_multiply_fusion), kind=kOutput, calls=%fused_computation.4 | convolution fusion | flops 211951872 | bytes 75008 | tf_op jit(solution)/shard_map/dot_general | solution.py:121
  (127 shorter events, 22.0 us)
Async XLA Ops:
  0.6 14.9 %copy-start.15 = (s32[1024]{0:T(1024)S(1)}, s32[1024]{0:T(1024)}, u32[]{:S(2)}) copy-start(s32[1024]{0:T(1024)} %param.15) | copy-start | bytes 12292
  0.6 14.9 %copy-start.17 = (s32[1024,1]{0,1:T(1,128)S(1)}, s32[1024,1]{0,1:T(1,128)}, u32[]{:S(2)}) copy-start(s32[1024,1]{0,1:T(1,128)} %param.14) | copy-start | bytes 12292
  0.7 33.1 %copy-start.14 = (s32[8,128]{1,0:T(8,128)S(1)}, s32[8,128]{1,0:T(8,128)}, u32[]{:S(2)}) copy-start(s32[8,128]{1,0:T(8,128)} %param.13) | copy-start | bytes 12292
  0.7 33.7 %copy-start.10 = (f32[2048]{0:T(1024)S(1)}, f32[2048]{0:T(1024)}, u32[]{:S(2)}) copy-start(f32[2048]{0:T(1024)} %param.12) | copy-start | bytes 24580
  0.7 33.7 %copy-start.8 = (f32[2,2048]{1,0:T(2,128)S(1)}, f32[2,2048]{1,0:T(2,128)}, u32[]{:S(2)}) copy-start(f32[2,2048]{1,0:T(2,128)} %param.11) | copy-start | bytes 49156
  0.7 33.7 %copy-start.18 = (f32[36]{0:T(128)S(1)}, f32[36]{0:T(128)}, u32[]{:S(2)}) copy-start(f32[36]{0:T(128)} %param.10) | copy-start | bytes 436
  0.7 33.7 %copy-start.19 = (f32[36]{0:T(128)S(1)}, f32[36]{0:T(128)}, u32[]{:S(2)}) copy-start(f32[36]{0:T(128)} %param.9) | copy-start | bytes 436
  2.2 91.7 %collective-permute-start.3 = (f32[162,4,128]{2,0,1:T(8,128)S(1)}, f32[162,4,128]{2,0,1:T(8,128)S(1)}, u32[]{:S(2)}, u32[]{:S(2)}) collective-permute-start(f32[162,4,128]{2,0,1:T(8,128)S(1)} %copy.77), channel_id=1, source_target_pairs={{1,0},{2,1},{3,2},{4,3},{5,4},{6,5},{7,6},{8,7},{9,8},{10,9},{11,1... | collective-permute-start | bytes 995336 | tf_op jit(solution)/shard_map/ppermute | solution.py:21
  13.6 80.4 %collective-permute-start.2 = (f32[162,4,128]{2,0,1:T(8,128)S(1)}, f32[162,4,128]{2,0,1:T(8,128)S(1)}, u32[]{:S(2)}, u32[]{:S(2)}) collective-permute-start(f32[162,4,128]{2,0,1:T(8,128)S(1)} %copy.76), channel_id=1, source_target_pairs={{0,1},{1,2},{2,3},{3,4},{4,5},{5,6},{6,7},{7,8},{8,9},{9,10},{10,1... | collective-permute-start | bytes 995336 | tf_op jit(solution)/shard_map/ppermute | solution.py:20
  16.1 19.0 %copy-start.9 = (s32[1024,1]{0,1:T(1,128)}, s32[1024,1]{0,1:T(1,128)S(1)}, u32[]{:S(2)}) copy-start(s32[1024,1]{0,1:T(1,128)S(1)} %get-tuple-element.6) | copy-start | bytes 12292
  17.8 28.9 %all-to-all-start = ((s32[96,1,22]{2,1,0:T(1,128)}), s32[96,1,22]{2,1,0:T(1,128)S(1)}, u32[]{:S(2)}, u32[]{:S(2)}) async-start(s32[96,1,22]{2,1,0:T(1,128)} %bitcast.3), calls=%async_computation | async-start | bytes 98304 | tf_op jit(solution)/shard_map/all_to_all | solution.py:73
  52.2 8.5 %copy-start.16 = (f32[162]{0:T(256)S(1)}, f32[162]{0:T(256)}, u32[]{:S(2)}) copy-start(f32[162]{0:T(256)} %get-tuple-element.3) | copy-start | bytes 1948
  52.2 9.1 %copy-start.4 = (f32[8,128]{1,0:T(8,128)S(1)}, f32[8,128]{1,0:T(8,128)}, u32[]{:S(2)}) copy-start(f32[8,128]{1,0:T(8,128)} %get-tuple-element.23) | copy-start | bytes 12292
  54.3 22.1 %all-to-all-start.1 = ((f32[3,96,22]{2,0,1:T(4,128)}), f32[3,96,22]{2,0,1:T(4,128)S(1)}, u32[]{:S(2)}, u32[]{:S(2)}) async-start(f32[3,96,22]{2,0,1:T(4,128)} %copy.62), calls=%async_computation.1 | async-start | bytes 393216 | tf_op jit(solution)/shard_map/all_to_all | solution.py:80
  80.3 9.8 %copy-start.3 = (f32[1,8,128]{2,1,0:T(8,128)S(1)}, f32[1,8,128]{2,1,0:T(8,128)}, u32[]{:S(2)}) copy-start(f32[1,8,128]{2,1,0:T(8,128)} %get-tuple-element.24) | copy-start | bytes 12292
  80.3 9.9 %copy-start.6 = (f32[162]{0:T(256)S(1)}, f32[162]{0:T(256)}, u32[]{:S(2)}) copy-start(f32[162]{0:T(256)} %get-tuple-element.29) | copy-start | bytes 1948
  80.3 9.9 %copy-start.7 = (f32[162]{0:T(256)S(1)}, f32[162]{0:T(256)}, u32[]{:S(2)}) copy-start(f32[162]{0:T(256)} %get-tuple-element.28) | copy-start | bytes 1948
  81.3 6.4 %collective-permute-start.1 = (f32[3,4,128]{2,1,0:T(4,128)S(1)}, f32[3,4,128]{2,1,0:T(4,128)S(1)}, u32[]{:S(2)}, u32[]{:S(2)}) collective-permute-start(f32[3,4,128]{2,1,0:T(4,128)S(1)} %get-tuple-element.22), channel_id=1, source_target_pairs={{1,0},{2,1},{3,2},{4,3},{5,4},{6,5},{7,6},{8,7},{9,8},{10,9},{11,1... | collective-permute-start | bytes 18440 | tf_op jit(solution)/shard_map/ppermute | solution.py:21
  84.6 5.5 %collective-permute-start = (f32[3,4,128]{2,1,0:T(4,128)S(1)}, f32[3,4,128]{2,1,0:T(4,128)S(1)}, u32[]{:S(2)}, u32[]{:S(2)}) collective-permute-start(f32[3,4,128]{2,1,0:T(4,128)S(1)} %get-tuple-element.21), channel_id=1, source_target_pairs={{0,1},{1,2},{2,3},{3,4},{4,5},{5,6},{6,7},{7,8},{8,9},{9,10},{10,1... | collective-permute-start | bytes 18440 | tf_op jit(solution)/shard_map/ppermute | solution.py:20
  93.6 1.1 copy-start
  106.0 0.7 copy-start.5
  107.0 0.8 copy-start.1
  107.0 0.8 copy-start.11
  107.0 0.8 copy-start.12
  107.0 0.8 copy-start.13
  109.0 10.4 %all-to-all-start.2 = ((f32[8,3,1024]{2,1,0:T(4,128)}), f32[8,3,1024]{2,1,0:T(4,128)S(1)}, u32[]{:S(2)}, u32[]{:S(2)}) async-start(f32[8,3,1024]{2,1,0:T(4,128)} %broadcast_in_dim.41), calls=%async_computation.2 | async-start | bytes 262144 | tf_op jit(solution)/shard_map/all_to_all | solution.py:102
  119.7 13.3 %copy-start.2 = (f32[96,1,22]{0,2,1:T(8,128)S(1)}, f32[96,1,22]{0,2,1:T(8,128)}, u32[]{:S(2)}) copy-start(f32[96,1,22]{0,2,1:T(8,128)} %get-tuple-element.4) | copy-start | bytes 25348
  124.5 25.6 %all-to-all-start.3 = ((f32[3,96,22]{2,0,1:T(4,128)}), f32[3,96,22]{2,0,1:T(4,128)S(1)}, u32[]{:S(2)}, u32[]{:S(2)}) async-start(f32[3,96,22]{2,0,1:T(4,128)} %copy.73), calls=%async_computation.3 | async-start | bytes 393216 | tf_op jit(solution)/shard_map/all_to_all | solution.py:113

commit v5 on v3

--- a/solution.py
+++ b/solution.py
@@ -65,7 +65,10 @@
     same_before = (owners[None, :] == owners[:, None]) & (cell_ids[None, :] < cell_ids[:, None])
     rank_in = jnp.sum(same_before.astype(jnp.int32), 1)
     position = owners * capacity + rank_in
-    requests = jnp.full((tile_count * capacity,), -1, jnp.int32).at[position].set(ocean_slot)
+    slot_ids = jnp.arange(tile_count * capacity, dtype=jnp.int32)
+    requests = (
+        jnp.sum(jnp.where(position[:, None] == slot_ids[None, :], ocean_slot[:, None] + 1, 0), 0) - 1
+    )
     asked_slots = lax.all_to_all(
         requests.reshape(tile_count, capacity), "tile", split_axis=0, concat_axis=0, tiled=True
     )

time: 154 us -> 151 us (0.981)
  local copies, waits for them, and re-layouts: 27.9 us -> 23.4 us
  other arithmetic: 16.5 us -> 18.2 us
    scatter x1 -> x0, local copies, waits for them, and re-layouts: 4.49 us -> none  [local(): jnp.full((tile_count * capacity,), -1, jnp.int32).at[position]]
where the time goes in v5:
time: 151 us; the launch traced here: 150 us
  waiting for transfers between devices  54.2 us (36%)
  starting transfers between devices  47.3 us (31%)
  local copies, waits for them, and re-layouts  23.4 us (15%)
  other arithmetic  18.2 us (12%)
  matrix products  5.95 us (4%)
    all_to_all x1, starting transfers between devices, local(): lax.all_to_all(requests.reshape(tile_count, capacity), 'tile', split_axis...  21.8 us
    all_to_all x1, waiting for transfers between devices, local(): lax.all_to_all(packed.reshape(3, tile_count, capacity), 'tile', split_axi...  16.9 us
    all_to_all x1, waiting for transfers between devices, local(): lax.all_to_all(answer, 'tile', split_axis=1, concat_axis=1, tiled=True)  15.9 us
    all_to_all x1, waiting for transfers between devices, local(): lax.all_to_all(requests.reshape(tile_count, capacity), 'tile', split_axis...  11 us
    all_to_all x1, starting transfers between devices, local(): lax.all_to_all(packed.reshape(3, tile_count, capacity), 'tile', split_axi...  8.83 us
    all_to_all x1, starting transfers between devices, local(): lax.all_to_all(answer, 'tile', split_axis=1, concat_axis=1, tiled=True)  6.35 us
    dot_general x1, matrix products, local(): jnp.dot(jnp.concatenate([arrived.reshape(3, -1) * weight[None], weight[No...  5.51 us
    all_to_all x1, waiting for transfers between devices, local(): lax.all_to_all(jnp.broadcast_to(partial_value[None], (sect_count,) + part...  4.72 us
  transfers between devices with their start and end apart: 6, of which 6 were waited for; matrix products, arithmetic and copies ran while one was open for 3% of the time, Pallas kernels for 0%

profile of v5, /device:TPU:8, one launch (start us, length us, event | category | flops | bytes accessed | tf_op | source)
XLA Modules:
  0.0 150.2 jit_solution(12957075402524557940)
XLA Ops:
  0.6 0.7 broadcast_add_fusion.9
  1.3 1.3 convert_reduce_fusion
  2.6 0.7 compare_select_fusion.2
  3.3 1.0 select_reduce_fusion
  4.3 0.8 sub.69
  5.0 21.8 %all-to-all-start = ((s32[96,1,22]{2,1,0:T(1,128)}), s32[96,1,22]{2,1,0:T(1,128)S(1)}, u32[]{:S(2)}, u32[]{:S(2)}) async-start(s32[96,1,22]{2,1,0:T(1,128)} %bitcast.3), calls=%async_computation | async-start | bytes 98304 | tf_op jit(solution)/shard_map/all_to_all | solution.py:72
  26.8 0.7 fusion.53
  27.5 0.8 pad_maximum_fusion.2
  28.3 0.8 select_reduce_fusion.1
  29.4 11.0 %all-to-all-done = s32[96,1,22]{2,1,0:T(1,128)S(1)} async-done(((s32[96,1,22]{2,1,0:T(1,128)}), s32[96,1,22]{2,1,0:T(1,128)S(1)}, u32[]{:S(2)}, u32[]{:S(2)}) %all-to-all-start) | async-done | bytes 8480 | tf_op jit(solution)/shard_map/all_to_all | solution.py:72
  40.5 4.0 %gather_fusion = f32[2112,3]{1,0:T(8,128)S(1)} fusion(f32[3,2048]{0,1:T(8,128)S(1)} %copy.59, s32[3072]{0:T(1024)S(1)} %pad_clamp_fusion), kind=kCustom, calls=%fused_computation | custom fusion | bytes 59136 | tf_op jit(solution)/shard_map/gather | solution.py:78
  45.3 0.8 copy.61
  46.1 6.3 %all-to-all-start.1 = ((f32[3,96,22]{2,0,1:T(4,128)}), f32[3,96,22]{2,0,1:T(4,128)S(1)}, u32[]{:S(2)}, u32[]{:S(2)}) async-start(f32[3,96,22]{2,0,1:T(4,128)} %copy.61), calls=%async_computation.1 | async-start | bytes 393216 | tf_op jit(solution)/shard_map/all_to_all | solution.py:79
  52.8 15.9 %all-to-all-done.1 = f32[3,96,22]{2,0,1:T(4,128)S(1)} async-done(((f32[3,96,22]{2,0,1:T(4,128)}), f32[3,96,22]{2,0,1:T(4,128)S(1)}, u32[]{:S(2)}, u32[]{:S(2)}) %all-to-all-start.1) | async-done | bytes 25376 | tf_op jit(solution)/shard_map/all_to_all | solution.py:79
  69.3 2.8 %gather_fusion.1 = f32[1024,3]{1,0:T(8,128)S(1)} fusion(f32[3,2112]{0,1:T(8,128)S(1)} %copy.63, s32[1024]{0:T(1024)S(1)} %broadcast_clamp_fusion), kind=kCustom, calls=%fused_computation.1 | custom fusion | bytes 28672 | tf_op jit(solution)/shard_map/gather | solution.py:80
  72.5 3.1 %collective-permute-start.1 = (f32[165,4,128]{2,0,1:T(8,128)S(1)}, f32[165,4,128]{2,0,1:T(8,128)S(1)}, u32[]{:S(2)}, u32[]{:S(2)}) collective-permute-start(f32[165,4,128]{2,0,1:T(8,128)S(1)} %copy.66), channel_id=1, source_target_pairs={{1,0},{2,1},{3,2},{4,3},{5,4},{6,5},{7,6},{8,7},{9,8},{10,9},{11,1... | collective-permute-start | bytes 1013768 | tf_op jit(solution)/shard_map/ppermute | solution.py:21
  75.6 2.9 %collective-permute-start = (f32[165,4,128]{2,0,1:T(8,128)S(1)}, f32[165,4,128]{2,0,1:T(8,128)S(1)}, u32[]{:S(2)}, u32[]{:S(2)}) collective-permute-start(f32[165,4,128]{2,0,1:T(8,128)S(1)} %copy.65), channel_id=1, source_target_pairs={{0,1},{1,2},{2,3},{3,4},{4,5},{5,6},{6,7},{7,8},{8,9},{9,10},{10,1... | collective-permute-start | bytes 1013768 | tf_op jit(solution)/shard_map/ppermute | solution.py:20
  79.0 2.6 %collective-permute-done.1 = f32[165,4,128]{2,0,1:T(8,128)S(1)} collective-permute-done((f32[165,4,128]{2,0,1:T(8,128)S(1)}, f32[165,4,128]{2,0,1:T(8,128)S(1)}, u32[]{:S(2)}, u32[]{:S(2)}) %collective-permute-start.1) | collective-permute-done | bytes 337952 | tf_op jit(solution)/shard_map/ppermute | solution.py:21
  81.7 3.1 %collective-permute-done = f32[165,4,128]{2,0,1:T(8,128)S(1)} collective-permute-done((f32[165,4,128]{2,0,1:T(8,128)S(1)}, f32[165,4,128]{2,0,1:T(8,128)S(1)}, u32[]{:S(2)}, u32[]{:S(2)}) %collective-permute-start) | collective-permute-done | bytes 337952 | tf_op jit(solution)/shard_map/ppermute | solution.py:20
  87.1 1.0 fusion.20
  88.6 0.8 fusion.16
  91.3 1.0 fusion.22
  95.4 1.2 fusion.24
  101.9 0.7 broadcast_in_dim.41
  102.5 4.3 %all-to-all-start.2 = ((f32[8,3,1024]{2,1,0:T(4,128)}), f32[8,3,1024]{2,1,0:T(4,128)S(1)}, u32[]{:S(2)}, u32[]{:S(2)}) async-start(f32[8,3,1024]{2,1,0:T(4,128)} %broadcast_in_dim.41), calls=%async_computation.2 | async-start | bytes 262144 | tf_op jit(solution)/shard_map/all_to_all | solution.py:101
  107.3 0.8 reduce.5
  108.2 4.7 %all-to-all-done.2 = f32[8,3,1024]{2,1,0:T(4,128)S(1)} async-done(((f32[8,3,1024]{2,1,0:T(4,128)}), f32[8,3,1024]{2,1,0:T(4,128)S(1)}, u32[]{:S(2)}, u32[]{:S(2)}) %all-to-all-start.2) | async-done | bytes 98336 | tf_op jit(solution)/shard_map/all_to_all | solution.py:101
  113.2 3.4 %scatter_custom_fusion = f32[3,2112]{0,1:T(8,128)S(1)} fusion(s32[1024]{0:T(1024)S(1)} %bitcast.70, f32[1024,3]{1,0:T(8,128)S(1)} %copy.70, f32[]{:T(128)} %constant.21.clone.1), kind=kCustom, calls=%fused_computation.78 | custom fusion | bytes 25348 | tf_op jit(solution)/shard_map/scatter | solution.py:111
  117.1 0.8 copy.72
  117.9 8.8 %all-to-all-start.3 = ((f32[3,96,22]{2,0,1:T(4,128)}), f32[3,96,22]{2,0,1:T(4,128)S(1)}, u32[]{:S(2)}, u32[]{:S(2)}) async-start(f32[3,96,22]{2,0,1:T(4,128)} %copy.72), calls=%async_computation.3 | async-start | bytes 393216 | tf_op jit(solution)/shard_map/all_to_all | solution.py:112
  127.0 16.9 %all-to-all-done.3 = f32[3,96,22]{2,0,1:T(4,128)S(1)} async-done(((f32[3,96,22]{2,0,1:T(4,128)}), f32[3,96,22]{2,0,1:T(4,128)S(1)}, u32[]{:S(2)}, u32[]{:S(2)}) %all-to-all-start.3) | async-done | bytes 25376 | tf_op jit(solution)/shard_map/all_to_all | solution.py:112
  144.0 5.5 %fusion = f32[4,2048]{1,0:T(4,128)S(1)} fusion(s32[2112]{0:T(1024)S(1)} %all_to_all.22, f32[1,2112]{1,0:T(1,128)S(1)} %reshape.241, f32[3,2112]{1,0:T(4,128)S(1)} %broadcast_multiply_fusion), kind=kOutput, calls=%fused_computation.4 | convolution fusion | flops 211951872 | bytes 75008 | tf_op jit(solution)/shard_map/dot_general | solution.py:120
  (85 shorter events, 18.3 us)
Async XLA Ops:
  5.0 35.4 %all-to-all-start = ((s32[96,1,22]{2,1,0:T(1,128)}), s32[96,1,22]{2,1,0:T(1,128)S(1)}, u32[]{:S(2)}, u32[]{:S(2)}) async-start(s32[96,1,22]{2,1,0:T(1,128)} %bitcast.3), calls=%async_computation | async-start | bytes 98304 | tf_op jit(solution)/shard_map/all_to_all | solution.py:72
  46.1 22.6 %all-to-all-start.1 = ((f32[3,96,22]{2,0,1:T(4,128)}), f32[3,96,22]{2,0,1:T(4,128)S(1)}, u32[]{:S(2)}, u32[]{:S(2)}) async-start(f32[3,96,22]{2,0,1:T(4,128)} %copy.61), calls=%async_computation.1 | async-start | bytes 393216 | tf_op jit(solution)/shard_map/all_to_all | solution.py:79
  52.5 19.7 %copy-start = (f32[162,8,128]{2,1,0:T(8,128)S(1)}, f32[162,8,128]{2,1,0:T(8,128)}, u32[]{:S(2)}) copy-start(f32[162,8,128]{2,1,0:T(8,128)} %param.8) | copy-start | bytes 1990660
  72.5 9.1 %collective-permute-start.1 = (f32[165,4,128]{2,0,1:T(8,128)S(1)}, f32[165,4,128]{2,0,1:T(8,128)S(1)}, u32[]{:S(2)}, u32[]{:S(2)}) collective-permute-start(f32[165,4,128]{2,0,1:T(8,128)S(1)} %copy.66), channel_id=1, source_target_pairs={{1,0},{2,1},{3,2},{4,3},{5,4},{6,5},{7,6},{8,7},{9,8},{10,9},{11,1... | collective-permute-start | bytes 1013768 | tf_op jit(solution)/shard_map/ppermute | solution.py:21
  75.6 9.1 %collective-permute-start = (f32[165,4,128]{2,0,1:T(8,128)S(1)}, f32[165,4,128]{2,0,1:T(8,128)S(1)}, u32[]{:S(2)}, u32[]{:S(2)}) collective-permute-start(f32[165,4,128]{2,0,1:T(8,128)S(1)} %copy.65), channel_id=1, source_target_pairs={{0,1},{1,2},{2,3},{3,4},{4,5},{5,6},{6,7},{7,8},{8,9},{9,10},{10,1... | collective-permute-start | bytes 1013768 | tf_op jit(solution)/shard_map/ppermute | solution.py:20
  100.6 0.8 copy-start.1
  102.5 10.4 %all-to-all-start.2 = ((f32[8,3,1024]{2,1,0:T(4,128)}), f32[8,3,1024]{2,1,0:T(4,128)S(1)}, u32[]{:S(2)}, u32[]{:S(2)}) async-start(f32[8,3,1024]{2,1,0:T(4,128)} %broadcast_in_dim.41), calls=%async_computation.2 | async-start | bytes 262144 | tf_op jit(solution)/shard_map/all_to_all | solution.py:101
  117.9 25.9 %all-to-all-start.3 = ((f32[3,96,22]{2,0,1:T(4,128)}), f32[3,96,22]{2,0,1:T(4,128)S(1)}, u32[]{:S(2)}, u32[]{:S(2)}) async-start(f32[3,96,22]{2,0,1:T(4,128)} %copy.72), calls=%async_computation.3 | async-start | bytes 393216 | tf_op jit(solution)/shard_map/all_to_all | solution.py:112

commit v6 on v5

--- a/solution.py
+++ b/solution.py
@@ -1,8 +1,11 @@
+import functools
 import math
 
 import jax
 import jax.numpy as jnp
 from jax import lax
+from jax.experimental import pallas as pl
+from jax.experimental.pallas import tpu as pltpu
 from jax.sharding import PartitionSpec as P
 
 NDIR = 36
@@ -38,6 +41,53 @@
     return flow_fields[2, 1:-1] * (middle - div_x - div_y)
 
 
+def propagate_kernel(speed_ref, energy_ref, flow_ref, out_ref, *, block, steps, rows_out):
+    rows = energy_ref.shape[1]
+    lanes = energy_ref.shape[2]
+    base = pl.program_id(0) * block
+    u = flow_ref[0]
+    v = flow_ref[1]
+    m = flow_ref[2]
+
+    def one_bin(b, carry):
+        vel_x = speed_ref[0, base + b] + u
+        vel_y = speed_ref[1, base + b] + v
+        face_x = 0.5 * (vel_x + pltpu.roll(vel_x, lanes - 1, 1))
+        face_y = 0.5 * (vel_y + pltpu.roll(vel_y, rows - 1, 0))
+        pos_x = jnp.maximum(face_x, 0.0)
+        neg_x = jnp.minimum(face_x, 0.0)
+        pos_y = jnp.maximum(face_y, 0.0)
+        neg_y = jnp.minimum(face_y, 0.0)
+        energy = energy_ref[b]
+        for _ in range(steps):
+            flux_x = pos_x * energy + neg_x * pltpu.roll(energy, lanes - 1, 1)
+            div_x = flux_x - pltpu.roll(flux_x, 1, 1)
+            flux_y = pos_y * energy + neg_y * pltpu.roll(energy, rows - 1, 0)
+            div_y = flux_y - pltpu.roll(flux_y, 1, 0)
+            energy = m * (energy - div_x - div_y)
+        out_ref[b] = pltpu.roll(energy, rows - steps, 0)[:rows_out]
+        return carry
+
+    lax.fori_loop(0, block, one_bin, 0)
+
+
+def propagate(speeds, extended, bins, rows_out):
+    rows, lanes = extended.shape[1:]
+    block = max(d for d in range(1, 33) if bins % d == 0)
+    kernel = functools.partial(propagate_kernel, block=block, steps=STEPS, rows_out=rows_out)
+    return pl.pallas_call(
+        kernel,
+        grid=(bins // block,),
+        in_specs=[
+            pl.BlockSpec(memory_space=pltpu.MemorySpace.SMEM),
+            pl.BlockSpec((block, rows, lanes), lambda i: (i, 0, 0)),
+            pl.BlockSpec((3, rows, lanes), lambda i: (bins // 3, 0, 0)),
+        ],
+        out_specs=pl.BlockSpec((block, rows_out, lanes), lambda i: (i, 0, 0)),
+        out_shape=jax.ShapeDtypeStruct((bins, rows_out, lanes), jnp.float32),
+    )(speeds, extended, extended)
+
+
 def local(
     spectrum, courant, group_ratio, ocean_currents, elevation, sea_mask, owner_tile, ocean_slot
 ):
@@ -58,8 +108,6 @@
     angles = (dir_ids.astype(jnp.float32) + 0.5) * (2.0 * math.pi / NDIR)
     cos_dir = jnp.cos(angles)
     sin_dir = jnp.sin(angles)
-    speed_x = (group_speed * cos_dir)[:, None, None]
-    speed_y = (group_speed * sin_dir)[:, None, None]
     owners = owner_tile[:, 0]
     cell_ids = jnp.arange(owners.shape[0], dtype=jnp.int32)
     same_before = (owners[None, :] == owners[:, None]) & (cell_ids[None, :] < cell_ids[:, None])
@@ -81,10 +129,8 @@
     sea_float = sea_mask.astype(jnp.float32)
     flow_fields = jnp.concatenate([at_cells[:2].reshape(2, row_count, columns), sea_float[None]], 0)
     extended = with_halo(jnp.concatenate([spectrum, flow_fields], 0), (("tile", 1),), STEPS)
-    energy = extended[:bin_count]
-    for sub_step in range(STEPS):
-        flows_now = extended[bin_count:, sub_step : extended.shape[1] - sub_step]
-        energy = advance(energy, flows_now, speed_x, speed_y)
+    speeds = jnp.stack([group_speed * cos_dir, group_speed * sin_dir], 0)
+    energy = propagate(speeds, extended, bin_count, row_count)
     weights = jnp.stack(
         [
             ratio_bin * (1.0 + cos_dir * cos_dir) - 0.5,

time: 151 us -> 234 us (1.55)
  Pallas kernels: 0 us -> 95 us
  other arithmetic: 18.2 us -> 9.1 us
  local copies, waits for them, and re-layouts: 23.4 us -> 18.5 us
  starting transfers between devices: 47.3 us -> 50.4 us
    pallas_call x0 -> x1, Pallas kernels: none -> 95 us  [propagate(): pl.pallas_call(kernel, grid=(bins // block,), in_specs=[pl.BlockSpec(memo...]
    add x16 -> x0, other arithmetic: 7.49 us -> none  [the longest x4 3.9 us: advance(): jnp.maximum(face_x, 0.0) * middle + jnp.minimum(face_x, 0.0) * east_side]
    slice x21 -> x0, local copies, waits for them, and re-layouts: 5.21 us -> none  [the longest x8 1.86 us: advance(): face_x = 0.5 * (mid_vel + jnp.roll(mid_vel, -1, axis=2))]
    all_to_all x1, starting transfers between devices: 8.83 us -> 12 us  [local(): lax.all_to_all(packed.reshape(3, tile_count, capacity), 'tile', split_axi...]
    mul x5 -> x0, other arithmetic: 2.59 us -> none  [the longest x4 2.53 us: advance(): return flow_fields[2, 1:-1] * (middle - div_x - div_y)]
  transfers between devices with their start and end apart: 6 -> 6, of which waited for: 6 -> 6; matrix products, arithmetic and copies ran while one was open for 3% -> 2% of each run, Pallas kernels for 0% -> 0%
where the time goes in v6:
time: 234 us
  Pallas kernels  95 us (41%)
  waiting for transfers between devices  53.8 us (23%)
  starting transfers between devices  50.4 us (22%)
  local copies, waits for them, and re-layouts  18.5 us (8%)
  other arithmetic  9.1 us (4%)
  matrix products  5.96 us (3%)
    pallas_call x1, Pallas kernels, propagate(): pl.pallas_call(kernel, grid=(bins // block,), in_specs=[pl.BlockSpec(memo...  95 us
    all_to_all x1, starting transfers between devices, local(): lax.all_to_all(requests.reshape(tile_count, capacity), 'tile', split_axis...  21.8 us
    all_to_all x1, waiting for transfers between devices, local(): lax.all_to_all(packed.reshape(3, tile_count, capacity), 'tile', split_axi...  16.9 us
    all_to_all x1, waiting for transfers between devices, local(): lax.all_to_all(answer, 'tile', split_axis=1, concat_axis=1, tiled=True)  16.1 us
    all_to_all x1, starting transfers between devices, local(): lax.all_to_all(packed.reshape(3, tile_count, capacity), 'tile', split_axi...  12 us
    all_to_all x1, waiting for transfers between devices, local(): lax.all_to_all(requests.reshape(tile_count, capacity), 'tile', split_axis...  11.7 us
    all_to_all x1, starting transfers between devices, local(): lax.all_to_all(answer, 'tile', split_axis=1, concat_axis=1, tiled=True)  6.48 us
    dot_general x1, matrix products, local(): jnp.dot(jnp.concatenate([arrived.reshape(3, -1) * weight[None], weight[No...  5.51 us
  transfers between devices with their start and end apart: 6, of which 6 were waited for; matrix products, arithmetic and copies ran while one was open for 2% of the time, Pallas kernels for 0%

profile of v6, /device:TPU:8, one launch (start us, length us, event | category | flops | bytes accessed | tf_op | source)
XLA Modules:
  0.0 233.7 jit_solution(11526929416590382118)
XLA Ops:
  0.6 1.3 convert_reduce_fusion
  1.9 0.7 compare_select_fusion.2
  2.6 0.7 broadcast_add_fusion.1
  3.3 1.0 select_reduce_fusion
  4.3 0.8 sub.20
  5.0 21.8 %all-to-all-start = ((s32[96,1,22]{2,1,0:T(1,128)}), s32[96,1,22]{2,1,0:T(1,128)S(1)}, u32[]{:S(2)}, u32[]{:S(2)}) async-start(s32[96,1,22]{2,1,0:T(1,128)} %bitcast.4), calls=%async_computation | async-start | bytes 98304 | tf_op jit(solution)/shard_map/all_to_all | solution.py:120
  26.8 0.7 fusion.25
  27.5 0.8 pad_maximum_fusion.2
  28.7 11.7 %all-to-all-done = s32[96,1,22]{2,1,0:T(1,128)S(1)} async-done(((s32[96,1,22]{2,1,0:T(1,128)}), s32[96,1,22]{2,1,0:T(1,128)S(1)}, u32[]{:S(2)}, u32[]{:S(2)}) %all-to-all-start) | async-done | bytes 8480 | tf_op jit(solution)/shard_map/all_to_all | solution.py:120
  40.8 4.0 %gather_fusion = f32[2112,3]{1,0:T(8,128)S(1)} fusion(f32[3,2048]{0,1:T(8,128)S(1)} %copy.53, s32[3072]{0:T(1024)S(1)} %pad_clamp_fusion), kind=kCustom, calls=%fused_computation | custom fusion | bytes 59136 | tf_op jit(solution)/shard_map/gather | solution.py:126
  45.3 0.8 copy.55
  46.1 6.5 %all-to-all-start.1 = ((f32[3,96,22]{2,0,1:T(4,128)}), f32[3,96,22]{2,0,1:T(4,128)S(1)}, u32[]{:S(2)}, u32[]{:S(2)}) async-start(f32[3,96,22]{2,0,1:T(4,128)} %copy.55), calls=%async_computation.1 | async-start | bytes 393216 | tf_op jit(solution)/shard_map/all_to_all | solution.py:127
  52.7 16.1 %all-to-all-done.1 = f32[3,96,22]{2,0,1:T(4,128)S(1)} async-done(((f32[3,96,22]{2,0,1:T(4,128)}), f32[3,96,22]{2,0,1:T(4,128)S(1)}, u32[]{:S(2)}, u32[]{:S(2)}) %all-to-all-start.1) | async-done | bytes 25376 | tf_op jit(solution)/shard_map/all_to_all | solution.py:127
  69.4 2.8 %gather_fusion.1 = f32[1024,3]{1,0:T(8,128)S(1)} fusion(f32[3,2112]{0,1:T(8,128)S(1)} %copy.57, s32[1024]{0:T(1024)S(1)} %broadcast_clamp_fusion), kind=kCustom, calls=%fused_computation.1 | custom fusion | bytes 28672 | tf_op jit(solution)/shard_map/gather | solution.py:128
  72.6 2.4 %collective-permute-start = (f32[165,4,128]{2,1,0:T(4,128)S(1)}, f32[165,4,128]{2,1,0:T(4,128)S(1)}, u32[]{:S(2)}, u32[]{:S(2)}) collective-permute-start(f32[165,4,128]{2,1,0:T(4,128)S(1)} %get-tuple-element.8), channel_id=1, source_target_pairs={{0,1},{1,2},{2,3},{3,4},{4,5},{5,6},{6,7},{7,8},{8,9},{9,10},{10,1... | collective-permute-start | bytes 1013768 | tf_op jit(solution)/shard_map/ppermute | solution.py:23
  75.0 3.4 %collective-permute-start.1 = (f32[165,4,128]{2,1,0:T(4,128)S(1)}, f32[165,4,128]{2,1,0:T(4,128)S(1)}, u32[]{:S(2)}, u32[]{:S(2)}) collective-permute-start(f32[165,4,128]{2,1,0:T(4,128)S(1)} %get-tuple-element.9), channel_id=1, source_target_pairs={{1,0},{2,1},{3,2},{4,3},{5,4},{6,5},{7,6},{8,7},{9,8},{10,9},{11,1... | collective-permute-start | bytes 1013768 | tf_op jit(solution)/shard_map/ppermute | solution.py:24
  78.8 0.6 pad_maximum_fusion.3.speed_ref
  79.7 1.9 collective-permute-done
  81.7 2.4 %collective-permute-done.1 = f32[165,4,128]{2,1,0:T(4,128)S(1)} collective-permute-done((f32[165,4,128]{2,1,0:T(4,128)S(1)}, f32[165,4,128]{2,1,0:T(4,128)S(1)}, u32[]{:S(2)}, u32[]{:S(2)}) %collective-permute-start.1) | collective-permute-done | bytes 337952 | tf_op jit(solution)/shard_map/ppermute | solution.py:24
  84.1 1.3 pad_maximum_fusion.energy_ref.flow_ref
  85.4 95.0 %shard_map.95 = f32[162,8,128]{2,1,0:T(8,128)} custom-call(f32[2,162]{1,0:T(2,128)} %pad_maximum_fusion.3.speed_ref, f32[165,16,128]{2,1,0:T(8,128)} %pad_maximum_fusion.energy_ref.flow_ref, f32[165,16,128]{2,1,0:T(8,128)} %pad_maximum_fusion.energy_ref.flow_ref), custom_call_target="tpu_custom_call" | custom-call | tf_op jit(solution)/shard_map/pallas_call | solution.py:78
  180.5 1.1 pad.19
  182.2 0.7 broadcast_in_dim.41
  182.8 4.3 %all-to-all-start.2 = ((f32[8,3,1024]{2,1,0:T(4,128)}), f32[8,3,1024]{2,1,0:T(4,128)S(1)}, u32[]{:S(2)}, u32[]{:S(2)}) async-start(f32[8,3,1024]{2,1,0:T(4,128)} %broadcast_in_dim.41), calls=%async_computation.2 | async-start | bytes 262144 | tf_op jit(solution)/shard_map/all_to_all | solution.py:147
  187.7 0.8 reduce.5
  188.6 4.7 %all-to-all-done.2 = f32[8,3,1024]{2,1,0:T(4,128)S(1)} async-done(((f32[8,3,1024]{2,1,0:T(4,128)}), f32[8,3,1024]{2,1,0:T(4,128)S(1)}, u32[]{:S(2)}, u32[]{:S(2)}) %all-to-all-start.2) | async-done | bytes 98336 | tf_op jit(solution)/shard_map/all_to_all | solution.py:147
  193.5 3.4 %scatter_custom_fusion = f32[3,2112]{0,1:T(8,128)S(1)} fusion(s32[1024]{0:T(1024)S(1)} %bitcast.41, f32[1024,3]{1,0:T(8,128)S(1)} %copy.60, f32[]{:T(128)} %constant.21.clone.1), kind=kCustom, calls=%fused_computation.14 | custom fusion | bytes 25348 | tf_op jit(solution)/shard_map/scatter | solution.py:157
  197.4 0.8 copy.62
  198.2 12.0 %all-to-all-start.3 = ((f32[3,96,22]{2,0,1:T(4,128)}), f32[3,96,22]{2,0,1:T(4,128)S(1)}, u32[]{:S(2)}, u32[]{:S(2)}) async-start(f32[3,96,22]{2,0,1:T(4,128)} %copy.62), calls=%async_computation.3 | async-start | bytes 393216 | tf_op jit(solution)/shard_map/all_to_all | solution.py:158
  210.5 16.9 %all-to-all-done.3 = f32[3,96,22]{2,0,1:T(4,128)S(1)} async-done(((f32[3,96,22]{2,0,1:T(4,128)}), f32[3,96,22]{2,0,1:T(4,128)S(1)}, u32[]{:S(2)}, u32[]{:S(2)}) %all-to-all-start.3) | async-done | bytes 25376 | tf_op jit(solution)/shard_map/all_to_all | solution.py:158
  227.6 5.5 %fusion = f32[4,2048]{1,0:T(4,128)S(1)} fusion(s32[2112]{0:T(1024)S(1)} %all_to_all.22, f32[1,2112]{1,0:T(1,128)S(1)} %reshape.231, f32[3,2112]{1,0:T(4,128)S(1)} %broadcast_multiply_fusion), kind=kOutput, calls=%fused_computation.4 | convolution fusion | flops 211951872 | bytes 75008 | tf_op jit(solution)/shard_map/dot_general | solution.py:166
  233.1 0.6 slice_divide_fusion
  (44 shorter events, 5.4 us)
Async XLA Ops:
  5.0 35.4 %all-to-all-start = ((s32[96,1,22]{2,1,0:T(1,128)}), s32[96,1,22]{2,1,0:T(1,128)S(1)}, u32[]{:S(2)}, u32[]{:S(2)}) async-start(s32[96,1,22]{2,1,0:T(1,128)} %bitcast.4), calls=%async_computation | async-start | bytes 98304 | tf_op jit(solution)/shard_map/all_to_all | solution.py:120
  44.8 7.9 %copy-start.1 = (f32[36]{0:T(128)S(1)}, f32[36]{0:T(128)}, u32[]{:S(2)}) copy-start(f32[36]{0:T(128)} %param.10) | copy-start | bytes 436
  44.8 7.9 %copy-start.2 = (f32[36]{0:T(128)S(1)}, f32[36]{0:T(128)}, u32[]{:S(2)}) copy-start(f32[36]{0:T(128)} %param.9) | copy-start | bytes 436
  46.1 26.3 %copy-start = (f32[162,8,128]{2,1,0:T(8,128)S(1)}, f32[162,8,128]{2,1,0:T(8,128)}, u32[]{:S(2)}) copy-start(f32[162,8,128]{2,1,0:T(8,128)} %param.8) | copy-start | bytes 1990660
  46.1 22.7 %all-to-all-start.1 = ((f32[3,96,22]{2,0,1:T(4,128)}), f32[3,96,22]{2,0,1:T(4,128)S(1)}, u32[]{:S(2)}, u32[]{:S(2)}) async-start(f32[3,96,22]{2,0,1:T(4,128)} %copy.55), calls=%async_computation.1 | async-start | bytes 393216 | tf_op jit(solution)/shard_map/all_to_all | solution.py:127
  72.6 9.1 %collective-permute-start = (f32[165,4,128]{2,1,0:T(4,128)S(1)}, f32[165,4,128]{2,1,0:T(4,128)S(1)}, u32[]{:S(2)}, u32[]{:S(2)}) collective-permute-start(f32[165,4,128]{2,1,0:T(4,128)S(1)} %get-tuple-element.8), channel_id=1, source_target_pairs={{0,1},{1,2},{2,3},{3,4},{4,5},{5,6},{6,7},{7,8},{8,9},{9,10},{10,1... | collective-permute-start | bytes 1013768 | tf_op jit(solution)/shard_map/ppermute | solution.py:23
  75.0 9.1 %collective-permute-start.1 = (f32[165,4,128]{2,1,0:T(4,128)S(1)}, f32[165,4,128]{2,1,0:T(4,128)S(1)}, u32[]{:S(2)}, u32[]{:S(2)}) collective-permute-start(f32[165,4,128]{2,1,0:T(4,128)S(1)} %get-tuple-element.9), channel_id=1, source_target_pairs={{1,0},{2,1},{3,2},{4,3},{5,4},{6,5},{7,6},{8,7},{9,8},{10,9},{11,1... | collective-permute-start | bytes 1013768 | tf_op jit(solution)/shard_map/ppermute | solution.py:24
  182.8 10.4 %all-to-all-start.2 = ((f32[8,3,1024]{2,1,0:T(4,128)}), f32[8,3,1024]{2,1,0:T(4,128)S(1)}, u32[]{:S(2)}, u32[]{:S(2)}) async-start(f32[8,3,1024]{2,1,0:T(4,128)} %broadcast_in_dim.41), calls=%async_computation.2 | async-start | bytes 262144 | tf_op jit(solution)/shard_map/all_to_all | solution.py:147
  198.2 29.2 %all-to-all-start.3 = ((f32[3,96,22]{2,0,1:T(4,128)}), f32[3,96,22]{2,0,1:T(4,128)S(1)}, u32[]{:S(2)}, u32[]{:S(2)}) async-start(f32[3,96,22]{2,0,1:T(4,128)} %copy.62), calls=%async_computation.3 | async-start | bytes 393216 | tf_op jit(solution)/shard_map/all_to_all | solution.py:158

commit v7 on v6

--- a/solution.py
+++ b/solution.py
@@ -68,7 +68,7 @@
         out_ref[b] = pltpu.roll(energy, rows - steps, 0)[:rows_out]
         return carry
 
-    lax.fori_loop(0, block, one_bin, 0)
+    lax.fori_loop(0, block, one_bin, 0, unroll=True)
 
 
 def propagate(speeds, extended, bins, rows_out):

time: 234 us -> 147 us (0.63)
  Pallas kernels: 95 us -> 6.89 us
    pallas_call x1, Pallas kernels: 95 us -> 6.89 us  [propagate(): pl.pallas_call(kernel, grid=(bins // block,), in_specs=[pl.BlockSpec(memo...]
  transfers between devices with their start and end apart: 6 -> 6, of which waited for: 6 -> 6; matrix products, arithmetic and copies ran while one was open for 2% -> 3% of each run, Pallas kernels for 0% -> 0%
where the time goes in v7:
time: 147 us; the launch traced here: 146 us
  waiting for transfers between devices  53.8 us (37%)
  starting transfers between devices  50.6 us (34%)
  local copies, waits for them, and re-layouts  18.5 us (13%)
  other arithmetic  9.1 us (6%)
  Pallas kernels  6.89 us (5%)
  matrix products  5.96 us (4%)
    all_to_all x1, starting transfers between devices, local(): lax.all_to_all(requests.reshape(tile_count, capacity), 'tile', split_axis...  21.8 us
    all_to_all x1, waiting for transfers between devices, local(): lax.all_to_all(packed.reshape(3, tile_count, capacity), 'tile', split_axi...  16.9 us
    all_to_all x1, waiting for transfers between devices, local(): lax.all_to_all(answer, 'tile', split_axis=1, concat_axis=1, tiled=True)  16.1 us
    all_to_all x1, starting transfers between devices, local(): lax.all_to_all(packed.reshape(3, tile_count, capacity), 'tile', split_axi...  12.2 us
    all_to_all x1, waiting for transfers between devices, local(): lax.all_to_all(requests.reshape(tile_count, capacity), 'tile', split_axis...  11.7 us
    pallas_call x1, Pallas kernels, propagate(): pl.pallas_call(kernel, grid=(bins // block,), in_specs=[pl.BlockSpec(memo...  6.89 us
    all_to_all x1, starting transfers between devices, local(): lax.all_to_all(answer, 'tile', split_axis=1, concat_axis=1, tiled=True)  6.48 us
    dot_general x1, matrix products, local(): jnp.dot(jnp.concatenate([arrived.reshape(3, -1) * weight[None], weight[No...  5.51 us
  transfers between devices with their start and end apart: 6, of which 6 were waited for; matrix products, arithmetic and copies ran while one was open for 3% of the time, Pallas kernels for 0%

profile of v7, /device:TPU:8, one launch (start us, length us, event | category | flops | bytes accessed | tf_op | source)
XLA Modules:
  0.0 145.8 jit_solution(1233398488963919722)
XLA Ops:
  0.6 1.3 convert_reduce_fusion
  1.9 0.7 compare_select_fusion.2
  2.6 0.7 broadcast_add_fusion.1
  3.3 1.0 select_reduce_fusion
  4.3 0.8 sub.20
  5.0 21.8 %all-to-all-start = ((s32[96,1,22]{2,1,0:T(1,128)}), s32[96,1,22]{2,1,0:T(1,128)S(1)}, u32[]{:S(2)}, u32[]{:S(2)}) async-start(s32[96,1,22]{2,1,0:T(1,128)} %bitcast.4), calls=%async_computation | async-start | bytes 98304 | tf_op jit(solution)/shard_map/all_to_all | solution.py:120
  26.8 0.7 fusion.25
  27.5 0.8 pad_maximum_fusion.2
  28.7 11.7 %all-to-all-done = s32[96,1,22]{2,1,0:T(1,128)S(1)} async-done(((s32[96,1,22]{2,1,0:T(1,128)}), s32[96,1,22]{2,1,0:T(1,128)S(1)}, u32[]{:S(2)}, u32[]{:S(2)}) %all-to-all-start) | async-done | bytes 8480 | tf_op jit(solution)/shard_map/all_to_all | solution.py:120
  40.8 4.0 %gather_fusion = f32[2112,3]{1,0:T(8,128)S(1)} fusion(f32[3,2048]{0,1:T(8,128)S(1)} %copy.53, s32[3072]{0:T(1024)S(1)} %pad_clamp_fusion), kind=kCustom, calls=%fused_computation | custom fusion | bytes 59136 | tf_op jit(solution)/shard_map/gather | solution.py:126
  45.3 0.8 copy.55
  46.1 6.5 %all-to-all-start.1 = ((f32[3,96,22]{2,0,1:T(4,128)}), f32[3,96,22]{2,0,1:T(4,128)S(1)}, u32[]{:S(2)}, u32[]{:S(2)}) async-start(f32[3,96,22]{2,0,1:T(4,128)} %copy.55), calls=%async_computation.1 | async-start | bytes 393216 | tf_op jit(solution)/shard_map/all_to_all | solution.py:127
  52.7 16.1 %all-to-all-done.1 = f32[3,96,22]{2,0,1:T(4,128)S(1)} async-done(((f32[3,96,22]{2,0,1:T(4,128)}), f32[3,96,22]{2,0,1:T(4,128)S(1)}, u32[]{:S(2)}, u32[]{:S(2)}) %all-to-all-start.1) | async-done | bytes 25376 | tf_op jit(solution)/shard_map/all_to_all | solution.py:127
  69.4 2.8 %gather_fusion.1 = f32[1024,3]{1,0:T(8,128)S(1)} fusion(f32[3,2112]{0,1:T(8,128)S(1)} %copy.57, s32[1024]{0:T(1024)S(1)} %broadcast_clamp_fusion), kind=kCustom, calls=%fused_computation.1 | custom fusion | bytes 28672 | tf_op jit(solution)/shard_map/gather | solution.py:128
  72.6 2.4 %collective-permute-start = (f32[165,4,128]{2,1,0:T(4,128)S(1)}, f32[165,4,128]{2,1,0:T(4,128)S(1)}, u32[]{:S(2)}, u32[]{:S(2)}) collective-permute-start(f32[165,4,128]{2,1,0:T(4,128)S(1)} %get-tuple-element.8), channel_id=1, source_target_pairs={{0,1},{1,2},{2,3},{3,4},{4,5},{5,6},{6,7},{7,8},{8,9},{9,10},{10,1... | collective-permute-start | bytes 1013768 | tf_op jit(solution)/shard_map/ppermute | solution.py:23
  75.0 3.4 %collective-permute-start.1 = (f32[165,4,128]{2,1,0:T(4,128)S(1)}, f32[165,4,128]{2,1,0:T(4,128)S(1)}, u32[]{:S(2)}, u32[]{:S(2)}) collective-permute-start(f32[165,4,128]{2,1,0:T(4,128)S(1)} %get-tuple-element.9), channel_id=1, source_target_pairs={{1,0},{2,1},{3,2},{4,3},{5,4},{6,5},{7,6},{8,7},{9,8},{10,9},{11,1... | collective-permute-start | bytes 1013768 | tf_op jit(solution)/shard_map/ppermute | solution.py:24
  78.8 0.6 pad_maximum_fusion.3.speed_ref
  79.7 1.9 %collective-permute-done = f32[165,4,128]{2,1,0:T(4,128)S(1)} collective-permute-done((f32[165,4,128]{2,1,0:T(4,128)S(1)}, f32[165,4,128]{2,1,0:T(4,128)S(1)}, u32[]{:S(2)}, u32[]{:S(2)}) %collective-permute-start) | collective-permute-done | bytes 337952 | tf_op jit(solution)/shard_map/ppermute | solution.py:23
  81.7 2.4 %collective-permute-done.1 = f32[165,4,128]{2,1,0:T(4,128)S(1)} collective-permute-done((f32[165,4,128]{2,1,0:T(4,128)S(1)}, f32[165,4,128]{2,1,0:T(4,128)S(1)}, u32[]{:S(2)}, u32[]{:S(2)}) %collective-permute-start.1) | collective-permute-done | bytes 337952 | tf_op jit(solution)/shard_map/ppermute | solution.py:24
  84.1 1.3 pad_maximum_fusion.energy_ref.flow_ref
  85.4 6.9 %shard_map.95 = f32[162,8,128]{2,1,0:T(8,128)} custom-call(f32[2,162]{1,0:T(2,128)} %pad_maximum_fusion.3.speed_ref, f32[165,16,128]{2,1,0:T(8,128)} %pad_maximum_fusion.energy_ref.flow_ref, f32[165,16,128]{2,1,0:T(8,128)} %pad_maximum_fusion.energy_ref.flow_ref), custom_call_target="tpu_custom_call" | custom-call | tf_op jit(solution)/shard_map/pallas_call | solution.py:78
  92.3 1.1 pad.19
  94.0 0.7 broadcast_in_dim.41
  94.7 4.3 %all-to-all-start.2 = ((f32[8,3,1024]{2,1,0:T(4,128)}), f32[8,3,1024]{2,1,0:T(4,128)S(1)}, u32[]{:S(2)}, u32[]{:S(2)}) async-start(f32[8,3,1024]{2,1,0:T(4,128)} %broadcast_in_dim.41), calls=%async_computation.2 | async-start | bytes 262144 | tf_op jit(solution)/shard_map/all_to_all | solution.py:147
  99.5 0.8 reduce.5
  100.4 4.7 %all-to-all-done.2 = f32[8,3,1024]{2,1,0:T(4,128)S(1)} async-done(((f32[8,3,1024]{2,1,0:T(4,128)}), f32[8,3,1024]{2,1,0:T(4,128)S(1)}, u32[]{:S(2)}, u32[]{:S(2)}) %all-to-all-start.2) | async-done | bytes 98336 | tf_op jit(solution)/shard_map/all_to_all | solution.py:147
  105.4 3.4 %scatter_custom_fusion = f32[3,2112]{0,1:T(8,128)S(1)} fusion(s32[1024]{0:T(1024)S(1)} %bitcast.41, f32[1024,3]{1,0:T(8,128)S(1)} %copy.60, f32[]{:T(128)} %constant.21.clone.1), kind=kCustom, calls=%fused_computation.14 | custom fusion | bytes 25348 | tf_op jit(solution)/shard_map/scatter | solution.py:157
  109.3 0.8 copy.62
  110.1 12.2 %all-to-all-start.3 = ((f32[3,96,22]{2,0,1:T(4,128)}), f32[3,96,22]{2,0,1:T(4,128)S(1)}, u32[]{:S(2)}, u32[]{:S(2)}) async-start(f32[3,96,22]{2,0,1:T(4,128)} %copy.62), calls=%async_computation.3 | async-start | bytes 393216 | tf_op jit(solution)/shard_map/all_to_all | solution.py:158
  122.6 16.9 %all-to-all-done.3 = f32[3,96,22]{2,0,1:T(4,128)S(1)} async-done(((f32[3,96,22]{2,0,1:T(4,128)}), f32[3,96,22]{2,0,1:T(4,128)S(1)}, u32[]{:S(2)}, u32[]{:S(2)}) %all-to-all-start.3) | async-done | bytes 25376 | tf_op jit(solution)/shard_map/all_to_all | solution.py:158
  139.6 5.5 %fusion = f32[4,2048]{1,0:T(4,128)S(1)} fusion(s32[2112]{0:T(1024)S(1)} %all_to_all.22, f32[1,2112]{1,0:T(1,128)S(1)} %reshape.231, f32[3,2112]{1,0:T(4,128)S(1)} %broadcast_multiply_fusion), kind=kOutput, calls=%fused_computation.4 | convolution fusion | flops 211951872 | bytes 75008 | tf_op jit(solution)/shard_map/dot_general | solution.py:166
  145.1 0.6 slice_divide_fusion
  (44 shorter events, 5.4 us)
Async XLA Ops:
  5.0 35.4 %all-to-all-start = ((s32[96,1,22]{2,1,0:T(1,128)}), s32[96,1,22]{2,1,0:T(1,128)S(1)}, u32[]{:S(2)}, u32[]{:S(2)}) async-start(s32[96,1,22]{2,1,0:T(1,128)} %bitcast.4), calls=%async_computation | async-start | bytes 98304 | tf_op jit(solution)/shard_map/all_to_all | solution.py:120
  44.8 7.9 %copy-start.1 = (f32[36]{0:T(128)S(1)}, f32[36]{0:T(128)}, u32[]{:S(2)}) copy-start(f32[36]{0:T(128)} %param.10) | copy-start | bytes 436
  44.8 7.9 %copy-start.2 = (f32[36]{0:T(128)S(1)}, f32[36]{0:T(128)}, u32[]{:S(2)}) copy-start(f32[36]{0:T(128)} %param.9) | copy-start | bytes 436
  46.1 26.3 %copy-start = (f32[162,8,128]{2,1,0:T(8,128)S(1)}, f32[162,8,128]{2,1,0:T(8,128)}, u32[]{:S(2)}) copy-start(f32[162,8,128]{2,1,0:T(8,128)} %param.8) | copy-start | bytes 1990660
  46.1 22.7 %all-to-all-start.1 = ((f32[3,96,22]{2,0,1:T(4,128)}), f32[3,96,22]{2,0,1:T(4,128)S(1)}, u32[]{:S(2)}, u32[]{:S(2)}) async-start(f32[3,96,22]{2,0,1:T(4,128)} %copy.55), calls=%async_computation.1 | async-start | bytes 393216 | tf_op jit(solution)/shard_map/all_to_all | solution.py:127
  72.6 9.1 %collective-permute-start = (f32[165,4,128]{2,1,0:T(4,128)S(1)}, f32[165,4,128]{2,1,0:T(4,128)S(1)}, u32[]{:S(2)}, u32[]{:S(2)}) collective-permute-start(f32[165,4,128]{2,1,0:T(4,128)S(1)} %get-tuple-element.8), channel_id=1, source_target_pairs={{0,1},{1,2},{2,3},{3,4},{4,5},{5,6},{6,7},{7,8},{8,9},{9,10},{10,1... | collective-permute-start | bytes 1013768 | tf_op jit(solution)/shard_map/ppermute | solution.py:23
  75.0 9.1 %collective-permute-start.1 = (f32[165,4,128]{2,1,0:T(4,128)S(1)}, f32[165,4,128]{2,1,0:T(4,128)S(1)}, u32[]{:S(2)}, u32[]{:S(2)}) collective-permute-start(f32[165,4,128]{2,1,0:T(4,128)S(1)} %get-tuple-element.9), channel_id=1, source_target_pairs={{1,0},{2,1},{3,2},{4,3},{5,4},{6,5},{7,6},{8,7},{9,8},{10,9},{11,1... | collective-permute-start | bytes 1013768 | tf_op jit(solution)/shard_map/ppermute | solution.py:24
  94.7 10.4 %all-to-all-start.2 = ((f32[8,3,1024]{2,1,0:T(4,128)}), f32[8,3,1024]{2,1,0:T(4,128)S(1)}, u32[]{:S(2)}, u32[]{:S(2)}) async-start(f32[8,3,1024]{2,1,0:T(4,128)} %broadcast_in_dim.41), calls=%async_computation.2 | async-start | bytes 262144 | tf_op jit(solution)/shard_map/all_to_all | solution.py:147
  110.1 29.3 %all-to-all-start.3 = ((f32[3,96,22]{2,0,1:T(4,128)}), f32[3,96,22]{2,0,1:T(4,128)S(1)}, u32[]{:S(2)}, u32[]{:S(2)}) async-start(f32[3,96,22]{2,0,1:T(4,128)} %copy.62), calls=%async_computation.3 | async-start | bytes 393216 | tf_op jit(solution)/shard_map/all_to_all | solution.py:158

commit v8 on v7

--- a/solution.py
+++ b/solution.py
@@ -123,9 +123,21 @@
     is_valid = asked_slots >= 0
     slot_index = jnp.where(is_valid, asked_slots, 0)
     surface = jnp.concatenate([ocean_currents, elevation[None]], 0)
-    answer = jnp.where(is_valid[None], surface[:, slot_index], 0.0)
+    asked_pick = (
+        asked_slots.reshape(-1)[:, None] == jnp.arange(ocean_cells, dtype=jnp.int32)[None, :]
+    ).astype(jnp.float32)
+    answer = lax.optimization_barrier(
+        jnp.dot(asked_pick, surface.T, precision=lax.Precision.HIGHEST)
+    ).T.reshape(
+        3, tile_count, capacity
+    )
     returned = lax.all_to_all(answer, "tile", split_axis=1, concat_axis=1, tiled=True)
-    at_cells = returned.reshape(3, tile_count * capacity)[:, position]
+    cell_pick = (position[:, None] == slot_ids[None, :]).astype(jnp.float32)
+    at_cells = lax.optimization_barrier(
+        jnp.dot(
+            cell_pick, returned.reshape(3, tile_count * capacity).T, precision=lax.Precision.HIGHEST
+        )
+    ).T
     sea_float = sea_mask.astype(jnp.float32)
     flow_fields = jnp.concatenate([at_cells[:2].reshape(2, row_count, columns), sea_float[None]], 0)
     extended = with_halo(jnp.concatenate([spectrum, flow_fields], 0), (("tile", 1),), STEPS)
@@ -160,14 +172,16 @@
     )
     flat_slots = asked_slots.reshape(-1)
     weight = is_valid.reshape(-1).astype(jnp.float32)
-    slot_pick = (flat_slots[:, None] == jnp.arange(ocean_cells, dtype=jnp.int32)[None, :]).astype(
+    slot_pick = (jnp.arange(ocean_cells, dtype=jnp.int32)[:, None] == flat_slots[None, :]).astype(
         jnp.float32
     )
-    summed = jnp.dot(
-        jnp.concatenate([arrived.reshape(3, -1) * weight[None], weight[None]], 0),
-        slot_pick,
-        precision=lax.Precision.HIGHEST,
-    )
+    summed = lax.optimization_barrier(
+        jnp.dot(
+            slot_pick,
+            jnp.concatenate([arrived.reshape(3, -1) * weight[None], weight[None]], 0).T,
+            precision=lax.Precision.HIGHEST,
+        )
+    ).T
     return (energy, summed[:3] / jnp.maximum(summed[3], 1.0)[None])
 
 

time: 147 us -> 151 us (1.027)
  matrix products: 5.96 us -> 19.5 us
  local copies, waits for them, and re-layouts: 18.5 us -> 9.77 us
  waiting for transfers between devices: 53.8 us -> 57.6 us
  starting transfers between devices: 50.6 us -> 47.1 us
    dot_general x1 -> x3, matrix products: 5.51 us -> 19.1 us  [the longest x1 8.46 us: local(): jnp.dot(asked_pick, surface.T, precision=lax.Precision.HIGHEST)]
    gather x4 -> x0, local copies, waits for them, and re-layouts: 7.32 us -> none  [the longest x3 4.51 us: local(): answer = jnp.where(is_valid[None], surface[:, slot_index], 0.0)]
    all_to_all x1, starting transfers between devices: 12.2 us -> 8.82 us  [local(): lax.all_to_all(packed.reshape(3, tile_count, capacity), 'tile', split_axi...]
  transfers between devices with their start and end apart: 6 -> 6, of which waited for: 6 -> 6; matrix products, arithmetic and copies ran while one was open for 3% -> 1% of each run, Pallas kernels for 0% -> 0%
where the time goes in v8:
time: 151 us; the launch traced here: 150 us
  waiting for transfers between devices  57.6 us (38%)
  starting transfers between devices  47.1 us (31%)
  matrix products  19.5 us (13%)
  local copies, waits for them, and re-layouts  9.77 us (6%)
  other arithmetic  8.09 us (5%)
  Pallas kernels  6.89 us (5%)
    all_to_all x1, starting transfers between devices, local(): lax.all_to_all(requests.reshape(tile_count, capacity), 'tile', split_axis...  21.8 us
    all_to_all x1, waiting for transfers between devices, local(): lax.all_to_all(packed.reshape(3, tile_count, capacity), 'tile', split_axi...  16.8 us
    all_to_all x1, waiting for transfers between devices, local(): lax.all_to_all(answer, 'tile', split_axis=1, concat_axis=1, tiled=True)  16.1 us
    all_to_all x1, waiting for transfers between devices, local(): lax.all_to_all(requests.reshape(tile_count, capacity), 'tile', split_axis...  12.9 us
    all_to_all x1, starting transfers between devices, local(): lax.all_to_all(packed.reshape(3, tile_count, capacity), 'tile', split_axi...  8.82 us
    dot_general x1, matrix products, local(): jnp.dot(asked_pick, surface.T, precision=lax.Precision.HIGHEST)  8.46 us
    dot_general x1, matrix products, local(): jnp.dot(slot_pick, jnp.concatenate([arrived.reshape(3, -1) * weight[None]...  7.91 us
    pallas_call x1, Pallas kernels, propagate(): pl.pallas_call(kernel, grid=(bins // block,), in_specs=[pl.BlockSpec(memo...  6.89 us
  transfers between devices with their start and end apart: 6, of which 6 were waited for; matrix products, arithmetic and copies ran while one was open for 1% of the time, Pallas kernels for 0%

profile of v8, /device:TPU:8, one launch (start us, length us, event | category | flops | bytes accessed | tf_op | source)
XLA Modules:
  0.0 149.8 jit_solution(15451184012099579653)
XLA Ops:
  0.6 0.7 broadcast_add_fusion.1
  1.3 1.3 convert_reduce_fusion
  2.6 0.7 compare_select_fusion
  3.3 1.0 select_reduce_fusion
  4.3 0.8 sub.20
  5.0 21.8 %all-to-all-start = ((s32[96,1,22]{2,1,0:T(1,128)}), s32[96,1,22]{2,1,0:T(1,128)S(1)}, u32[]{:S(2)}, u32[]{:S(2)}) async-start(s32[96,1,22]{2,1,0:T(1,128)} %bitcast.4), calls=%async_computation | async-start | bytes 98304 | tf_op jit(solution)/shard_map/all_to_all | solution.py:120
  26.8 0.7 fusion.32
  27.5 12.9 %all-to-all-done = s32[96,1,22]{2,1,0:T(1,128)S(1)} async-done(((s32[96,1,22]{2,1,0:T(1,128)}), s32[96,1,22]{2,1,0:T(1,128)S(1)}, u32[]{:S(2)}, u32[]{:S(2)}) %all-to-all-start) | async-done | bytes 8480 | tf_op jit(solution)/shard_map/all_to_all | solution.py:120
  40.4 0.5 broadcast.339
  40.9 0.8 reduce.7
  41.8 8.5 %fusion.1 = f32[2112,3]{0,1:T(4,128)S(1)} fusion(s32[2112]{0:T(1024)S(1)} %eq.91, f32[1,2048]{1,0:T(1,128)} %bitcast.49, f32[2,2048]{1,0:T(2,128)} %param.11), kind=kOutput, calls=%fused_computation.4 | convolution fusion | flops 160045056 | bytes 58368 | tf_op jit(solution)/shard_map/dot_general | solution.py:130
  50.5 0.8 copy.21
  51.3 6.4 %all-to-all-start.1 = ((f32[3,96,22]{2,0,1:T(4,128)}), f32[3,96,22]{2,0,1:T(4,128)S(1)}, u32[]{:S(2)}, u32[]{:S(2)}) async-start(f32[3,96,22]{2,0,1:T(4,128)} %copy.21), calls=%async_computation.1 | async-start | bytes 393216 | tf_op jit(solution)/shard_map/all_to_all | solution.py:134
  57.7 16.1 %all-to-all-done.1 = f32[3,96,22]{2,0,1:T(4,128)S(1)} async-done(((f32[3,96,22]{2,0,1:T(4,128)}), f32[3,96,22]{2,0,1:T(4,128)S(1)}, u32[]{:S(2)}, u32[]{:S(2)}) %all-to-all-start.1) | async-done | bytes 25376 | tf_op jit(solution)/shard_map/all_to_all | solution.py:134
  74.0 2.7 %fusion.4 = f32[1024,3]{0,1:T(4,128)S(1)} fusion(f32[3,2112]{1,0:T(4,128)S(1)} %reshape.195, s32[1024]{0:T(1024)S(1)} %bitcast.47), kind=kOutput, calls=%fused_computation.9 | convolution fusion | flops 80019456 | bytes 41728 | tf_op jit(solution)/shard_map/dot_general | solution.py:137
  77.0 3.1 %collective-permute-start.1 = (f32[165,4,128]{2,1,0:T(4,128)S(1)}, f32[165,4,128]{2,1,0:T(4,128)S(1)}, u32[]{:S(2)}, u32[]{:S(2)}) collective-permute-start(f32[165,4,128]{2,1,0:T(4,128)S(1)} %get-tuple-element.7), channel_id=1, source_target_pairs={{1,0},{2,1},{3,2},{4,3},{5,4},{6,5},{7,6},{8,7},{9,8},{10,9},{11,1... | collective-permute-start | bytes 1013768 | tf_op jit(solution)/shard_map/ppermute | solution.py:24
  80.1 2.7 %collective-permute-start = (f32[165,4,128]{2,1,0:T(4,128)S(1)}, f32[165,4,128]{2,1,0:T(4,128)S(1)}, u32[]{:S(2)}, u32[]{:S(2)}) collective-permute-start(f32[165,4,128]{2,1,0:T(4,128)S(1)} %get-tuple-element.6), channel_id=1, source_target_pairs={{0,1},{1,2},{2,3},{3,4},{4,5},{5,6},{6,7},{7,8},{8,9},{9,10},{10,1... | collective-permute-start | bytes 1013768 | tf_op jit(solution)/shard_map/ppermute | solution.py:23
  82.9 0.6 pad_maximum_fusion.2.speed_ref
  83.5 2.5 %collective-permute-done.1 = f32[165,4,128]{2,1,0:T(4,128)S(1)} collective-permute-done((f32[165,4,128]{2,1,0:T(4,128)S(1)}, f32[165,4,128]{2,1,0:T(4,128)S(1)}, u32[]{:S(2)}, u32[]{:S(2)}) %collective-permute-start.1) | collective-permute-done | bytes 337952 | tf_op jit(solution)/shard_map/ppermute | solution.py:24
  86.0 3.1 %collective-permute-done = f32[165,4,128]{2,1,0:T(4,128)S(1)} collective-permute-done((f32[165,4,128]{2,1,0:T(4,128)S(1)}, f32[165,4,128]{2,1,0:T(4,128)S(1)}, u32[]{:S(2)}, u32[]{:S(2)}) %collective-permute-start) | collective-permute-done | bytes 337952 | tf_op jit(solution)/shard_map/ppermute | solution.py:23
  89.2 1.3 pad_maximum_fusion.energy_ref.flow_ref
  90.5 6.9 %shard_map.95 = f32[162,8,128]{2,1,0:T(8,128)} custom-call(f32[2,162]{1,0:T(2,128)} %pad_maximum_fusion.2.speed_ref, f32[165,16,128]{2,1,0:T(8,128)} %pad_maximum_fusion.energy_ref.flow_ref, f32[165,16,128]{2,1,0:T(8,128)} %pad_maximum_fusion.energy_ref.flow_ref), custom_call_target="tpu_custom_call" | custom-call | tf_op jit(solution)/shard_map/pallas_call | solution.py:78
  97.4 1.1 pad.17
  99.1 0.7 broadcast_in_dim.25
  99.8 4.3 %all-to-all-start.2 = ((f32[8,3,1024]{2,1,0:T(4,128)}), f32[8,3,1024]{2,1,0:T(4,128)S(1)}, u32[]{:S(2)}, u32[]{:S(2)}) async-start(f32[8,3,1024]{2,1,0:T(4,128)} %broadcast_in_dim.25), calls=%async_computation.2 | async-start | bytes 262144 | tf_op jit(solution)/shard_map/all_to_all | solution.py:159
  104.1 6.1 %all-to-all-done.2 = f32[8,3,1024]{2,1,0:T(4,128)S(1)} async-done(((f32[8,3,1024]{2,1,0:T(4,128)}), f32[8,3,1024]{2,1,0:T(4,128)S(1)}, u32[]{:S(2)}, u32[]{:S(2)}) %all-to-all-start.2) | async-done | bytes 98336 | tf_op jit(solution)/shard_map/all_to_all | solution.py:159
  110.4 3.4 %scatter_custom_fusion = f32[3,2112]{0,1:T(8,128)S(1)} fusion(s32[1024]{0:T(1024)S(1)} %bitcast.45, f32[1024,3]{1,0:T(8,128)S(1)} %copy.23, f32[]{:T(128)} %constant.23.clone.1), kind=kCustom, calls=%fused_computation.17 | custom fusion | bytes 25348 | tf_op jit(solution)/shard_map/scatter | solution.py:169
  114.4 0.8 copy.25
  115.1 8.8 %all-to-all-start.3 = ((f32[3,96,22]{2,0,1:T(4,128)}), f32[3,96,22]{2,0,1:T(4,128)S(1)}, u32[]{:S(2)}, u32[]{:S(2)}) async-start(f32[3,96,22]{2,0,1:T(4,128)} %copy.25), calls=%async_computation.3 | async-start | bytes 393216 | tf_op jit(solution)/shard_map/all_to_all | solution.py:170
  124.3 16.8 %all-to-all-done.3 = f32[3,96,22]{2,0,1:T(4,128)S(1)} async-done(((f32[3,96,22]{2,0,1:T(4,128)}), f32[3,96,22]{2,0,1:T(4,128)S(1)}, u32[]{:S(2)}, u32[]{:S(2)}) %all-to-all-start.3) | async-done | bytes 25376 | tf_op jit(solution)/shard_map/all_to_all | solution.py:170
  141.3 7.9 %fusion = f32[2048,4]{0,1:T(4,128)S(1)} fusion(s32[2112]{0:T(1024)S(1)} %eq.91, f32[1,2112]{1,0:T(1,128)S(1)} %reshape.202, f32[3,2112]{1,0:T(4,128)S(1)} %broadcast_multiply_fusion), kind=kOutput, calls=%fused_computation.2 | convolution fusion | flops 211951872 | bytes 75008 | tf_op jit(solution)/shard_map/dot_general | solution.py:179
  149.2 0.6 slice_divide_fusion
  (32 shorter events, 2.7 us)
Async XLA Ops:
  5.0 35.4 %all-to-all-start = ((s32[96,1,22]{2,1,0:T(1,128)}), s32[96,1,22]{2,1,0:T(1,128)S(1)}, u32[]{:S(2)}, u32[]{:S(2)}) async-start(s32[96,1,22]{2,1,0:T(1,128)} %bitcast.4), calls=%async_computation | async-start | bytes 98304 | tf_op jit(solution)/shard_map/all_to_all | solution.py:120
  41.8 15.8 %copy-start.1 = (f32[36]{0:T(128)S(1)}, f32[36]{0:T(128)}, u32[]{:S(2)}) copy-start(f32[36]{0:T(128)} %param.10) | copy-start | bytes 436
  41.8 15.8 %copy-start.2 = (f32[36]{0:T(128)S(1)}, f32[36]{0:T(128)}, u32[]{:S(2)}) copy-start(f32[36]{0:T(128)} %param.9) | copy-start | bytes 436
  51.3 22.6 %all-to-all-start.1 = ((f32[3,96,22]{2,0,1:T(4,128)}), f32[3,96,22]{2,0,1:T(4,128)S(1)}, u32[]{:S(2)}, u32[]{:S(2)}) async-start(f32[3,96,22]{2,0,1:T(4,128)} %copy.21), calls=%async_computation.1 | async-start | bytes 393216 | tf_op jit(solution)/shard_map/all_to_all | solution.py:134
  74.0 2.7 %copy-start = (f32[162,8,128]{2,1,0:T(8,128)S(1)}, f32[162,8,128]{2,1,0:T(8,128)}, u32[]{:S(2)}) copy-start(f32[162,8,128]{2,1,0:T(8,128)} %param.8) | copy-start | bytes 1990660
  77.0 9.1 %collective-permute-start.1 = (f32[165,4,128]{2,1,0:T(4,128)S(1)}, f32[165,4,128]{2,1,0:T(4,128)S(1)}, u32[]{:S(2)}, u32[]{:S(2)}) collective-permute-start(f32[165,4,128]{2,1,0:T(4,128)S(1)} %get-tuple-element.7), channel_id=1, source_target_pairs={{1,0},{2,1},{3,2},{4,3},{5,4},{6,5},{7,6},{8,7},{9,8},{10,9},{11,1... | collective-permute-start | bytes 1013768 | tf_op jit(solution)/shard_map/ppermute | solution.py:24
  80.1 9.1 %collective-permute-start = (f32[165,4,128]{2,1,0:T(4,128)S(1)}, f32[165,4,128]{2,1,0:T(4,128)S(1)}, u32[]{:S(2)}, u32[]{:S(2)}) collective-permute-start(f32[165,4,128]{2,1,0:T(4,128)S(1)} %get-tuple-element.6), channel_id=1, source_target_pairs={{0,1},{1,2},{2,3},{3,4},{4,5},{5,6},{6,7},{7,8},{8,9},{9,10},{10,1... | collective-permute-start | bytes 1013768 | tf_op jit(solution)/shard_map/ppermute | solution.py:23
  99.8 10.4 %all-to-all-start.2 = ((f32[8,3,1024]{2,1,0:T(4,128)}), f32[8,3,1024]{2,1,0:T(4,128)S(1)}, u32[]{:S(2)}, u32[]{:S(2)}) async-start(f32[8,3,1024]{2,1,0:T(4,128)} %broadcast_in_dim.25), calls=%async_computation.2 | async-start | bytes 262144 | tf_op jit(solution)/shard_map/all_to_all | solution.py:159
  115.1 25.9 %all-to-all-start.3 = ((f32[3,96,22]{2,0,1:T(4,128)}), f32[3,96,22]{2,0,1:T(4,128)S(1)}, u32[]{:S(2)}, u32[]{:S(2)}) async-start(f32[3,96,22]{2,0,1:T(4,128)} %copy.25), calls=%async_computation.3 | async-start | bytes 393216 | tf_op jit(solution)/shard_map/all_to_all | solution.py:170

commit v9 on v7

--- a/solution.py
+++ b/solution.py
@@ -41,13 +41,19 @@
     return flow_fields[2, 1:-1] * (middle - div_x - div_y)
 
 
-def propagate_kernel(speed_ref, energy_ref, flow_ref, out_ref, *, block, steps, rows_out):
+def propagate_kernel(
+    speed_ref, weight_ref, energy_ref, flow_ref, out_ref, stress_ref, *, block, steps, rows_out
+):
     rows = energy_ref.shape[1]
     lanes = energy_ref.shape[2]
     base = pl.program_id(0) * block
     u = flow_ref[0]
     v = flow_ref[1]
     m = flow_ref[2]
+
+    @pl.when(pl.program_id(0) == 0)
+    def _():
+        stress_ref[...] = jnp.zeros(stress_ref.shape, jnp.float32)
 
     def one_bin(b, carry):
         vel_x = speed_ref[0, base + b] + u
@@ -65,13 +71,17 @@
             flux_y = pos_y * energy + neg_y * pltpu.roll(energy, rows - 1, 0)
             div_y = flux_y - pltpu.roll(flux_y, 1, 0)
             energy = m * (energy - div_x - div_y)
-        out_ref[b] = pltpu.roll(energy, rows - steps, 0)[:rows_out]
-        return carry
-
-    lax.fori_loop(0, block, one_bin, 0, unroll=True)
-
-
-def propagate(speeds, extended, bins, rows_out):
+        kept = pltpu.roll(energy, rows - steps, 0)[:rows_out]
+        out_ref[b] = kept
+        return tuple(carry[k] + weight_ref[k, base + b] * kept for k in range(3))
+
+    zero = jnp.zeros((rows_out, lanes), jnp.float32)
+    sums = lax.fori_loop(0, block, one_bin, (zero, zero, zero), unroll=True)
+    for k in range(3):
+        stress_ref[k] = stress_ref[k] + sums[k]
+
+
+def propagate(speeds, weights, extended, bins, rows_out):
     rows, lanes = extended.shape[1:]
     block = max(d for d in range(1, 33) if bins % d == 0)
     kernel = functools.partial(propagate_kernel, block=block, steps=STEPS, rows_out=rows_out)
@@ -80,13 +90,19 @@
         grid=(bins // block,),
         in_specs=[
             pl.BlockSpec(memory_space=pltpu.MemorySpace.SMEM),
+            pl.BlockSpec(memory_space=pltpu.MemorySpace.SMEM),
             pl.BlockSpec((block, rows, lanes), lambda i: (i, 0, 0)),
             pl.BlockSpec((3, rows, lanes), lambda i: (bins // 3, 0, 0)),
         ],
-        out_specs=pl.BlockSpec((block, rows_out, lanes), lambda i: (i, 0, 0)),
-        out_shape=jax.ShapeDtypeStruct((bins, rows_out, lanes), jnp.float32),
-    )(speeds, extended, extended)
-
+        out_specs=[
+            pl.BlockSpec((block, rows_out, lanes), lambda i: (i, 0, 0)),
+            pl.BlockSpec((3, rows_out, lanes), lambda i: (0, 0, 0)),
+        ],
+        out_shape=[
+            jax.ShapeDtypeStruct((bins, rows_out, lanes), jnp.float32),
+            jax.ShapeDtypeStruct((3, rows_out, lanes), jnp.float32),
+        ],
+    )(speeds, weights, extended, extended)
 
 def local(
     spectrum, courant, group_ratio, ocean_currents, elevation, sea_mask, owner_tile, ocean_slot
@@ -130,7 +146,6 @@
     flow_fields = jnp.concatenate([at_cells[:2].reshape(2, row_count, columns), sea_float[None]], 0)
     extended = with_halo(jnp.concatenate([spectrum, flow_fields], 0), (("tile", 1),), STEPS)
     speeds = jnp.stack([group_speed * cos_dir, group_speed * sin_dir], 0)
-    energy = propagate(speeds, extended, bin_count, row_count)
     weights = jnp.stack(
         [
             ratio_bin * (1.0 + cos_dir * cos_dir) - 0.5,
@@ -139,9 +154,8 @@
         ],
         0,
     ) * (4.0 / (NDIR * NFREQ))
-    partial_value = jnp.dot(
-        weights, energy.reshape(bin_count, cell_count), precision=lax.Precision.HIGHEST
-    )
+    energy, partial_value = propagate(speeds, weights, extended, bin_count, row_count)
+    partial_value = partial_value.reshape(3, cell_count)
     partial_value = partial_value * ((1.0 + at_cells[2]) * sea_float.reshape(-1))
     sect_count = lax.axis_size("sect")
     every_part = lax.all_to_all(

time: 147 us -> 145 us (0.986)
  other arithmetic: 9.1 us -> 11.1 us
  transfers between devices with their start and end apart: 6 -> 6, of which waited for: 6 -> 6; matrix products, arithmetic and copies ran while one was open for 3% -> 4% of each run, Pallas kernels for 0% -> 0%
where the time goes in v9:
time: 145 us; the launch traced here: 144 us
  waiting for transfers between devices  52.5 us (36%)
  starting transfers between devices  50.3 us (35%)
  local copies, waits for them, and re-layouts  17.2 us (12%)
  other arithmetic  11.1 us (8%)
  Pallas kernels  6.9 us (5%)
  matrix products  5.51 us (4%)
    all_to_all x1, starting transfers between devices, local(): lax.all_to_all(requests.reshape(tile_count, capacity), 'tile', split_axis...  21.8 us
    all_to_all x1, waiting for transfers between devices, local(): lax.all_to_all(packed.reshape(3, tile_count, capacity), 'tile', split_axi...  16.9 us
    all_to_all x1, waiting for transfers between devices, local(): lax.all_to_all(answer, 'tile', split_axis=1, concat_axis=1, tiled=True)  15.9 us
    all_to_all x1, starting transfers between devices, local(): lax.all_to_all(packed.reshape(3, tile_count, capacity), 'tile', split_axi...  12 us
    all_to_all x1, waiting for transfers between devices, local(): lax.all_to_all(requests.reshape(tile_count, capacity), 'tile', split_axis...  11 us
    pallas_call x1, Pallas kernels, propagate(): pl.pallas_call(kernel, grid=(bins // block,), in_specs=[pl.BlockSpec(memo...  6.9 us
    all_to_all x1, starting transfers between devices, local(): lax.all_to_all(answer, 'tile', split_axis=1, concat_axis=1, tiled=True)  6.35 us
    dot_general x1, matrix products, local(): jnp.dot(jnp.concatenate([arrived.reshape(3, -1) * weight[None], weight[No...  5.51 us
  transfers between devices with their start and end apart: 6, of which 6 were waited for; matrix products, arithmetic and copies ran while one was open for 4% of the time, Pallas kernels for 0%

profile of v9, /device:TPU:8, one launch (start us, length us, event | category | flops | bytes accessed | tf_op | source)
XLA Modules:
  0.0 144.4 jit_solution(14164105996447002426)
XLA Ops:
  0.6 1.3 convert_reduce_fusion
  1.9 0.7 compare_select_fusion.2
  2.6 0.7 broadcast_add_fusion.1
  3.3 1.0 select_reduce_fusion
  4.3 0.8 sub.22
  5.0 21.8 %all-to-all-start = ((s32[96,1,22]{2,1,0:T(1,128)}), s32[96,1,22]{2,1,0:T(1,128)S(1)}, u32[]{:S(2)}, u32[]{:S(2)}) async-start(s32[96,1,22]{2,1,0:T(1,128)} %bitcast.5), calls=%async_computation | async-start | bytes 98304 | tf_op jit(solution)/shard_map/all_to_all | solution.py:136
  26.8 0.7 fusion.18
  27.5 0.8 pad_maximum_fusion.2
  28.3 0.8 select_reduce_fusion.1
  29.4 11.0 %all-to-all-done = s32[96,1,22]{2,1,0:T(1,128)S(1)} async-done(((s32[96,1,22]{2,1,0:T(1,128)}), s32[96,1,22]{2,1,0:T(1,128)S(1)}, u32[]{:S(2)}, u32[]{:S(2)}) %all-to-all-start) | async-done | bytes 8480 | tf_op jit(solution)/shard_map/all_to_all | solution.py:136
  40.8 4.0 %gather_fusion = f32[2112,3]{1,0:T(8,128)S(1)} fusion(f32[3,2048]{0,1:T(8,128)S(1)} %copy.53, s32[3072]{0:T(1024)S(1)} %pad_clamp_fusion), kind=kCustom, calls=%fused_computation | custom fusion | bytes 59136 | tf_op jit(solution)/shard_map/gather | solution.py:142
  45.3 0.8 copy.55
  46.1 6.3 %all-to-all-start.1 = ((f32[3,96,22]{2,0,1:T(4,128)}), f32[3,96,22]{2,0,1:T(4,128)S(1)}, u32[]{:S(2)}, u32[]{:S(2)}) async-start(f32[3,96,22]{2,0,1:T(4,128)} %copy.55), calls=%async_computation.1 | async-start | bytes 393216 | tf_op jit(solution)/shard_map/all_to_all | solution.py:143
  52.8 15.9 %all-to-all-done.1 = f32[3,96,22]{2,0,1:T(4,128)S(1)} async-done(((f32[3,96,22]{2,0,1:T(4,128)}), f32[3,96,22]{2,0,1:T(4,128)S(1)}, u32[]{:S(2)}, u32[]{:S(2)}) %all-to-all-start.1) | async-done | bytes 25376 | tf_op jit(solution)/shard_map/all_to_all | solution.py:143
  69.3 2.8 %gather_fusion.1 = f32[1024,3]{1,0:T(8,128)S(1)} fusion(f32[3,2112]{0,1:T(8,128)S(1)} %copy.57, s32[1024]{0:T(1024)S(1)} %broadcast_clamp_fusion), kind=kCustom, calls=%fused_computation.1 | custom fusion | bytes 28672 | tf_op jit(solution)/shard_map/gather | solution.py:144
  72.4 2.4 %collective-permute-start = (f32[165,4,128]{2,1,0:T(4,128)S(1)}, f32[165,4,128]{2,1,0:T(4,128)S(1)}, u32[]{:S(2)}, u32[]{:S(2)}) collective-permute-start(f32[165,4,128]{2,1,0:T(4,128)S(1)} %get-tuple-element.12), channel_id=1, source_target_pairs={{0,1},{1,2},{2,3},{3,4},{4,5},{5,6},{6,7},{7,8},{8,9},{9,10},{10,1... | collective-permute-start | bytes 1013768 | tf_op jit(solution)/shard_map/ppermute | solution.py:23
  74.9 3.4 %collective-permute-start.1 = (f32[165,4,128]{2,1,0:T(4,128)S(1)}, f32[165,4,128]{2,1,0:T(4,128)S(1)}, u32[]{:S(2)}, u32[]{:S(2)}) collective-permute-start(f32[165,4,128]{2,1,0:T(4,128)S(1)} %get-tuple-element.13), channel_id=1, source_target_pairs={{1,0},{2,1},{3,2},{4,3},{5,4},{6,5},{7,6},{8,7},{9,8},{10,9},{11,1... | collective-permute-start | bytes 1013768 | tf_op jit(solution)/shard_map/ppermute | solution.py:24
  79.9 1.6 %collective-permute-done = f32[165,4,128]{2,1,0:T(4,128)S(1)} collective-permute-done((f32[165,4,128]{2,1,0:T(4,128)S(1)}, f32[165,4,128]{2,1,0:T(4,128)S(1)}, u32[]{:S(2)}, u32[]{:S(2)}) %collective-permute-start) | collective-permute-done | bytes 337952 | tf_op jit(solution)/shard_map/ppermute | solution.py:23
  81.5 2.4 %collective-permute-done.1 = f32[165,4,128]{2,1,0:T(4,128)S(1)} collective-permute-done((f32[165,4,128]{2,1,0:T(4,128)S(1)}, f32[165,4,128]{2,1,0:T(4,128)S(1)}, u32[]{:S(2)}, u32[]{:S(2)}) %collective-permute-start.1) | collective-permute-done | bytes 337952 | tf_op jit(solution)/shard_map/ppermute | solution.py:24
  83.9 1.3 pad_maximum_fusion.energy_ref.flow_ref
  85.3 6.9 %shard_map.95 = (f32[162,8,128]{2,1,0:T(8,128)}, f32[3,8,128]{2,1,0:T(8,128)}) custom-call(f32[2,162]{1,0:T(2,128)} %pad_maximum_fusion.3.speed_ref, f32[3,162]{1,0:T(4,128)} %maximum_multiply_fusion.weight_ref, f32[165,16,128]{2,1,0:T(8,128)} %pad_maximum_fusion.energy_ref.flow_ref, f32[165,16,128]{2,1,0:T(8,128)} %pad_maximum_fusion.energy_ref.flow_ref), custom_call_target="tpu_custom_call" | custom-call | tf_op jit(solution)/shard_map/pallas_call | solution.py:88
  92.2 0.7 bitcast_multiply_fusion
  92.9 0.7 broadcast_in_dim.41
  93.5 4.3 %all-to-all-start.2 = ((f32[8,3,1024]{2,1,0:T(4,128)}), f32[8,3,1024]{2,1,0:T(4,128)S(1)}, u32[]{:S(2)}, u32[]{:S(2)}) async-start(f32[8,3,1024]{2,1,0:T(4,128)} %broadcast_in_dim.41), calls=%async_computation.2 | async-start | bytes 262144 | tf_op jit(solution)/shard_map/all_to_all | solution.py:161
  98.3 0.8 reduce.5
  99.2 4.7 %all-to-all-done.2 = f32[8,3,1024]{2,1,0:T(4,128)S(1)} async-done(((f32[8,3,1024]{2,1,0:T(4,128)}), f32[8,3,1024]{2,1,0:T(4,128)S(1)}, u32[]{:S(2)}, u32[]{:S(2)}) %all-to-all-start.2) | async-done | bytes 98336 | tf_op jit(solution)/shard_map/all_to_all | solution.py:161
  104.2 3.4 %scatter_custom_fusion = f32[3,2112]{0,1:T(8,128)S(1)} fusion(s32[1024]{0:T(1024)S(1)} %bitcast.38, f32[1024,3]{1,0:T(8,128)S(1)} %copy.60, f32[]{:T(128)} %constant.21.clone.1), kind=kCustom, calls=%fused_computation.13 | custom fusion | bytes 25348 | tf_op jit(solution)/shard_map/scatter | solution.py:171
  108.1 0.8 copy.62
  108.9 12.0 %all-to-all-start.3 = ((f32[3,96,22]{2,0,1:T(4,128)}), f32[3,96,22]{2,0,1:T(4,128)S(1)}, u32[]{:S(2)}, u32[]{:S(2)}) async-start(f32[3,96,22]{2,0,1:T(4,128)} %copy.62), calls=%async_computation.3 | async-start | bytes 393216 | tf_op jit(solution)/shard_map/all_to_all | solution.py:172
  121.2 16.9 %all-to-all-done.3 = f32[3,96,22]{2,0,1:T(4,128)S(1)} async-done(((f32[3,96,22]{2,0,1:T(4,128)}), f32[3,96,22]{2,0,1:T(4,128)S(1)}, u32[]{:S(2)}, u32[]{:S(2)}) %all-to-all-start.3) | async-done | bytes 25376 | tf_op jit(solution)/shard_map/all_to_all | solution.py:172
  138.3 5.5 %fusion = f32[4,2048]{1,0:T(4,128)S(1)} fusion(s32[2112]{0:T(1024)S(1)} %all_to_all.22, f32[1,2112]{1,0:T(1,128)S(1)} %reshape.251, f32[3,2112]{1,0:T(4,128)S(1)} %broadcast_multiply_fusion), kind=kOutput, calls=%fused_computation.4 | convolution fusion | flops 211951872 | bytes 75008 | tf_op jit(solution)/shard_map/dot_general | solution.py:180
  143.8 0.6 slice_divide_fusion
  (39 shorter events, 5.9 us)
Async XLA Ops:
  5.0 35.4 %all-to-all-start = ((s32[96,1,22]{2,1,0:T(1,128)}), s32[96,1,22]{2,1,0:T(1,128)S(1)}, u32[]{:S(2)}, u32[]{:S(2)}) async-start(s32[96,1,22]{2,1,0:T(1,128)} %bitcast.5), calls=%async_computation | async-start | bytes 98304 | tf_op jit(solution)/shard_map/all_to_all | solution.py:136
  46.1 22.6 %all-to-all-start.1 = ((f32[3,96,22]{2,0,1:T(4,128)}), f32[3,96,22]{2,0,1:T(4,128)S(1)}, u32[]{:S(2)}, u32[]{:S(2)}) async-start(f32[3,96,22]{2,0,1:T(4,128)} %copy.55), calls=%async_computation.1 | async-start | bytes 393216 | tf_op jit(solution)/shard_map/all_to_all | solution.py:143
  52.5 19.7 %copy-start = (f32[162,8,128]{2,1,0:T(8,128)S(1)}, f32[162,8,128]{2,1,0:T(8,128)}, u32[]{:S(2)}) copy-start(f32[162,8,128]{2,1,0:T(8,128)} %param.8) | copy-start | bytes 1990660
  72.4 9.1 %collective-permute-start = (f32[165,4,128]{2,1,0:T(4,128)S(1)}, f32[165,4,128]{2,1,0:T(4,128)S(1)}, u32[]{:S(2)}, u32[]{:S(2)}) collective-permute-start(f32[165,4,128]{2,1,0:T(4,128)S(1)} %get-tuple-element.12), channel_id=1, source_target_pairs={{0,1},{1,2},{2,3},{3,4},{4,5},{5,6},{6,7},{7,8},{8,9},{9,10},{10,1... | collective-permute-start | bytes 1013768 | tf_op jit(solution)/shard_map/ppermute | solution.py:23
  74.9 9.1 %collective-permute-start.1 = (f32[165,4,128]{2,1,0:T(4,128)S(1)}, f32[165,4,128]{2,1,0:T(4,128)S(1)}, u32[]{:S(2)}, u32[]{:S(2)}) collective-permute-start(f32[165,4,128]{2,1,0:T(4,128)S(1)} %get-tuple-element.13), channel_id=1, source_target_pairs={{1,0},{2,1},{3,2},{4,3},{5,4},{6,5},{7,6},{8,7},{9,8},{10,9},{11,1... | collective-permute-start | bytes 1013768 | tf_op jit(solution)/shard_map/ppermute | solution.py:24
  93.5 10.4 %all-to-all-start.2 = ((f32[8,3,1024]{2,1,0:T(4,128)}), f32[8,3,1024]{2,1,0:T(4,128)S(1)}, u32[]{:S(2)}, u32[]{:S(2)}) async-start(f32[8,3,1024]{2,1,0:T(4,128)} %broadcast_in_dim.41), calls=%async_computation.2 | async-start | bytes 262144 | tf_op jit(solution)/shard_map/all_to_all | solution.py:161
  108.9 29.2 %all-to-all-start.3 = ((f32[3,96,22]{2,0,1:T(4,128)}), f32[3,96,22]{2,0,1:T(4,128)S(1)}, u32[]{:S(2)}, u32[]{:S(2)}) async-start(f32[3,96,22]{2,0,1:T(4,128)} %copy.62), calls=%async_computation.3 | async-start | bytes 393216 | tf_op jit(solution)/shard_map/all_to_all | solution.py:172

commit v10 on v9

--- a/solution.py
+++ b/solution.py
@@ -104,6 +104,20 @@
         ],
     )(speeds, weights, extended, extended)
 
+def pick_matmul(values, pick):
+    parts = []
+    rest = values
+    for _ in range(2):
+        head = lax.reduce_precision(rest, exponent_bits=8, mantissa_bits=7)
+        parts.append(head)
+        rest = rest - head
+    parts.append(rest)
+    rows = values.shape[0]
+    stacked = jnp.concatenate(parts, 0).astype(jnp.bfloat16)
+    product = jnp.dot(stacked, pick, preferred_element_type=jnp.float32)
+    return (product[:rows] + product[rows : 2 * rows]) + product[2 * rows :]
+
+
 def local(
     spectrum, courant, group_ratio, ocean_currents, elevation, sea_mask, owner_tile, ocean_slot
 ):
@@ -139,9 +153,12 @@
     is_valid = asked_slots >= 0
     slot_index = jnp.where(is_valid, asked_slots, 0)
     surface = jnp.concatenate([ocean_currents, elevation[None]], 0)
-    answer = jnp.where(is_valid[None], surface[:, slot_index], 0.0)
+    ocean_ids = jnp.arange(ocean_cells, dtype=jnp.int32)
+    slot_pick = (ocean_ids[:, None] == asked_slots.reshape(-1)[None, :]).astype(jnp.bfloat16)
+    answer = pick_matmul(surface, slot_pick).reshape(3, tile_count, capacity)
     returned = lax.all_to_all(answer, "tile", split_axis=1, concat_axis=1, tiled=True)
-    at_cells = returned.reshape(3, tile_count * capacity)[:, position]
+    cell_pick = (slot_ids[:, None] == position[None, :]).astype(jnp.bfloat16)
+    at_cells = pick_matmul(returned.reshape(3, tile_count * capacity), cell_pick)
     sea_float = sea_mask.astype(jnp.float32)
     flow_fields = jnp.concatenate([at_cells[:2].reshape(2, row_count, columns), sea_float[None]], 0)
     extended = with_halo(jnp.concatenate([spectrum, flow_fields], 0), (("tile", 1),), STEPS)
@@ -174,13 +191,8 @@
     )
     flat_slots = asked_slots.reshape(-1)
     weight = is_valid.reshape(-1).astype(jnp.float32)
-    slot_pick = (flat_slots[:, None] == jnp.arange(ocean_cells, dtype=jnp.int32)[None, :]).astype(
-        jnp.float32
-    )
-    summed = jnp.dot(
-        jnp.concatenate([arrived.reshape(3, -1) * weight[None], weight[None]], 0),
-        slot_pick,
-        precision=lax.Precision.HIGHEST,
+    summed = pick_matmul(
+        jnp.concatenate([arrived.reshape(3, -1) * weight[None], weight[None]], 0), slot_pick.T
     )
     return (energy, summed[:3] / jnp.maximum(summed[3], 1.0)[None])
 

time: 145 us -> 139 us (0.959)
  local copies, waits for them, and re-layouts: 17.2 us -> 8.49 us
  starting transfers between devices: 50.3 us -> 47.3 us
  matrix products: 5.51 us -> 7.94 us
  waiting for transfers between devices: 52.5 us -> 54.7 us
    gather x4 -> x0, local copies, waits for them, and re-layouts: 7.32 us -> none  [the longest x3 4.51 us: local(): answer = jnp.where(is_valid[None], surface[:, slot_index], 0.0)]
    all_to_all x1, starting transfers between devices: 12 us -> 8.82 us  [local(): lax.all_to_all(packed.reshape(3, tile_count, capacity), 'tile', split_axi...]
    dot_general x1 -> x3, matrix products: 5.51 us -> 7.94 us  [pick_matmul(): product = jnp.dot(stacked, pick, preferred_element_type=jnp.float32)]
    ppermute x1, waiting for transfers between devices: 1.65 us -> 3.12 us  [with_halo(): before = lax.ppermute(last, axis, up)]
  transfers between devices with their start and end apart: 6 -> 6, of which waited for: 6 -> 6; matrix products, arithmetic and copies ran while one was open for 4% -> 3% of each run, Pallas kernels for 0% -> 0%
where the time goes in v10:
time: 139 us; the launch traced here: 138 us
  waiting for transfers between devices  54.7 us (39%)
  starting transfers between devices  47.3 us (34%)
  other arithmetic  11.6 us (8%)
  local copies, waits for them, and re-layouts  8.49 us (6%)
  matrix products  7.94 us (6%)
  Pallas kernels  6.9 us (5%)
    all_to_all x1, starting transfers between devices, local(): lax.all_to_all(requests.reshape(tile_count, capacity), 'tile', split_axis...  21.8 us
    all_to_all x1, waiting for transfers between devices, local(): lax.all_to_all(packed.reshape(3, tile_count, capacity), 'tile', split_axi...  16.8 us
    all_to_all x1, waiting for transfers between devices, local(): lax.all_to_all(answer, 'tile', split_axis=1, concat_axis=1, tiled=True)  16.2 us
    all_to_all x1, waiting for transfers between devices, local(): lax.all_to_all(requests.reshape(tile_count, capacity), 'tile', split_axis...  10.6 us
    all_to_all x1, starting transfers between devices, local(): lax.all_to_all(packed.reshape(3, tile_count, capacity), 'tile', split_axi...  8.82 us
    dot_general x3, matrix products, pick_matmul(): product = jnp.dot(stacked, pick, preferred_element_type=jnp.float32)  7.94 us
    pallas_call x1, Pallas kernels, propagate(): pl.pallas_call(kernel, grid=(bins // block,), in_specs=[pl.BlockSpec(memo...  6.9 us
    all_to_all x1, starting transfers between devices, local(): lax.all_to_all(answer, 'tile', split_axis=1, concat_axis=1, tiled=True)  6.35 us
  transfers between devices with their start and end apart: 6, of which 6 were waited for; matrix products, arithmetic and copies ran while one was open for 3% of the time, Pallas kernels for 0%

profile of v10, /device:TPU:8, one launch (start us, length us, event | category | flops | bytes accessed | tf_op | source)
XLA Modules:
  0.0 137.8 jit_solution(18031461717269083761)
XLA Ops:
  0.6 1.3 convert_reduce_fusion
  1.9 0.7 broadcast_add_fusion.1
  2.6 0.7 compare_select_fusion
  3.3 1.0 select_reduce_fusion
  4.3 0.8 sub.42
  5.0 21.8 %all-to-all-start = ((s32[96,1,22]{2,1,0:T(1,128)}), s32[96,1,22]{2,1,0:T(1,128)S(1)}, u32[]{:S(2)}, u32[]{:S(2)}) async-start(s32[96,1,22]{2,1,0:T(1,128)} %bitcast.6), calls=%async_computation | async-start | bytes 98304 | tf_op jit(solution)/shard_map/all_to_all | solution.py:150
  26.8 0.7 multiply_add_fusion
  27.5 0.7 fusion.38
  28.2 0.8 reduce-precision_convert_fusion.5
  29.0 0.8 select_reduce_fusion.1
  29.7 10.6 %all-to-all-done = s32[96,1,22]{2,1,0:T(1,128)S(1)} async-done(((s32[96,1,22]{2,1,0:T(1,128)}), s32[96,1,22]{2,1,0:T(1,128)S(1)}, u32[]{:S(2)}, u32[]{:S(2)}) %all-to-all-start) | async-done | bytes 8480 | tf_op jit(solution)/shard_map/all_to_all | solution.py:150
  40.9 0.8 reduce.7
  41.8 3.2 %fusion.1 = f32[9,2112]{1,0:T(8,128)S(1)} fusion(s32[2112]{0:T(1024)S(1)} %eq.85, bf16[3,2048]{1,0:T(4,128)(2,1)S(1)} %get-tuple-element.19, bf16[3,2048]{1,0:T(4,128)(2,1)S(1)} %get-tuple-element.20, bf16[3,2048]{1,0:T(4,128)(2,1)S(1)} %get-tuple-element.18), kind=kOutput, calls=%fused_computation.3 | convolution fusion | flops 82292736 | bytes 121344 | tf_op jit(solution)/shard_map/dot_general | solution.py:117
  45.2 0.8 copy.21
  46.0 6.3 %all-to-all-start.1 = ((f32[3,96,22]{2,0,1:T(4,128)}), f32[3,96,22]{2,0,1:T(4,128)S(1)}, u32[]{:S(2)}, u32[]{:S(2)}) async-start(f32[3,96,22]{2,0,1:T(4,128)} %copy.21), calls=%async_computation.1 | async-start | bytes 393216 | tf_op jit(solution)/shard_map/all_to_all | solution.py:159
  52.4 16.2 %all-to-all-done.1 = f32[3,96,22]{2,0,1:T(4,128)S(1)} async-done(((f32[3,96,22]{2,0,1:T(4,128)}), f32[3,96,22]{2,0,1:T(4,128)S(1)}, u32[]{:S(2)}, u32[]{:S(2)}) %all-to-all-start.1) | async-done | bytes 25376 | tf_op jit(solution)/shard_map/all_to_all | solution.py:159
  68.8 1.6 %fusion.4 = f32[9,1024]{1,0:T(8,128)S(1)} fusion(s32[1024]{0:T(1024)S(1)} %multiply_add_fusion, bf16[3,2112]{1,0:T(4,128)(2,1)S(1)} %get-tuple-element.16, bf16[3,2112]{1,0:T(4,128)(2,1)S(1)} %get-tuple-element.17, bf16[3,2112]{1,0:T(4,128)(2,1)S(1)} %get-tuple-element.15), kind=kOutput, calls=%fused_computation.9 | convolution fusion | flops 41205120 | bytes 78976 | tf_op jit(solution)/shard_map/dot_general | solution.py:117
  70.6 3.1 %collective-permute-start.1 = (f32[165,4,128]{2,1,0:T(4,128)S(1)}, f32[165,4,128]{2,1,0:T(4,128)S(1)}, u32[]{:S(2)}, u32[]{:S(2)}) collective-permute-start(f32[165,4,128]{2,1,0:T(4,128)S(1)} %get-tuple-element.11), channel_id=1, source_target_pairs={{1,0},{2,1},{3,2},{4,3},{5,4},{6,5},{7,6},{8,7},{9,8},{10,9},{11,1... | collective-permute-start | bytes 1013768 | tf_op jit(solution)/shard_map/ppermute | solution.py:24
  73.7 2.9 %collective-permute-start = (f32[165,4,128]{2,1,0:T(4,128)S(1)}, f32[165,4,128]{2,1,0:T(4,128)S(1)}, u32[]{:S(2)}, u32[]{:S(2)}) collective-permute-start(f32[165,4,128]{2,1,0:T(4,128)S(1)} %get-tuple-element.10), channel_id=1, source_target_pairs={{0,1},{1,2},{2,3},{3,4},{4,5},{5,6},{6,7},{7,8},{8,9},{9,10},{10,1... | collective-permute-start | bytes 1013768 | tf_op jit(solution)/shard_map/ppermute | solution.py:23
  77.8 1.8 %collective-permute-done.1 = f32[165,4,128]{2,1,0:T(4,128)S(1)} collective-permute-done((f32[165,4,128]{2,1,0:T(4,128)S(1)}, f32[165,4,128]{2,1,0:T(4,128)S(1)}, u32[]{:S(2)}, u32[]{:S(2)}) %collective-permute-start.1) | collective-permute-done | bytes 337952 | tf_op jit(solution)/shard_map/ppermute | solution.py:24
  79.6 3.1 %collective-permute-done = f32[165,4,128]{2,1,0:T(4,128)S(1)} collective-permute-done((f32[165,4,128]{2,1,0:T(4,128)S(1)}, f32[165,4,128]{2,1,0:T(4,128)S(1)}, u32[]{:S(2)}, u32[]{:S(2)}) %collective-permute-start) | collective-permute-done | bytes 337952 | tf_op jit(solution)/shard_map/ppermute | solution.py:23
  82.8 1.3 pad_maximum_fusion.energy_ref.flow_ref
  84.1 6.9 %shard_map.95 = (f32[162,8,128]{2,1,0:T(8,128)}, f32[3,8,128]{2,1,0:T(8,128)}) custom-call(f32[2,162]{1,0:T(2,128)} %pad_maximum_fusion.4.speed_ref, f32[3,162]{1,0:T(4,128)} %maximum_multiply_fusion.weight_ref, f32[165,16,128]{2,1,0:T(8,128)} %pad_maximum_fusion.energy_ref.flow_ref, f32[165,16,128]{2,1,0:T(8,128)} %pad_maximum_fusion.energy_ref.flow_ref), custom_call_target="tpu_custom_call" | custom-call | tf_op jit(solution)/shard_map/pallas_call | solution.py:88
  91.0 0.7 bitcast_multiply_fusion
  91.7 0.7 broadcast_in_dim.25
  92.4 4.3 %all-to-all-start.2 = ((f32[8,3,1024]{2,1,0:T(4,128)}), f32[8,3,1024]{2,1,0:T(4,128)S(1)}, u32[]{:S(2)}, u32[]{:S(2)}) async-start(f32[8,3,1024]{2,1,0:T(4,128)} %broadcast_in_dim.25), calls=%async_computation.2 | async-start | bytes 262144 | tf_op jit(solution)/shard_map/all_to_all | solution.py:178
  96.7 6.1 %all-to-all-done.2 = f32[8,3,1024]{2,1,0:T(4,128)S(1)} async-done(((f32[8,3,1024]{2,1,0:T(4,128)}), f32[8,3,1024]{2,1,0:T(4,128)S(1)}, u32[]{:S(2)}, u32[]{:S(2)}) %all-to-all-start.2) | async-done | bytes 98336 | tf_op jit(solution)/shard_map/all_to_all | solution.py:178
  103.1 3.4 %scatter_custom_fusion = f32[3,2112]{0,1:T(8,128)S(1)} fusion(s32[1024]{0:T(1024)S(1)} %bitcast.37, f32[1024,3]{1,0:T(8,128)S(1)} %copy.23, f32[]{:T(128)} %constant.23.clone.1), kind=kCustom, calls=%fused_computation.16 | custom fusion | bytes 25348 | tf_op jit(solution)/shard_map/scatter | solution.py:188
  107.0 0.8 copy.25
  107.7 8.8 %all-to-all-start.3 = ((f32[3,96,22]{2,0,1:T(4,128)}), f32[3,96,22]{2,0,1:T(4,128)S(1)}, u32[]{:S(2)}, u32[]{:S(2)}) async-start(f32[3,96,22]{2,0,1:T(4,128)} %copy.25), calls=%async_computation.3 | async-start | bytes 393216 | tf_op jit(solution)/shard_map/all_to_all | solution.py:189
  116.9 16.8 %all-to-all-done.3 = f32[3,96,22]{2,0,1:T(4,128)S(1)} async-done(((f32[3,96,22]{2,0,1:T(4,128)}), f32[3,96,22]{2,0,1:T(4,128)S(1)}, u32[]{:S(2)}, u32[]{:S(2)}) %all-to-all-start.3) | async-done | bytes 25376 | tf_op jit(solution)/shard_map/all_to_all | solution.py:189
  133.9 3.2 %fusion = f32[12,2048]{1,0:T(8,128)S(1)} fusion(s32[2112]{0:T(1024)S(1)} %eq.85, bf16[4,2112]{1,0:T(4,128)(2,1)S(1)} %get-tuple-element.14, bf16[4,2112]{1,0:T(4,128)(2,1)S(1)} %get-tuple-element.13, bf16[4,2112]{1,0:T(4,128)(2,1)S(1)} %get-tuple-element.12), kind=kOutput, calls=%fused_computation.2 | convolution fusion | flops 108286464 | bytes 157440 | tf_op jit(solution)/shard_map/dot_general | solution.py:117
  (34 shorter events, 4.4 us)
Async XLA Ops:
  5.0 35.4 %all-to-all-start = ((s32[96,1,22]{2,1,0:T(1,128)}), s32[96,1,22]{2,1,0:T(1,128)S(1)}, u32[]{:S(2)}, u32[]{:S(2)}) async-start(s32[96,1,22]{2,1,0:T(1,128)} %bitcast.6), calls=%async_computation | async-start | bytes 98304 | tf_op jit(solution)/shard_map/all_to_all | solution.py:150
  46.0 22.6 %all-to-all-start.1 = ((f32[3,96,22]{2,0,1:T(4,128)}), f32[3,96,22]{2,0,1:T(4,128)S(1)}, u32[]{:S(2)}, u32[]{:S(2)}) async-start(f32[3,96,22]{2,0,1:T(4,128)} %copy.21), calls=%async_computation.1 | async-start | bytes 393216 | tf_op jit(solution)/shard_map/all_to_all | solution.py:159
  68.7 1.7 %copy-start = (f32[162,8,128]{2,1,0:T(8,128)S(1)}, f32[162,8,128]{2,1,0:T(8,128)}, u32[]{:S(2)}) copy-start(f32[162,8,128]{2,1,0:T(8,128)} %param.8) | copy-start | bytes 1990660
  70.6 9.1 %collective-permute-start.1 = (f32[165,4,128]{2,1,0:T(4,128)S(1)}, f32[165,4,128]{2,1,0:T(4,128)S(1)}, u32[]{:S(2)}, u32[]{:S(2)}) collective-permute-start(f32[165,4,128]{2,1,0:T(4,128)S(1)} %get-tuple-element.11), channel_id=1, source_target_pairs={{1,0},{2,1},{3,2},{4,3},{5,4},{6,5},{7,6},{8,7},{9,8},{10,9},{11,1... | collective-permute-start | bytes 1013768 | tf_op jit(solution)/shard_map/ppermute | solution.py:24
  73.7 9.1 %collective-permute-start = (f32[165,4,128]{2,1,0:T(4,128)S(1)}, f32[165,4,128]{2,1,0:T(4,128)S(1)}, u32[]{:S(2)}, u32[]{:S(2)}) collective-permute-start(f32[165,4,128]{2,1,0:T(4,128)S(1)} %get-tuple-element.10), channel_id=1, source_target_pairs={{0,1},{1,2},{2,3},{3,4},{4,5},{5,6},{6,7},{7,8},{8,9},{9,10},{10,1... | collective-permute-start | bytes 1013768 | tf_op jit(solution)/shard_map/ppermute | solution.py:23
  92.4 10.4 %all-to-all-start.2 = ((f32[8,3,1024]{2,1,0:T(4,128)}), f32[8,3,1024]{2,1,0:T(4,128)S(1)}, u32[]{:S(2)}, u32[]{:S(2)}) async-start(f32[8,3,1024]{2,1,0:T(4,128)} %broadcast_in_dim.25), calls=%async_computation.2 | async-start | bytes 262144 | tf_op jit(solution)/shard_map/all_to_all | solution.py:178
  107.7 25.9 %all-to-all-start.3 = ((f32[3,96,22]{2,0,1:T(4,128)}), f32[3,96,22]{2,0,1:T(4,128)S(1)}, u32[]{:S(2)}, u32[]{:S(2)}) async-start(f32[3,96,22]{2,0,1:T(4,128)} %copy.25), calls=%async_computation.3 | async-start | bytes 393216 | tf_op jit(solution)/shard_map/all_to_all | solution.py:189

commit v11 on v10

--- a/solution.py
+++ b/solution.py
@@ -151,7 +151,6 @@
         requests.reshape(tile_count, capacity), "tile", split_axis=0, concat_axis=0, tiled=True
     )
     is_valid = asked_slots >= 0
-    slot_index = jnp.where(is_valid, asked_slots, 0)
     surface = jnp.concatenate([ocean_currents, elevation[None]], 0)
     ocean_ids = jnp.arange(ocean_cells, dtype=jnp.int32)
     slot_pick = (ocean_ids[:, None] == asked_slots.reshape(-1)[None, :]).astype(jnp.bfloat16)
@@ -185,11 +184,10 @@
     partial_value = every_part[0]
     for part in range(1, sect_count):
         partial_value = partial_value + every_part[part]
-    packed = jnp.zeros((3, tile_count * capacity), jnp.float32).at[:, position].set(partial_value)
+    packed = pick_matmul(partial_value, cell_pick.T)
     arrived = lax.all_to_all(
         packed.reshape(3, tile_count, capacity), "tile", split_axis=1, concat_axis=1, tiled=True
     )
-    flat_slots = asked_slots.reshape(-1)
     weight = is_valid.reshape(-1).astype(jnp.float32)
     summed = pick_matmul(
         jnp.concatenate([arrived.reshape(3, -1) * weight[None], weight[None]], 0), slot_pick.T

time: 139 us -> 139 us (level)
  local copies, waits for them, and re-layouts: 8.49 us -> 4.54 us
  starting transfers between devices: 47.3 us -> 50.5 us
  matrix products: 7.94 us -> 9.46 us
    scatter x2 -> x0, local copies, waits for them, and re-layouts: 3.7 us -> none  [local(): jnp.zeros((3, tile_count * capacity), jnp.float32).at[:, position]]
    all_to_all x1, starting transfers between devices: 8.82 us -> 12 us  [local(): lax.all_to_all(packed.reshape(3, tile_count, capacity), 'tile', split_axi...]
    dot_general x3 -> x4, matrix products: 7.94 us -> 9.46 us  [pick_matmul(): product = jnp.dot(stacked, pick, preferred_element_type=jnp.float32)]
where the time goes in v11:
time: 139 us; the launch traced here: 138 us
  waiting for transfers between devices  54 us (39%)
  starting transfers between devices  50.5 us (36%)
  other arithmetic  11.7 us (8%)
  matrix products  9.46 us (7%)
  Pallas kernels  6.9 us (5%)
  local copies, waits for them, and re-layouts  4.54 us (3%)
    all_to_all x1, starting transfers between devices, local(): lax.all_to_all(requests.reshape(tile_count, capacity), 'tile', split_axis...  21.8 us
    all_to_all x1, waiting for transfers between devices, local(): lax.all_to_all(packed.reshape(3, tile_count, capacity), 'tile', split_axi...  16.8 us
    all_to_all x1, waiting for transfers between devices, local(): lax.all_to_all(answer, 'tile', split_axis=1, concat_axis=1, tiled=True)  16.2 us
    all_to_all x1, starting transfers between devices, local(): lax.all_to_all(packed.reshape(3, tile_count, capacity), 'tile', split_axi...  12 us
    all_to_all x1, waiting for transfers between devices, local(): lax.all_to_all(requests.reshape(tile_count, capacity), 'tile', split_axis...  10.6 us
    dot_general x4, matrix products, pick_matmul(): product = jnp.dot(stacked, pick, preferred_element_type=jnp.float32)  9.46 us
    pallas_call x1, Pallas kernels, propagate(): pl.pallas_call(kernel, grid=(bins // block,), in_specs=[pl.BlockSpec(memo...  6.9 us
    all_to_all x1, starting transfers between devices, local(): lax.all_to_all(answer, 'tile', split_axis=1, concat_axis=1, tiled=True)  6.35 us
  transfers between devices with their start and end apart: 6, of which 6 were waited for; matrix products, arithmetic and copies ran while one was open for 3% of the time, Pallas kernels for 0%

profile of v11, /device:TPU:8, one launch (start us, length us, event | category | flops | bytes accessed | tf_op | source)
XLA Modules:
  0.0 137.9 jit_solution(9730037327202690501)
XLA Ops:
  0.6 1.3 convert_reduce_fusion
  1.9 0.7 multiply_add_fusion.1
  2.6 0.7 broadcast_add_fusion.1
  3.3 1.0 select_reduce_fusion
  4.3 0.8 sub.48
  5.0 21.8 %all-to-all-start = ((s32[96,1,22]{2,1,0:T(1,128)}), s32[96,1,22]{2,1,0:T(1,128)S(1)}, u32[]{:S(2)}, u32[]{:S(2)}) async-start(s32[96,1,22]{2,1,0:T(1,128)} %bitcast.6), calls=%async_computation | async-start | bytes 98304 | tf_op jit(solution)/shard_map/all_to_all | solution.py:150
  26.8 0.7 multiply_add_fusion
  27.5 0.7 fusion.46
  28.2 0.8 reduce-precision_convert_fusion.5
  29.0 0.8 select_reduce_fusion.1
  29.7 10.6 %all-to-all-done = s32[96,1,22]{2,1,0:T(1,128)S(1)} async-done(((s32[96,1,22]{2,1,0:T(1,128)}), s32[96,1,22]{2,1,0:T(1,128)S(1)}, u32[]{:S(2)}, u32[]{:S(2)}) %all-to-all-start) | async-done | bytes 8480 | tf_op jit(solution)/shard_map/all_to_all | solution.py:150
  40.9 0.8 reduce.7
  41.8 3.2 %fusion.1 = f32[9,2112]{1,0:T(8,128)S(1)} fusion(s32[2112]{0:T(1024)S(1)} %eq.85, bf16[3,2048]{1,0:T(4,128)(2,1)S(1)} %get-tuple-element.19, bf16[3,2048]{1,0:T(4,128)(2,1)S(1)} %get-tuple-element.20, bf16[3,2048]{1,0:T(4,128)(2,1)S(1)} %get-tuple-element.18), kind=kOutput, calls=%fused_computation.2 | convolution fusion | flops 82292736 | bytes 121344 | tf_op jit(solution)/shard_map/dot_general | solution.py:117
  45.2 0.8 copy.16
  46.0 6.3 %all-to-all-start.1 = ((f32[3,96,22]{2,0,1:T(4,128)}), f32[3,96,22]{2,0,1:T(4,128)S(1)}, u32[]{:S(2)}, u32[]{:S(2)}) async-start(f32[3,96,22]{2,0,1:T(4,128)} %copy.16), calls=%async_computation.1 | async-start | bytes 393216 | tf_op jit(solution)/shard_map/all_to_all | solution.py:158
  52.4 16.2 %all-to-all-done.1 = f32[3,96,22]{2,0,1:T(4,128)S(1)} async-done(((f32[3,96,22]{2,0,1:T(4,128)}), f32[3,96,22]{2,0,1:T(4,128)S(1)}, u32[]{:S(2)}, u32[]{:S(2)}) %all-to-all-start.1) | async-done | bytes 25376 | tf_op jit(solution)/shard_map/all_to_all | solution.py:158
  68.8 1.6 %fusion.5 = f32[9,1024]{1,0:T(8,128)S(1)} fusion(s32[1024]{0:T(1024)S(1)} %multiply_add_fusion, bf16[3,2112]{1,0:T(4,128)(2,1)S(1)} %get-tuple-element.16, bf16[3,2112]{1,0:T(4,128)(2,1)S(1)} %get-tuple-element.17, bf16[3,2112]{1,0:T(4,128)(2,1)S(1)} %get-tuple-element.15), kind=kOutput, calls=%fused_computation.7 | convolution fusion | flops 41205120 | bytes 78976 | tf_op jit(solution)/shard_map/dot_general | solution.py:117
  70.6 2.4 %collective-permute-start = (f32[165,4,128]{2,1,0:T(4,128)S(1)}, f32[165,4,128]{2,1,0:T(4,128)S(1)}, u32[]{:S(2)}, u32[]{:S(2)}) collective-permute-start(f32[165,4,128]{2,1,0:T(4,128)S(1)} %get-tuple-element.10), channel_id=1, source_target_pairs={{0,1},{1,2},{2,3},{3,4},{4,5},{5,6},{6,7},{7,8},{8,9},{9,10},{10,1... | collective-permute-start | bytes 1013768 | tf_op jit(solution)/shard_map/ppermute | solution.py:23
  73.0 3.6 %collective-permute-start.1 = (f32[165,4,128]{2,1,0:T(4,128)S(1)}, f32[165,4,128]{2,1,0:T(4,128)S(1)}, u32[]{:S(2)}, u32[]{:S(2)}) collective-permute-start(f32[165,4,128]{2,1,0:T(4,128)S(1)} %get-tuple-element.11), channel_id=1, source_target_pairs={{1,0},{2,1},{3,2},{4,3},{5,4},{6,5},{7,6},{8,7},{9,8},{10,9},{11,1... | collective-permute-start | bytes 1013768 | tf_op jit(solution)/shard_map/ppermute | solution.py:24
  77.8 1.8 %collective-permute-done = f32[165,4,128]{2,1,0:T(4,128)S(1)} collective-permute-done((f32[165,4,128]{2,1,0:T(4,128)S(1)}, f32[165,4,128]{2,1,0:T(4,128)S(1)}, u32[]{:S(2)}, u32[]{:S(2)}) %collective-permute-start) | collective-permute-done | bytes 337952 | tf_op jit(solution)/shard_map/ppermute | solution.py:23
  79.6 2.4 %collective-permute-done.1 = f32[165,4,128]{2,1,0:T(4,128)S(1)} collective-permute-done((f32[165,4,128]{2,1,0:T(4,128)S(1)}, f32[165,4,128]{2,1,0:T(4,128)S(1)}, u32[]{:S(2)}, u32[]{:S(2)}) %collective-permute-start.1) | collective-permute-done | bytes 337952 | tf_op jit(solution)/shard_map/ppermute | solution.py:24
  82.1 1.3 pad_maximum_fusion.energy_ref.flow_ref
  83.4 6.9 %shard_map.95 = (f32[162,8,128]{2,1,0:T(8,128)}, f32[3,8,128]{2,1,0:T(8,128)}) custom-call(f32[2,162]{1,0:T(2,128)} %pad_maximum_fusion.4.speed_ref, f32[3,162]{1,0:T(4,128)} %maximum_multiply_fusion.weight_ref, f32[165,16,128]{2,1,0:T(8,128)} %pad_maximum_fusion.energy_ref.flow_ref, f32[165,16,128]{2,1,0:T(8,128)} %pad_maximum_fusion.energy_ref.flow_ref), custom_call_target="tpu_custom_call" | custom-call | tf_op jit(solution)/shard_map/pallas_call | solution.py:88
  90.3 0.7 bitcast_multiply_fusion
  91.0 0.7 broadcast_in_dim.22
  91.7 4.3 %all-to-all-start.2 = ((f32[8,3,1024]{2,1,0:T(4,128)}), f32[8,3,1024]{2,1,0:T(4,128)S(1)}, u32[]{:S(2)}, u32[]{:S(2)}) async-start(f32[8,3,1024]{2,1,0:T(4,128)} %broadcast_in_dim.22), calls=%async_computation.2 | async-start | bytes 262144 | tf_op jit(solution)/shard_map/all_to_all | solution.py:177
  96.0 6.1 %all-to-all-done.2 = f32[8,3,1024]{2,1,0:T(4,128)S(1)} async-done(((f32[8,3,1024]{2,1,0:T(4,128)}), f32[8,3,1024]{2,1,0:T(4,128)S(1)}, u32[]{:S(2)}, u32[]{:S(2)}) %all-to-all-start.2) | async-done | bytes 98336 | tf_op jit(solution)/shard_map/all_to_all | solution.py:177
  102.1 1.5 %fusion.4 = f32[9,2112]{1,0:T(8,128)S(1)} fusion(s32[1024]{0:T(1024)S(1)} %multiply_add_fusion, bf16[3,1024]{1,0:T(4,128)(2,1)S(1)} %get-tuple-element.22, bf16[3,1024]{1,0:T(4,128)(2,1)S(1)} %get-tuple-element.21, bf16[3,1024]{1,0:T(4,128)(2,1)S(1)} %get-tuple-element.8), kind=kOutput, calls=%fused_computation.6 | convolution fusion | flops 41146368 | bytes 98560 | tf_op jit(solution)/shard_map/dot_general | solution.py:117
  103.9 0.8 copy.18
  104.6 12.0 %all-to-all-start.3 = ((f32[3,96,22]{2,0,1:T(4,128)}), f32[3,96,22]{2,0,1:T(4,128)S(1)}, u32[]{:S(2)}, u32[]{:S(2)}) async-start(f32[3,96,22]{2,0,1:T(4,128)} %copy.18), calls=%async_computation.3 | async-start | bytes 393216 | tf_op jit(solution)/shard_map/all_to_all | solution.py:188
  117.0 16.8 %all-to-all-done.3 = f32[3,96,22]{2,0,1:T(4,128)S(1)} async-done(((f32[3,96,22]{2,0,1:T(4,128)}), f32[3,96,22]{2,0,1:T(4,128)S(1)}, u32[]{:S(2)}, u32[]{:S(2)}) %all-to-all-start.3) | async-done | bytes 25376 | tf_op jit(solution)/shard_map/all_to_all | solution.py:188
  134.0 3.2 %fusion = f32[12,2048]{1,0:T(8,128)S(1)} fusion(s32[2112]{0:T(1024)S(1)} %eq.85, bf16[4,2112]{1,0:T(4,128)(2,1)S(1)} %get-tuple-element.14, bf16[4,2112]{1,0:T(4,128)(2,1)S(1)} %get-tuple-element.13, bf16[4,2112]{1,0:T(4,128)(2,1)S(1)} %get-tuple-element.12), kind=kOutput, calls=%fused_computation.1 | convolution fusion | flops 108286464 | bytes 157440 | tf_op jit(solution)/shard_map/dot_general | solution.py:117
  (34 shorter events, 3.9 us)
Async XLA Ops:
  5.0 35.4 %all-to-all-start = ((s32[96,1,22]{2,1,0:T(1,128)}), s32[96,1,22]{2,1,0:T(1,128)S(1)}, u32[]{:S(2)}, u32[]{:S(2)}) async-start(s32[96,1,22]{2,1,0:T(1,128)} %bitcast.6), calls=%async_computation | async-start | bytes 98304 | tf_op jit(solution)/shard_map/all_to_all | solution.py:150
  46.0 22.6 %all-to-all-start.1 = ((f32[3,96,22]{2,0,1:T(4,128)}), f32[3,96,22]{2,0,1:T(4,128)S(1)}, u32[]{:S(2)}, u32[]{:S(2)}) async-start(f32[3,96,22]{2,0,1:T(4,128)} %copy.16), calls=%async_computation.1 | async-start | bytes 393216 | tf_op jit(solution)/shard_map/all_to_all | solution.py:158
  68.7 1.7 %copy-start = (f32[162,8,128]{2,1,0:T(8,128)S(1)}, f32[162,8,128]{2,1,0:T(8,128)}, u32[]{:S(2)}) copy-start(f32[162,8,128]{2,1,0:T(8,128)} %param.8) | copy-start | bytes 1990660
  70.6 9.1 %collective-permute-start = (f32[165,4,128]{2,1,0:T(4,128)S(1)}, f32[165,4,128]{2,1,0:T(4,128)S(1)}, u32[]{:S(2)}, u32[]{:S(2)}) collective-permute-start(f32[165,4,128]{2,1,0:T(4,128)S(1)} %get-tuple-element.10), channel_id=1, source_target_pairs={{0,1},{1,2},{2,3},{3,4},{4,5},{5,6},{6,7},{7,8},{8,9},{9,10},{10,1... | collective-permute-start | bytes 1013768 | tf_op jit(solution)/shard_map/ppermute | solution.py:23
  73.0 9.1 %collective-permute-start.1 = (f32[165,4,128]{2,1,0:T(4,128)S(1)}, f32[165,4,128]{2,1,0:T(4,128)S(1)}, u32[]{:S(2)}, u32[]{:S(2)}) collective-permute-start(f32[165,4,128]{2,1,0:T(4,128)S(1)} %get-tuple-element.11), channel_id=1, source_target_pairs={{1,0},{2,1},{3,2},{4,3},{5,4},{6,5},{7,6},{8,7},{9,8},{10,9},{11,1... | collective-permute-start | bytes 1013768 | tf_op jit(solution)/shard_map/ppermute | solution.py:24
  91.7 10.4 %all-to-all-start.2 = ((f32[8,3,1024]{2,1,0:T(4,128)}), f32[8,3,1024]{2,1,0:T(4,128)S(1)}, u32[]{:S(2)}, u32[]{:S(2)}) async-start(f32[8,3,1024]{2,1,0:T(4,128)} %broadcast_in_dim.22), calls=%async_computation.2 | async-start | bytes 262144 | tf_op jit(solution)/shard_map/all_to_all | solution.py:177
  104.6 29.2 %all-to-all-start.3 = ((f32[3,96,22]{2,0,1:T(4,128)}), f32[3,96,22]{2,0,1:T(4,128)S(1)}, u32[]{:S(2)}, u32[]{:S(2)}) async-start(f32[3,96,22]{2,0,1:T(4,128)} %copy.18), calls=%async_computation.3 | async-start | bytes 393216 | tf_op jit(solution)/shard_map/all_to_all | solution.py:188

commit v12 on v11

--- a/solution.py
+++ b/solution.py
@@ -144,9 +144,9 @@
     rank_in = jnp.sum(same_before.astype(jnp.int32), 1)
     position = owners * capacity + rank_in
     slot_ids = jnp.arange(tile_count * capacity, dtype=jnp.int32)
-    requests = (
-        jnp.sum(jnp.where(position[:, None] == slot_ids[None, :], ocean_slot[:, None] + 1, 0), 0) - 1
-    )
+    cell_pick = (slot_ids[:, None] == position[None, :]).astype(jnp.bfloat16)
+    wanted = pick_matmul((ocean_slot + 1).astype(jnp.float32)[None], cell_pick.T)
+    requests = jnp.round(wanted[0]).astype(jnp.int32) - 1
     asked_slots = lax.all_to_all(
         requests.reshape(tile_count, capacity), "tile", split_axis=0, concat_axis=0, tiled=True
     )
@@ -156,7 +156,6 @@
     slot_pick = (ocean_ids[:, None] == asked_slots.reshape(-1)[None, :]).astype(jnp.bfloat16)
     answer = pick_matmul(surface, slot_pick).reshape(3, tile_count, capacity)
     returned = lax.all_to_all(answer, "tile", split_axis=1, concat_axis=1, tiled=True)
-    cell_pick = (slot_ids[:, None] == position[None, :]).astype(jnp.bfloat16)
     at_cells = pick_matmul(returned.reshape(3, tile_count * capacity), cell_pick)
     sea_float = sea_mask.astype(jnp.float32)
     flow_fields = jnp.concatenate([at_cells[:2].reshape(2, row_count, columns), sea_float[None]], 0)

time: 139 us -> 139 us (level)
  other arithmetic: 11.7 us -> 7.96 us
  waiting for transfers between devices: 54 us -> 56.7 us
  matrix products: 9.46 us -> 11 us
    all_to_all x1, waiting for transfers between devices: 10.6 us -> 13.3 us  [local(): lax.all_to_all(requests.reshape(tile_count, capacity), 'tile', split_axis...]
    dot_general x4 -> x5, matrix products: 9.46 us -> 11 us  [pick_matmul(): product = jnp.dot(stacked, pick, preferred_element_type=jnp.float32)]
  transfers between devices with their start and end apart: 6 -> 6, of which waited for: 6 -> 6; matrix products, arithmetic and copies ran while one was open for 3% -> 1% of each run, Pallas kernels for 0% -> 0%
where the time goes in v12:
time: 139 us
  waiting for transfers between devices  56.7 us (41%)
  starting transfers between devices  50.5 us (36%)
  matrix products  11 us (8%)
  other arithmetic  7.96 us (6%)
  Pallas kernels  6.9 us (5%)
  local copies, waits for them, and re-layouts  4.57 us (3%)
    all_to_all x1, starting transfers between devices, local(): lax.all_to_all(requests.reshape(tile_count, capacity), 'tile', split_axis...  21.8 us
    all_to_all x1, waiting for transfers between devices, local(): lax.all_to_all(packed.reshape(3, tile_count, capacity), 'tile', split_axi...  16.8 us
    all_to_all x1, waiting for transfers between devices, local(): lax.all_to_all(answer, 'tile', split_axis=1, concat_axis=1, tiled=True)  16.2 us
    all_to_all x1, waiting for transfers between devices, local(): lax.all_to_all(requests.reshape(tile_count, capacity), 'tile', split_axis...  13.3 us
    all_to_all x1, starting transfers between devices, local(): lax.all_to_all(packed.reshape(3, tile_count, capacity), 'tile', split_axi...  12 us
    dot_general x5, matrix products, pick_matmul(): product = jnp.dot(stacked, pick, preferred_element_type=jnp.float32)  11 us
    pallas_call x1, Pallas kernels, propagate(): pl.pallas_call(kernel, grid=(bins // block,), in_specs=[pl.BlockSpec(memo...  6.9 us
    all_to_all x1, starting transfers between devices, local(): lax.all_to_all(answer, 'tile', split_axis=1, concat_axis=1, tiled=True)  6.35 us
  transfers between devices with their start and end apart: 6, of which 6 were waited for; matrix products, arithmetic and copies ran while one was open for 1% of the time, Pallas kernels for 0%

profile of v12, /device:TPU:8, one launch (start us, length us, event | category | flops | bytes accessed | tf_op | source)
XLA Modules:
  0.0 138.6 jit_solution(11982240832377829705)
XLA Ops:
  0.7 1.3 convert_reduce_fusion
  2.0 0.7 multiply_add_fusion
  2.7 0.7 reduce-precision_convert_fusion.9
  3.4 1.5 %fusion.6 = f32[3,2112]{1,0:T(4,128)S(1)} fusion(s32[1024]{0:T(1024)S(1)} %multiply_add_fusion, bf16[1,1024]{1,0:T(2,128)(2,1)S(1)} %sub.59, bf16[1,1024]{1,0:T(2,128)(2,1)S(1)} %reduce_precision.41, bf16[1,1024]{1,0:T(2,128)(2,1)S(1)} %reduce_precision.39), kind=kOutput, calls=%fused_computation.8 | convolution fusion | flops 15157248 | bytes 35584 | tf_op jit(solution)/shard_map/dot_general | solution.py:117
  4.9 0.8 sub.61
  5.7 21.8 %all-to-all-start = ((s32[96,1,22]{2,1,0:T(1,128)}), s32[96,1,22]{2,1,0:T(1,128)S(1)}, u32[]{:S(2)}, u32[]{:S(2)}) async-start(s32[96,1,22]{2,1,0:T(1,128)} %bitcast.4), calls=%async_computation | async-start | bytes 98304 | tf_op jit(solution)/shard_map/all_to_all | solution.py:150
  27.7 13.3 %all-to-all-done = s32[96,1,22]{2,1,0:T(1,128)S(1)} async-done(((s32[96,1,22]{2,1,0:T(1,128)}), s32[96,1,22]{2,1,0:T(1,128)S(1)}, u32[]{:S(2)}, u32[]{:S(2)}) %all-to-all-start) | async-done | bytes 8480 | tf_op jit(solution)/shard_map/all_to_all | solution.py:150
  41.0 0.5 broadcast.349
  41.6 0.8 reduce.9
  42.5 3.2 %fusion.1 = f32[9,2112]{1,0:T(8,128)S(1)} fusion(s32[2112]{0:T(1024)S(1)} %eq.66, bf16[3,2048]{1,0:T(4,128)(2,1)S(1)} %get-tuple-element.19, bf16[3,2048]{1,0:T(4,128)(2,1)S(1)} %get-tuple-element.20, bf16[3,2048]{1,0:T(4,128)(2,1)S(1)} %get-tuple-element.18), kind=kOutput, calls=%fused_computation.2 | convolution fusion | flops 82292736 | bytes 121344 | tf_op jit(solution)/shard_map/dot_general | solution.py:117
  45.8 0.8 copy.16
  46.6 6.3 %all-to-all-start.1 = ((f32[3,96,22]{2,0,1:T(4,128)}), f32[3,96,22]{2,0,1:T(4,128)S(1)}, u32[]{:S(2)}, u32[]{:S(2)}) async-start(f32[3,96,22]{2,0,1:T(4,128)} %copy.16), calls=%async_computation.1 | async-start | bytes 393216 | tf_op jit(solution)/shard_map/all_to_all | solution.py:158
  53.0 16.2 %all-to-all-done.1 = f32[3,96,22]{2,0,1:T(4,128)S(1)} async-done(((f32[3,96,22]{2,0,1:T(4,128)}), f32[3,96,22]{2,0,1:T(4,128)S(1)}, u32[]{:S(2)}, u32[]{:S(2)}) %all-to-all-start.1) | async-done | bytes 25376 | tf_op jit(solution)/shard_map/all_to_all | solution.py:158
  69.4 1.6 %fusion.5 = f32[9,1024]{1,0:T(8,128)S(1)} fusion(s32[1024]{0:T(1024)S(1)} %multiply_add_fusion, bf16[3,2112]{1,0:T(4,128)(2,1)S(1)} %get-tuple-element.16, bf16[3,2112]{1,0:T(4,128)(2,1)S(1)} %get-tuple-element.17, bf16[3,2112]{1,0:T(4,128)(2,1)S(1)} %get-tuple-element.15), kind=kOutput, calls=%fused_computation.7 | convolution fusion | flops 41205120 | bytes 78976 | tf_op jit(solution)/shard_map/dot_general | solution.py:117
  71.2 2.4 %collective-permute-start = (f32[165,4,128]{2,1,0:T(4,128)S(1)}, f32[165,4,128]{2,1,0:T(4,128)S(1)}, u32[]{:S(2)}, u32[]{:S(2)}) collective-permute-start(f32[165,4,128]{2,1,0:T(4,128)S(1)} %get-tuple-element.10), channel_id=1, source_target_pairs={{0,1},{1,2},{2,3},{3,4},{4,5},{5,6},{6,7},{7,8},{8,9},{9,10},{10,1... | collective-permute-start | bytes 1013768 | tf_op jit(solution)/shard_map/ppermute | solution.py:23
  73.6 3.6 %collective-permute-start.1 = (f32[165,4,128]{2,1,0:T(4,128)S(1)}, f32[165,4,128]{2,1,0:T(4,128)S(1)}, u32[]{:S(2)}, u32[]{:S(2)}) collective-permute-start(f32[165,4,128]{2,1,0:T(4,128)S(1)} %get-tuple-element.11), channel_id=1, source_target_pairs={{1,0},{2,1},{3,2},{4,3},{5,4},{6,5},{7,6},{8,7},{9,8},{10,9},{11,1... | collective-permute-start | bytes 1013768 | tf_op jit(solution)/shard_map/ppermute | solution.py:24
  77.3 0.6 pad_maximum_fusion.4.speed_ref
  77.9 0.6 maximum_multiply_fusion.weight_ref
  78.5 1.8 %collective-permute-done = f32[165,4,128]{2,1,0:T(4,128)S(1)} collective-permute-done((f32[165,4,128]{2,1,0:T(4,128)S(1)}, f32[165,4,128]{2,1,0:T(4,128)S(1)}, u32[]{:S(2)}, u32[]{:S(2)}) %collective-permute-start) | collective-permute-done | bytes 337952 | tf_op jit(solution)/shard_map/ppermute | solution.py:23
  80.3 2.4 %collective-permute-done.1 = f32[165,4,128]{2,1,0:T(4,128)S(1)} collective-permute-done((f32[165,4,128]{2,1,0:T(4,128)S(1)}, f32[165,4,128]{2,1,0:T(4,128)S(1)}, u32[]{:S(2)}, u32[]{:S(2)}) %collective-permute-start.1) | collective-permute-done | bytes 337952 | tf_op jit(solution)/shard_map/ppermute | solution.py:24
  82.7 1.3 pad_maximum_fusion.energy_ref.flow_ref
  84.1 6.9 %shard_map.95 = (f32[162,8,128]{2,1,0:T(8,128)}, f32[3,8,128]{2,1,0:T(8,128)}) custom-call(f32[2,162]{1,0:T(2,128)} %pad_maximum_fusion.4.speed_ref, f32[3,162]{1,0:T(4,128)} %maximum_multiply_fusion.weight_ref, f32[165,16,128]{2,1,0:T(8,128)} %pad_maximum_fusion.energy_ref.flow_ref, f32[165,16,128]{2,1,0:T(8,128)} %pad_maximum_fusion.energy_ref.flow_ref), custom_call_target="tpu_custom_call" | custom-call | tf_op jit(solution)/shard_map/pallas_call | solution.py:88
  91.0 0.7 bitcast_multiply_fusion
  91.7 0.7 broadcast_in_dim.8
  92.3 4.3 %all-to-all-start.2 = ((f32[8,3,1024]{2,1,0:T(4,128)}), f32[8,3,1024]{2,1,0:T(4,128)S(1)}, u32[]{:S(2)}, u32[]{:S(2)}) async-start(f32[8,3,1024]{2,1,0:T(4,128)} %broadcast_in_dim.8), calls=%async_computation.2 | async-start | bytes 262144 | tf_op jit(solution)/shard_map/all_to_all | solution.py:176
  96.6 6.1 %all-to-all-done.2 = f32[8,3,1024]{2,1,0:T(4,128)S(1)} async-done(((f32[8,3,1024]{2,1,0:T(4,128)}), f32[8,3,1024]{2,1,0:T(4,128)S(1)}, u32[]{:S(2)}, u32[]{:S(2)}) %all-to-all-start.2) | async-done | bytes 98336 | tf_op jit(solution)/shard_map/all_to_all | solution.py:176
  102.8 1.5 %fusion.4 = f32[9,2112]{1,0:T(8,128)S(1)} fusion(s32[1024]{0:T(1024)S(1)} %multiply_add_fusion, bf16[3,1024]{1,0:T(4,128)(2,1)S(1)} %get-tuple-element.22, bf16[3,1024]{1,0:T(4,128)(2,1)S(1)} %get-tuple-element.21, bf16[3,1024]{1,0:T(4,128)(2,1)S(1)} %get-tuple-element.8), kind=kOutput, calls=%fused_computation.6 | convolution fusion | flops 41146368 | bytes 98560 | tf_op jit(solution)/shard_map/dot_general | solution.py:117
  104.5 0.8 copy.18
  105.3 12.0 %all-to-all-start.3 = ((f32[3,96,22]{2,0,1:T(4,128)}), f32[3,96,22]{2,0,1:T(4,128)S(1)}, u32[]{:S(2)}, u32[]{:S(2)}) async-start(f32[3,96,22]{2,0,1:T(4,128)} %copy.18), calls=%async_computation.3 | async-start | bytes 393216 | tf_op jit(solution)/shard_map/all_to_all | solution.py:187
  117.7 16.8 %all-to-all-done.3 = f32[3,96,22]{2,0,1:T(4,128)S(1)} async-done(((f32[3,96,22]{2,0,1:T(4,128)}), f32[3,96,22]{2,0,1:T(4,128)S(1)}, u32[]{:S(2)}, u32[]{:S(2)}) %all-to-all-start.3) | async-done | bytes 25376 | tf_op jit(solution)/shard_map/all_to_all | solution.py:187
  134.7 3.2 %fusion = f32[12,2048]{1,0:T(8,128)S(1)} fusion(s32[2112]{0:T(1024)S(1)} %eq.66, bf16[4,2112]{1,0:T(4,128)(2,1)S(1)} %get-tuple-element.14, bf16[4,2112]{1,0:T(4,128)(2,1)S(1)} %get-tuple-element.13, bf16[4,2112]{1,0:T(4,128)(2,1)S(1)} %get-tuple-element.12), kind=kOutput, calls=%fused_computation.1 | convolution fusion | flops 108286464 | bytes 157440 | tf_op jit(solution)/shard_map/dot_general | solution.py:117
  138.0 0.6 slice_divide_fusion
  (46 shorter events, 1.7 us)
Async XLA Ops:
  0.6 26.9 %copy-start.3 = (s32[8,128]{1,0:T(8,128)S(1)}, s32[8,128]{1,0:T(8,128)}, u32[]{:S(2)}) copy-start(s32[8,128]{1,0:T(8,128)} %param.13) | copy-start | bytes 12292
  0.6 26.9 %copy-start.2 = (f32[2048]{0:T(1024)S(1)}, f32[2048]{0:T(1024)}, u32[]{:S(2)}) copy-start(f32[2048]{0:T(1024)} %param.12) | copy-start | bytes 24580
  0.7 26.9 %copy-start.1 = (f32[2,2048]{1,0:T(2,128)S(1)}, f32[2,2048]{1,0:T(2,128)}, u32[]{:S(2)}) copy-start(f32[2,2048]{1,0:T(2,128)} %param.11) | copy-start | bytes 49156
  0.7 26.9 %copy-start.4 = (f32[36]{0:T(128)S(1)}, f32[36]{0:T(128)}, u32[]{:S(2)}) copy-start(f32[36]{0:T(128)} %param.10) | copy-start | bytes 436
  0.7 26.9 %copy-start.5 = (f32[36]{0:T(128)S(1)}, f32[36]{0:T(128)}, u32[]{:S(2)}) copy-start(f32[36]{0:T(128)} %param.9) | copy-start | bytes 436
  5.7 35.4 %all-to-all-start = ((s32[96,1,22]{2,1,0:T(1,128)}), s32[96,1,22]{2,1,0:T(1,128)S(1)}, u32[]{:S(2)}, u32[]{:S(2)}) async-start(s32[96,1,22]{2,1,0:T(1,128)} %bitcast.4), calls=%async_computation | async-start | bytes 98304 | tf_op jit(solution)/shard_map/all_to_all | solution.py:150
  46.6 22.6 %all-to-all-start.1 = ((f32[3,96,22]{2,0,1:T(4,128)}), f32[3,96,22]{2,0,1:T(4,128)S(1)}, u32[]{:S(2)}, u32[]{:S(2)}) async-start(f32[3,96,22]{2,0,1:T(4,128)} %copy.16), calls=%async_computation.1 | async-start | bytes 393216 | tf_op jit(solution)/shard_map/all_to_all | solution.py:158
  69.4 1.7 %copy-start = (f32[162,8,128]{2,1,0:T(8,128)S(1)}, f32[162,8,128]{2,1,0:T(8,128)}, u32[]{:S(2)}) copy-start(f32[162,8,128]{2,1,0:T(8,128)} %param.8) | copy-start | bytes 1990660
  71.2 9.1 %collective-permute-start = (f32[165,4,128]{2,1,0:T(4,128)S(1)}, f32[165,4,128]{2,1,0:T(4,128)S(1)}, u32[]{:S(2)}, u32[]{:S(2)}) collective-permute-start(f32[165,4,128]{2,1,0:T(4,128)S(1)} %get-tuple-element.10), channel_id=1, source_target_pairs={{0,1},{1,2},{2,3},{3,4},{4,5},{5,6},{6,7},{7,8},{8,9},{9,10},{10,1... | collective-permute-start | bytes 1013768 | tf_op jit(solution)/shard_map/ppermute | solution.py:23
  73.6 9.1 %collective-permute-start.1 = (f32[165,4,128]{2,1,0:T(4,128)S(1)}, f32[165,4,128]{2,1,0:T(4,128)S(1)}, u32[]{:S(2)}, u32[]{:S(2)}) collective-permute-start(f32[165,4,128]{2,1,0:T(4,128)S(1)} %get-tuple-element.11), channel_id=1, source_target_pairs={{1,0},{2,1},{3,2},{4,3},{5,4},{6,5},{7,6},{8,7},{9,8},{10,9},{11,1... | collective-permute-start | bytes 1013768 | tf_op jit(solution)/shard_map/ppermute | solution.py:24
  92.3 10.4 %all-to-all-start.2 = ((f32[8,3,1024]{2,1,0:T(4,128)}), f32[8,3,1024]{2,1,0:T(4,128)S(1)}, u32[]{:S(2)}, u32[]{:S(2)}) async-start(f32[8,3,1024]{2,1,0:T(4,128)} %broadcast_in_dim.8), calls=%async_computation.2 | async-start | bytes 262144 | tf_op jit(solution)/shard_map/all_to_all | solution.py:176
  105.3 29.2 %all-to-all-start.3 = ((f32[3,96,22]{2,0,1:T(4,128)}), f32[3,96,22]{2,0,1:T(4,128)S(1)}, u32[]{:S(2)}, u32[]{:S(2)}) async-start(f32[3,96,22]{2,0,1:T(4,128)} %copy.18), calls=%async_computation.3 | async-start | bytes 393216 | tf_op jit(solution)/shard_map/all_to_all | solution.py:187

commit v13 on v11

--- a/solution.py
+++ b/solution.py
@@ -42,20 +42,44 @@
 
 
 def propagate_kernel(
-    speed_ref, weight_ref, energy_ref, flow_ref, out_ref, stress_ref, *, block, steps, rows_out
+    speed_ref,
+    weight_ref,
+    energy_ref,
+    flow_ref,
+    before_ref,
+    after_ref,
+    flow_before_ref,
+    flow_after_ref,
+    factor_ref,
+    out_ref,
+    stress_ref,
+    window_ref,
+    flow_window_ref,
+    *,
+    block,
+    steps,
 ):
-    rows = energy_ref.shape[1]
+    rows_out = energy_ref.shape[1]
+    width = before_ref.shape[1]
+    rows = rows_out + 2 * width
     lanes = energy_ref.shape[2]
     base = pl.program_id(0) * block
-    u = flow_ref[0]
-    v = flow_ref[1]
-    m = flow_ref[2]
 
     @pl.when(pl.program_id(0) == 0)
     def _():
         stress_ref[...] = jnp.zeros(stress_ref.shape, jnp.float32)
 
+    flow_window_ref[:, :rows_out] = flow_ref[...]
+    flow_window_ref[:, rows_out : rows_out + width] = flow_after_ref[...]
+    flow_window_ref[:, rows_out + width :] = flow_before_ref[...]
+    u = flow_window_ref[0]
+    v = flow_window_ref[1]
+    m = flow_window_ref[2]
+
     def one_bin(b, carry):
+        window_ref[b, :rows_out] = energy_ref[b]
+        window_ref[b, rows_out : rows_out + width] = after_ref[b]
+        window_ref[b, rows_out + width :] = before_ref[b]
         vel_x = speed_ref[0, base + b] + u
         vel_y = speed_ref[1, base + b] + v
         face_x = 0.5 * (vel_x + pltpu.roll(vel_x, lanes - 1, 1))
@@ -64,14 +88,14 @@
         neg_x = jnp.minimum(face_x, 0.0)
         pos_y = jnp.maximum(face_y, 0.0)
         neg_y = jnp.minimum(face_y, 0.0)
-        energy = energy_ref[b]
+        energy = window_ref[b]
         for _ in range(steps):
             flux_x = pos_x * energy + neg_x * pltpu.roll(energy, lanes - 1, 1)
             div_x = flux_x - pltpu.roll(flux_x, 1, 1)
             flux_y = pos_y * energy + neg_y * pltpu.roll(energy, rows - 1, 0)
             div_y = flux_y - pltpu.roll(flux_y, 1, 0)
             energy = m * (energy - div_x - div_y)
-        kept = pltpu.roll(energy, rows - steps, 0)[:rows_out]
+        kept = energy[:rows_out]
         out_ref[b] = kept
         return tuple(carry[k] + weight_ref[k, base + b] * kept for k in range(3))
 
@@ -80,19 +104,31 @@
     for k in range(3):
         stress_ref[k] = stress_ref[k] + sums[k]
 
-
-def propagate(speeds, weights, extended, bins, rows_out):
-    rows, lanes = extended.shape[1:]
+    @pl.when(pl.program_id(0) == pl.num_programs(0) - 1)
+    def _():
+        for k in range(3):
+            stress_ref[k] = stress_ref[k] * factor_ref[...]
+
+
+def propagate(speeds, weights, spectrum, flow_fields, before, after, factor):
+    bins, rows_out, lanes = spectrum.shape
+    width = before.shape[1]
     block = max(d for d in range(1, 33) if bins % d == 0)
-    kernel = functools.partial(propagate_kernel, block=block, steps=STEPS, rows_out=rows_out)
+    kernel = functools.partial(propagate_kernel, block=block, steps=STEPS)
+    flows_at = bins // 3
     return pl.pallas_call(
         kernel,
         grid=(bins // block,),
         in_specs=[
             pl.BlockSpec(memory_space=pltpu.MemorySpace.SMEM),
             pl.BlockSpec(memory_space=pltpu.MemorySpace.SMEM),
-            pl.BlockSpec((block, rows, lanes), lambda i: (i, 0, 0)),
-            pl.BlockSpec((3, rows, lanes), lambda i: (bins // 3, 0, 0)),
+            pl.BlockSpec((block, rows_out, lanes), lambda i: (i, 0, 0)),
+            pl.BlockSpec((3, rows_out, lanes), lambda i: (0, 0, 0)),
+            pl.BlockSpec((block, width, lanes), lambda i: (i, 0, 0)),
+            pl.BlockSpec((block, width, lanes), lambda i: (i, 0, 0)),
+            pl.BlockSpec((3, width, lanes), lambda i: (flows_at, 0, 0)),
+            pl.BlockSpec((3, width, lanes), lambda i: (flows_at, 0, 0)),
+            pl.BlockSpec((rows_out, lanes), lambda i: (0, 0)),
         ],
         out_specs=[
             pl.BlockSpec((block, rows_out, lanes), lambda i: (i, 0, 0)),
@@ -102,7 +138,20 @@
             jax.ShapeDtypeStruct((bins, rows_out, lanes), jnp.float32),
             jax.ShapeDtypeStruct((3, rows_out, lanes), jnp.float32),
         ],
-    )(speeds, weights, extended, extended)
+        scratch_shapes=[
+            pltpu.VMEM((block, rows_out + 2 * width, lanes), jnp.float32),
+            pltpu.VMEM((3, rows_out + 2 * width, lanes), jnp.float32),
+        ],
+    )(speeds, weights, spectrum, flow_fields, before, after, before, after, factor)
+
+
+def halo_pieces(x, axis, dim, width):
+    size, length = (lax.axis_size(axis), x.shape[dim])
+    up = [(i, (i + 1) % size) for i in range(size - 1)]
+    down = [(j, i) for i, j in up]
+    last = lax.slice_in_dim(x, length - width, length, axis=dim)
+    leading = lax.slice_in_dim(x, 0, width, axis=dim)
+    return lax.ppermute(last, axis, up), lax.ppermute(leading, axis, down)
 
 def pick_matmul(values, pick):
     parts = []
@@ -160,7 +209,7 @@
     at_cells = pick_matmul(returned.reshape(3, tile_count * capacity), cell_pick)
     sea_float = sea_mask.astype(jnp.float32)
     flow_fields = jnp.concatenate([at_cells[:2].reshape(2, row_count, columns), sea_float[None]], 0)
-    extended = with_halo(jnp.concatenate([spectrum, flow_fields], 0), (("tile", 1),), STEPS)
+    before, after = halo_pieces(jnp.concatenate([spectrum, flow_fields], 0), "tile", 1, STEPS)
     speeds = jnp.stack([group_speed * cos_dir, group_speed * sin_dir], 0)
     weights = jnp.stack(
         [
@@ -170,9 +219,11 @@
         ],
         0,
     ) * (4.0 / (NDIR * NFREQ))
-    energy, partial_value = propagate(speeds, weights, extended, bin_count, row_count)
+    factor = ((1.0 + at_cells[2]) * sea_float.reshape(-1)).reshape(row_count, columns)
+    energy, partial_value = propagate(
+        speeds, weights, spectrum, flow_fields, before, after, factor
+    )
     partial_value = partial_value.reshape(3, cell_count)
-    partial_value = partial_value * ((1.0 + at_cells[2]) * sea_float.reshape(-1))
     sect_count = lax.axis_size("sect")
     every_part = lax.all_to_all(
         jnp.broadcast_to(partial_value[None], (sect_count,) + partial_value.shape),

time: 139 us -> 136 us (0.978)
  starting transfers between devices: 50.5 us -> 47.3 us
  local copies, waits for them, and re-layouts: 4.54 us -> 6 us
    all_to_all x1, starting transfers between devices: 12 us -> 8.82 us  [local(): lax.all_to_all(packed.reshape(3, tile_count, capacity), 'tile', split_axi...]
    unnamed x4 -> x11, local copies, waits for them, and re-layouts: 0.01 us -> 1.48 us
  transfers between devices with their start and end apart: 6 -> 6, of which waited for: 6 -> 6; matrix products, arithmetic and copies ran while one was open for 3% -> 4% of each run, Pallas kernels for 0% -> 0%
where the time goes in v13:
time: 136 us; the launch traced here: 135 us
  waiting for transfers between devices  53.5 us (39%)
  starting transfers between devices  47.3 us (35%)
  other arithmetic  10.8 us (8%)
  matrix products  9.46 us (7%)
  Pallas kernels  7.4 us (5%)
  local copies, waits for them, and re-layouts  6 us (4%)
    all_to_all x1, starting transfers between devices, local(): lax.all_to_all(requests.reshape(tile_count, capacity), 'tile', split_axis...  21.8 us
    all_to_all x1, waiting for transfers between devices, local(): lax.all_to_all(packed.reshape(3, tile_count, capacity), 'tile', split_axi...  16.8 us
    all_to_all x1, waiting for transfers between devices, local(): lax.all_to_all(answer, 'tile', split_axis=1, concat_axis=1, tiled=True)  15.7 us
    all_to_all x1, waiting for transfers between devices, local(): lax.all_to_all(requests.reshape(tile_count, capacity), 'tile', split_axis...  9.96 us
    dot_general x4, matrix products, pick_matmul(): product = jnp.dot(stacked, pick, preferred_element_type=jnp.float32)  9.46 us
    all_to_all x1, starting transfers between devices, local(): lax.all_to_all(packed.reshape(3, tile_count, capacity), 'tile', split_axi...  8.82 us
    pallas_call x1, Pallas kernels, propagate(): pl.pallas_call(kernel, grid=(bins // block,), in_specs=[pl.BlockSpec(memo...  7.4 us
    all_to_all x1, starting transfers between devices, local(): lax.all_to_all(answer, 'tile', split_axis=1, concat_axis=1, tiled=True)  6.35 us
  transfers between devices with their start and end apart: 6, of which 6 were waited for; matrix products, arithmetic and copies ran while one was open for 4% of the time, Pallas kernels for 0%

profile of v13, /device:TPU:8, one launch (start us, length us, event | category | flops | bytes accessed | tf_op | source)
XLA Modules:
  0.0 135.3 jit_solution(8247649404496343559)
XLA Ops:
  0.6 1.3 convert_reduce_fusion
  1.9 0.7 multiply_add_fusion.1
  2.6 0.7 broadcast_add_fusion.1
  3.3 1.0 select_reduce_fusion
  4.3 0.8 sub.48
  5.0 21.8 %all-to-all-start = ((s32[96,1,22]{2,1,0:T(1,128)}), s32[96,1,22]{2,1,0:T(1,128)S(1)}, u32[]{:S(2)}, u32[]{:S(2)}) async-start(s32[96,1,22]{2,1,0:T(1,128)} %bitcast.6), calls=%async_computation | async-start | bytes 98304 | tf_op jit(solution)/shard_map/all_to_all | solution.py:199
  26.8 0.7 multiply_add_fusion
  27.5 0.7 convert_bitcast_fusion
  28.2 0.8 select_reduce_fusion.1
  29.0 0.8 reduce-precision_convert_fusion.5
  30.4 10.0 %all-to-all-done = s32[96,1,22]{2,1,0:T(1,128)S(1)} async-done(((s32[96,1,22]{2,1,0:T(1,128)}), s32[96,1,22]{2,1,0:T(1,128)S(1)}, u32[]{:S(2)}, u32[]{:S(2)}) %all-to-all-start) | async-done | bytes 8480 | tf_op jit(solution)/shard_map/all_to_all | solution.py:199
  40.9 0.8 reduce.7
  41.8 3.2 %fusion.1 = f32[9,2112]{1,0:T(8,128)S(1)} fusion(s32[2112]{0:T(1024)S(1)} %eq.85, bf16[3,2048]{1,0:T(4,128)(2,1)S(1)} %get-tuple-element.19, bf16[3,2048]{1,0:T(4,128)(2,1)S(1)} %get-tuple-element.20, bf16[3,2048]{1,0:T(4,128)(2,1)S(1)} %get-tuple-element.18), kind=kOutput, calls=%fused_computation.2 | convolution fusion | flops 82292736 | bytes 121344 | tf_op jit(solution)/shard_map/dot_general | solution.py:166
  45.2 0.8 copy.16
  46.0 6.3 %all-to-all-start.1 = ((f32[3,96,22]{2,0,1:T(4,128)}), f32[3,96,22]{2,0,1:T(4,128)S(1)}, u32[]{:S(2)}, u32[]{:S(2)}) async-start(f32[3,96,22]{2,0,1:T(4,128)} %copy.16), calls=%async_computation.1 | async-start | bytes 393216 | tf_op jit(solution)/shard_map/all_to_all | solution.py:207
  52.9 15.7 %all-to-all-done.1 = f32[3,96,22]{2,0,1:T(4,128)S(1)} async-done(((f32[3,96,22]{2,0,1:T(4,128)}), f32[3,96,22]{2,0,1:T(4,128)S(1)}, u32[]{:S(2)}, u32[]{:S(2)}) %all-to-all-start.1) | async-done | bytes 25376 | tf_op jit(solution)/shard_map/all_to_all | solution.py:207
  68.8 1.6 %fusion.5 = f32[9,1024]{1,0:T(8,128)S(1)} fusion(s32[1024]{0:T(1024)S(1)} %multiply_add_fusion, bf16[3,2112]{1,0:T(4,128)(2,1)S(1)} %get-tuple-element.16, bf16[3,2112]{1,0:T(4,128)(2,1)S(1)} %get-tuple-element.17, bf16[3,2112]{1,0:T(4,128)(2,1)S(1)} %get-tuple-element.15), kind=kOutput, calls=%fused_computation.7 | convolution fusion | flops 41205120 | bytes 78976 | tf_op jit(solution)/shard_map/dot_general | solution.py:166
  70.6 3.1 %collective-permute-start.1 = (f32[165,4,128]{2,1,0:T(4,128)S(1)}, f32[165,4,128]{2,1,0:T(4,128)S(1)}, u32[]{:S(2)}, u32[]{:S(2)}) collective-permute-start(f32[165,4,128]{2,1,0:T(4,128)S(1)} %get-tuple-element.10), channel_id=1, source_target_pairs={{1,0},{2,1},{3,2},{4,3},{5,4},{6,5},{7,6},{8,7},{9,8},{10,9},{11,1... | collective-permute-start | bytes 1013768 | tf_op jit(solution)/shard_map/ppermute | solution.py:154
  73.7 2.9 %collective-permute-start = (f32[165,4,128]{2,1,0:T(4,128)S(1)}, f32[165,4,128]{2,1,0:T(4,128)S(1)}, u32[]{:S(2)}, u32[]{:S(2)}) collective-permute-start(f32[165,4,128]{2,1,0:T(4,128)S(1)} %get-tuple-element.11), channel_id=1, source_target_pairs={{0,1},{1,2},{2,3},{3,4},{4,5},{5,6},{6,7},{7,8},{8,9},{9,10},{10,1... | collective-permute-start | bytes 1013768 | tf_op jit(solution)/shard_map/ppermute | solution.py:154
  77.8 1.8 %collective-permute-done.1.after_ref.flow_after_ref = f32[165,4,128]{2,1,0:T(4,128)S(1)} collective-permute-done((f32[165,4,128]{2,1,0:T(4,128)S(1)}, f32[165,4,128]{2,1,0:T(4,128)S(1)}, u32[]{:S(2)}, u32[]{:S(2)}) %collective-permute-start.1) | collective-permute-done | bytes 337952 | tf_op jit(solution)/shard_map/ppermute | solution.py:154
  79.6 3.1 %collective-permute-done.before_ref.flow_before_ref = f32[165,4,128]{2,1,0:T(4,128)S(1)} collective-permute-done((f32[165,4,128]{2,1,0:T(4,128)S(1)}, f32[165,4,128]{2,1,0:T(4,128)S(1)}, u32[]{:S(2)}, u32[]{:S(2)}) %collective-permute-start) | collective-permute-done | bytes 337952 | tf_op jit(solution)/shard_map/ppermute | solution.py:154
  82.8 0.7 copy-done.2
  83.5 7.4 %shard_map.95 = (f32[162,8,128]{2,1,0:T(8,128)}, f32[3,8,128]{2,1,0:T(8,128)}) custom-call(f32[2,162]{1,0:T(2,128)} %pad_maximum_fusion.4.speed_ref, f32[3,162]{1,0:T(4,128)} %maximum_multiply_fusion.weight_ref, f32[162,8,128]{2,1,0:T(8,128)} %energy_ref.1, f32[3,8,128]{2,1,0:T(8,128)} %pad_maximum_fusion.3.flow_ref, f32[165,4,128]{2,1,0:T(4,128)} %copy-done.2, ...), custom_call_target="tpu_custom_call" | custom-call | tf_op jit(solution)/shard_map/pallas_call | solution.py:119
  90.9 0.7 copy.24
  91.6 0.7 broadcast_in_dim.25
  92.3 4.3 %all-to-all-start.2 = ((f32[8,3,1024]{2,1,0:T(4,128)}), f32[8,3,1024]{2,1,0:T(4,128)S(1)}, u32[]{:S(2)}, u32[]{:S(2)}) async-start(f32[8,3,1024]{2,1,0:T(4,128)} %broadcast_in_dim.25), calls=%async_computation.2 | async-start | bytes 262144 | tf_op jit(solution)/shard_map/all_to_all | solution.py:228
  96.6 6.1 %all-to-all-done.2 = f32[8,3,1024]{2,1,0:T(4,128)S(1)} async-done(((f32[8,3,1024]{2,1,0:T(4,128)}), f32[8,3,1024]{2,1,0:T(4,128)S(1)}, u32[]{:S(2)}, u32[]{:S(2)}) %all-to-all-start.2) | async-done | bytes 98336 | tf_op jit(solution)/shard_map/all_to_all | solution.py:228
  102.8 1.5 %fusion.4 = f32[9,2112]{1,0:T(8,128)S(1)} fusion(s32[1024]{0:T(1024)S(1)} %multiply_add_fusion, bf16[3,1024]{1,0:T(4,128)(2,1)S(1)} %get-tuple-element.22, bf16[3,1024]{1,0:T(4,128)(2,1)S(1)} %get-tuple-element.21, bf16[3,1024]{1,0:T(4,128)(2,1)S(1)} %get-tuple-element.8), kind=kOutput, calls=%fused_computation.6 | convolution fusion | flops 41146368 | bytes 98560 | tf_op jit(solution)/shard_map/dot_general | solution.py:166
  104.5 0.8 copy.18
  105.3 8.8 %all-to-all-start.3 = ((f32[3,96,22]{2,0,1:T(4,128)}), f32[3,96,22]{2,0,1:T(4,128)S(1)}, u32[]{:S(2)}, u32[]{:S(2)}) async-start(f32[3,96,22]{2,0,1:T(4,128)} %copy.18), calls=%async_computation.3 | async-start | bytes 393216 | tf_op jit(solution)/shard_map/all_to_all | solution.py:239
  114.4 16.8 %all-to-all-done.3 = f32[3,96,22]{2,0,1:T(4,128)S(1)} async-done(((f32[3,96,22]{2,0,1:T(4,128)}), f32[3,96,22]{2,0,1:T(4,128)S(1)}, u32[]{:S(2)}, u32[]{:S(2)}) %all-to-all-start.3) | async-done | bytes 25376 | tf_op jit(solution)/shard_map/all_to_all | solution.py:239
  131.4 3.2 %fusion = f32[12,2048]{1,0:T(8,128)S(1)} fusion(s32[2112]{0:T(1024)S(1)} %eq.85, bf16[4,2112]{1,0:T(4,128)(2,1)S(1)} %get-tuple-element.14, bf16[4,2112]{1,0:T(4,128)(2,1)S(1)} %get-tuple-element.13, bf16[4,2112]{1,0:T(4,128)(2,1)S(1)} %get-tuple-element.12), kind=kOutput, calls=%fused_computation.1 | convolution fusion | flops 108286464 | bytes 157440 | tf_op jit(solution)/shard_map/dot_general | solution.py:166
  (41 shorter events, 5.1 us)
Async XLA Ops:
  5.0 35.4 %all-to-all-start = ((s32[96,1,22]{2,1,0:T(1,128)}), s32[96,1,22]{2,1,0:T(1,128)S(1)}, u32[]{:S(2)}, u32[]{:S(2)}) async-start(s32[96,1,22]{2,1,0:T(1,128)} %bitcast.6), calls=%async_computation | async-start | bytes 98304 | tf_op jit(solution)/shard_map/all_to_all | solution.py:199
  46.0 22.6 %all-to-all-start.1 = ((f32[3,96,22]{2,0,1:T(4,128)}), f32[3,96,22]{2,0,1:T(4,128)S(1)}, u32[]{:S(2)}, u32[]{:S(2)}) async-start(f32[3,96,22]{2,0,1:T(4,128)} %copy.16), calls=%async_computation.1 | async-start | bytes 393216 | tf_op jit(solution)/shard_map/all_to_all | solution.py:207
  68.8 1.6 %copy-start = (f32[162,8,128]{2,1,0:T(8,128)S(1)}, f32[162,8,128]{2,1,0:T(8,128)}, u32[]{:S(2)}) copy-start(f32[162,8,128]{2,1,0:T(8,128)} %energy_ref.1) | copy-start | bytes 1990660
  70.4 6.8 %copy-start.3 = (s32[8,128]{1,0:T(8,128)S(1)}, s32[8,128]{1,0:T(8,128)}, u32[]{:S(2)}) copy-start(s32[8,128]{1,0:T(8,128)} %param.13) | copy-start | bytes 12292
  70.6 9.1 %collective-permute-start.1 = (f32[165,4,128]{2,1,0:T(4,128)S(1)}, f32[165,4,128]{2,1,0:T(4,128)S(1)}, u32[]{:S(2)}, u32[]{:S(2)}) collective-permute-start(f32[165,4,128]{2,1,0:T(4,128)S(1)} %get-tuple-element.10), channel_id=1, source_target_pairs={{1,0},{2,1},{3,2},{4,3},{5,4},{6,5},{7,6},{8,7},{9,8},{10,9},{11,1... | collective-permute-start | bytes 1013768 | tf_op jit(solution)/shard_map/ppermute | solution.py:154
  73.7 9.1 %collective-permute-start = (f32[165,4,128]{2,1,0:T(4,128)S(1)}, f32[165,4,128]{2,1,0:T(4,128)S(1)}, u32[]{:S(2)}, u32[]{:S(2)}) collective-permute-start(f32[165,4,128]{2,1,0:T(4,128)S(1)} %get-tuple-element.11), channel_id=1, source_target_pairs={{0,1},{1,2},{2,3},{3,4},{4,5},{5,6},{6,7},{7,8},{8,9},{9,10},{10,1... | collective-permute-start | bytes 1013768 | tf_op jit(solution)/shard_map/ppermute | solution.py:154
  79.6 3.1 %copy-start.1 = (f32[165,4,128]{2,1,0:T(4,128)}, f32[165,4,128]{2,1,0:T(4,128)S(1)}, u32[]{:S(2)}) copy-start(f32[165,4,128]{2,1,0:T(4,128)S(1)} %collective-permute-done.1.after_ref.flow_after_ref) | copy-start | bytes 1013764
  82.8 0.7 copy-start.2
  92.3 10.4 %all-to-all-start.2 = ((f32[8,3,1024]{2,1,0:T(4,128)}), f32[8,3,1024]{2,1,0:T(4,128)S(1)}, u32[]{:S(2)}, u32[]{:S(2)}) async-start(f32[8,3,1024]{2,1,0:T(4,128)} %broadcast_in_dim.25), calls=%async_computation.2 | async-start | bytes 262144 | tf_op jit(solution)/shard_map/all_to_all | solution.py:228
  105.3 25.9 %all-to-all-start.3 = ((f32[3,96,22]{2,0,1:T(4,128)}), f32[3,96,22]{2,0,1:T(4,128)S(1)}, u32[]{:S(2)}, u32[]{:S(2)}) async-start(f32[3,96,22]{2,0,1:T(4,128)} %copy.18), calls=%async_computation.3 | async-start | bytes 393216 | tf_op jit(solution)/shard_map/all_to_all | solution.py:239

commit v14 on v13

--- a/solution.py
+++ b/solution.py
@@ -67,7 +67,7 @@
 
     @pl.when(pl.program_id(0) == 0)
     def _():
-        stress_ref[...] = jnp.zeros(stress_ref.shape, jnp.float32)
+        stress_ref[0] = jnp.zeros(stress_ref.shape[1:], jnp.float32)
 
     flow_window_ref[:, :rows_out] = flow_ref[...]
     flow_window_ref[:, rows_out : rows_out + width] = flow_after_ref[...]
@@ -102,15 +102,17 @@
     zero = jnp.zeros((rows_out, lanes), jnp.float32)
     sums = lax.fori_loop(0, block, one_bin, (zero, zero, zero), unroll=True)
     for k in range(3):
-        stress_ref[k] = stress_ref[k] + sums[k]
+        stress_ref[0, k] = stress_ref[0, k] + sums[k]
 
     @pl.when(pl.program_id(0) == pl.num_programs(0) - 1)
     def _():
         for k in range(3):
-            stress_ref[k] = stress_ref[k] * factor_ref[...]
-
-
-def propagate(speeds, weights, spectrum, flow_fields, before, after, factor):
+            scaled = stress_ref[0, k] * factor_ref[...]
+            for copy in range(stress_ref.shape[0]):
+                stress_ref[copy, k] = scaled
+
+
+def propagate(speeds, weights, spectrum, flow_fields, before, after, factor, copies):
     bins, rows_out, lanes = spectrum.shape
     width = before.shape[1]
     block = max(d for d in range(1, 33) if bins % d == 0)
@@ -132,11 +134,11 @@
         ],
         out_specs=[
             pl.BlockSpec((block, rows_out, lanes), lambda i: (i, 0, 0)),
-            pl.BlockSpec((3, rows_out, lanes), lambda i: (0, 0, 0)),
+            pl.BlockSpec((copies, 3, rows_out, lanes), lambda i: (0, 0, 0, 0)),
         ],
         out_shape=[
             jax.ShapeDtypeStruct((bins, rows_out, lanes), jnp.float32),
-            jax.ShapeDtypeStruct((3, rows_out, lanes), jnp.float32),
+            jax.ShapeDtypeStruct((copies, 3, rows_out, lanes), jnp.float32),
         ],
         scratch_shapes=[
             pltpu.VMEM((block, rows_out + 2 * width, lanes), jnp.float32),
@@ -220,21 +222,15 @@
         0,
     ) * (4.0 / (NDIR * NFREQ))
     factor = ((1.0 + at_cells[2]) * sea_float.reshape(-1)).reshape(row_count, columns)
-    energy, partial_value = propagate(
-        speeds, weights, spectrum, flow_fields, before, after, factor
-    )
-    partial_value = partial_value.reshape(3, cell_count)
     sect_count = lax.axis_size("sect")
-    every_part = lax.all_to_all(
-        jnp.broadcast_to(partial_value[None], (sect_count,) + partial_value.shape),
-        "sect",
-        0,
-        0,
-        tiled=True,
-    )
+    energy, partial_copies = propagate(
+        speeds, weights, spectrum, flow_fields, before, after, factor, sect_count
+    )
+    every_part = lax.all_to_all(partial_copies, "sect", 0, 0, tiled=True)
     partial_value = every_part[0]
     for part in range(1, sect_count):
         partial_value = partial_value + every_part[part]
+    partial_value = partial_value.reshape(3, cell_count)
     packed = pick_matmul(partial_value, cell_pick.T)
     arrived = lax.all_to_all(
         packed.reshape(3, tile_count, capacity), "tile", split_axis=1, concat_axis=1, tiled=True

time: 136 us -> 134 us (0.985)
  local copies, waits for them, and re-layouts: 6 us -> 4.62 us
where the time goes in v14:
time: 134 us
  waiting for transfers between devices  53.2 us (40%)
  starting transfers between devices  47.3 us (35%)
  other arithmetic  10.8 us (8%)
  matrix products  9.47 us (7%)
  Pallas kernels  7.44 us (6%)
  local copies, waits for them, and re-layouts  4.62 us (3%)
    all_to_all x1, starting transfers between devices, local(): lax.all_to_all(requests.reshape(tile_count, capacity), 'tile', split_axis...  21.8 us
    all_to_all x1, waiting for transfers between devices, local(): lax.all_to_all(packed.reshape(3, tile_count, capacity), 'tile', split_axi...  16.9 us
    all_to_all x1, waiting for transfers between devices, local(): lax.all_to_all(answer, 'tile', split_axis=1, concat_axis=1, tiled=True)  15.6 us
    all_to_all x1, waiting for transfers between devices, local(): lax.all_to_all(requests.reshape(tile_count, capacity), 'tile', split_axis...  9.96 us
    dot_general x4, matrix products, pick_matmul(): product = jnp.dot(stacked, pick, preferred_element_type=jnp.float32)  9.47 us
    all_to_all x1, starting transfers between devices, local(): lax.all_to_all(packed.reshape(3, tile_count, capacity), 'tile', split_axi...  8.82 us
    pallas_call x1, Pallas kernels, propagate(): pl.pallas_call(kernel, grid=(bins // block,), in_specs=[pl.BlockSpec(memo...  7.44 us
    all_to_all x1, starting transfers between devices, local(): lax.all_to_all(answer, 'tile', split_axis=1, concat_axis=1, tiled=True)  6.35 us
  transfers between devices with their start and end apart: 6, of which 6 were waited for; matrix products, arithmetic and copies ran while one was open for 4% of the time, Pallas kernels for 0%

profile of v14, /device:TPU:8, one launch (start us, length us, event | category | flops | bytes accessed | tf_op | source)
XLA Modules:
  0.0 133.7 jit_solution(11535321164500729521)
XLA Ops:
  0.6 1.3 convert_reduce_fusion
  1.9 0.7 multiply_add_fusion.1
  2.6 0.7 broadcast_add_fusion.1
  3.3 1.0 select_reduce_fusion
  4.3 0.8 sub.48
  5.0 21.8 %all-to-all-start = ((s32[96,1,22]{2,1,0:T(1,128)}), s32[96,1,22]{2,1,0:T(1,128)S(1)}, u32[]{:S(2)}, u32[]{:S(2)}) async-start(s32[96,1,22]{2,1,0:T(1,128)} %bitcast.6), calls=%async_computation | async-start | bytes 98304 | tf_op jit(solution)/shard_map/all_to_all | solution.py:201
  26.8 0.7 multiply_add_fusion
  27.5 0.7 convert_bitcast_fusion
  28.2 0.8 select_reduce_fusion.1
  29.0 0.8 reduce-precision_convert_fusion.5
  29.8 0.6 maximum_multiply_fusion.weight_ref
  30.4 10.0 %all-to-all-done = s32[96,1,22]{2,1,0:T(1,128)S(1)} async-done(((s32[96,1,22]{2,1,0:T(1,128)}), s32[96,1,22]{2,1,0:T(1,128)S(1)}, u32[]{:S(2)}, u32[]{:S(2)}) %all-to-all-start) | async-done | bytes 8480 | tf_op jit(solution)/shard_map/all_to_all | solution.py:201
  40.9 0.8 reduce.7
  41.8 3.2 %fusion.1 = f32[9,2112]{1,0:T(8,128)S(1)} fusion(s32[2112]{0:T(1024)S(1)} %eq.85, bf16[3,2048]{1,0:T(4,128)(2,1)S(1)} %get-tuple-element.17, bf16[3,2048]{1,0:T(4,128)(2,1)S(1)} %get-tuple-element.18, bf16[3,2048]{1,0:T(4,128)(2,1)S(1)} %get-tuple-element.16), kind=kOutput, calls=%fused_computation.2 | convolution fusion | flops 82292736 | bytes 121344 | tf_op jit(solution)/shard_map/dot_general | solution.py:168
  45.2 0.8 copy.16
  46.0 6.3 %all-to-all-start.1 = ((f32[3,96,22]{2,0,1:T(4,128)}), f32[3,96,22]{2,0,1:T(4,128)S(1)}, u32[]{:S(2)}, u32[]{:S(2)}) async-start(f32[3,96,22]{2,0,1:T(4,128)} %copy.16), calls=%async_computation.1 | async-start | bytes 393216 | tf_op jit(solution)/shard_map/all_to_all | solution.py:209
  52.9 15.6 %all-to-all-done.1 = f32[3,96,22]{2,0,1:T(4,128)S(1)} async-done(((f32[3,96,22]{2,0,1:T(4,128)}), f32[3,96,22]{2,0,1:T(4,128)S(1)}, u32[]{:S(2)}, u32[]{:S(2)}) %all-to-all-start.1) | async-done | bytes 25376 | tf_op jit(solution)/shard_map/all_to_all | solution.py:209
  68.8 1.6 %fusion.5 = f32[9,1024]{1,0:T(8,128)S(1)} fusion(s32[1024]{0:T(1024)S(1)} %multiply_add_fusion, bf16[3,2112]{1,0:T(4,128)(2,1)S(1)} %get-tuple-element.14, bf16[3,2112]{1,0:T(4,128)(2,1)S(1)} %get-tuple-element.15, bf16[3,2112]{1,0:T(4,128)(2,1)S(1)} %get-tuple-element.13), kind=kOutput, calls=%fused_computation.7 | convolution fusion | flops 41205120 | bytes 78976 | tf_op jit(solution)/shard_map/dot_general | solution.py:168
  70.6 3.1 %collective-permute-start.1 = (f32[165,4,128]{2,1,0:T(4,128)S(1)}, f32[165,4,128]{2,1,0:T(4,128)S(1)}, u32[]{:S(2)}, u32[]{:S(2)}) collective-permute-start(f32[165,4,128]{2,1,0:T(4,128)S(1)} %get-tuple-element.8), channel_id=1, source_target_pairs={{1,0},{2,1},{3,2},{4,3},{5,4},{6,5},{7,6},{8,7},{9,8},{10,9},{11,1... | collective-permute-start | bytes 1013768 | tf_op jit(solution)/shard_map/ppermute | solution.py:156
  73.7 2.9 %collective-permute-start = (f32[165,4,128]{2,1,0:T(4,128)S(1)}, f32[165,4,128]{2,1,0:T(4,128)S(1)}, u32[]{:S(2)}, u32[]{:S(2)}) collective-permute-start(f32[165,4,128]{2,1,0:T(4,128)S(1)} %get-tuple-element.9), channel_id=1, source_target_pairs={{0,1},{1,2},{2,3},{3,4},{4,5},{5,6},{6,7},{7,8},{8,9},{9,10},{10,1... | collective-permute-start | bytes 1013768 | tf_op jit(solution)/shard_map/ppermute | solution.py:156
  77.8 1.8 %collective-permute-done.1.after_ref.flow_after_ref = f32[165,4,128]{2,1,0:T(4,128)S(1)} collective-permute-done((f32[165,4,128]{2,1,0:T(4,128)S(1)}, f32[165,4,128]{2,1,0:T(4,128)S(1)}, u32[]{:S(2)}, u32[]{:S(2)}) %collective-permute-start.1) | collective-permute-done | bytes 337952 | tf_op jit(solution)/shard_map/ppermute | solution.py:156
  79.6 3.1 %collective-permute-done.before_ref.flow_before_ref = f32[165,4,128]{2,1,0:T(4,128)S(1)} collective-permute-done((f32[165,4,128]{2,1,0:T(4,128)S(1)}, f32[165,4,128]{2,1,0:T(4,128)S(1)}, u32[]{:S(2)}, u32[]{:S(2)}) %collective-permute-start) | collective-permute-done | bytes 337952 | tf_op jit(solution)/shard_map/ppermute | solution.py:156
  82.8 0.7 copy-done.2
  83.5 7.4 %shard_map.95 = (f32[162,8,128]{2,1,0:T(8,128)}, f32[8,3,8,128]{3,2,1,0:T(8,128)}) custom-call(f32[2,162]{1,0:T(2,128)} %pad_maximum_fusion.4.speed_ref, f32[3,162]{1,0:T(4,128)} %maximum_multiply_fusion.weight_ref, f32[162,8,128]{2,1,0:T(8,128)} %energy_ref.1, f32[3,8,128]{2,1,0:T(8,128)} %pad_maximum_fusion.3.flow_ref, f32[165,4,128]{2,1,0:T(4,128)} %copy-done.2, ...), custom_call_target="tpu_custom_call" | custom-call | tf_op jit(solution)/shard_map/pallas_call | solution.py:121
  90.9 4.3 %all-to-all-start.2 = ((f32[8,3,8,128]{3,2,1,0:T(8,128)}), f32[8,3,8,128]{3,2,1,0:T(8,128)S(1)}, u32[]{:S(2)}, u32[]{:S(2)}) async-start(f32[8,3,8,128]{3,2,1,0:T(8,128)} %get-tuple-element.5), calls=%async_computation.2 | async-start | bytes 196608 | tf_op jit(solution)/shard_map/all_to_all | solution.py:229
  95.3 5.8 %all-to-all-done.2 = f32[8,3,8,128]{3,2,1,0:T(8,128)S(1)} async-done(((f32[8,3,8,128]{3,2,1,0:T(8,128)}), f32[8,3,8,128]{3,2,1,0:T(8,128)S(1)}, u32[]{:S(2)}, u32[]{:S(2)}) %all-to-all-start.2) | async-done | bytes 98336 | tf_op jit(solution)/shard_map/all_to_all | solution.py:229
  101.1 1.5 %fusion.4 = f32[9,2112]{1,0:T(8,128)S(1)} fusion(s32[1024]{0:T(1024)S(1)} %multiply_add_fusion, bf16[3,1024]{1,0:T(4,128)(2,1)S(1)} %get-tuple-element.20, bf16[3,1024]{1,0:T(4,128)(2,1)S(1)} %get-tuple-element.21, bf16[3,1024]{1,0:T(4,128)(2,1)S(1)} %get-tuple-element.19), kind=kOutput, calls=%fused_computation.6 | convolution fusion | flops 41146368 | bytes 98560 | tf_op jit(solution)/shard_map/dot_general | solution.py:168
  102.8 0.8 copy.18
  103.6 8.8 %all-to-all-start.3 = ((f32[3,96,22]{2,0,1:T(4,128)}), f32[3,96,22]{2,0,1:T(4,128)S(1)}, u32[]{:S(2)}, u32[]{:S(2)}) async-start(f32[3,96,22]{2,0,1:T(4,128)} %copy.18), calls=%async_computation.3 | async-start | bytes 393216 | tf_op jit(solution)/shard_map/all_to_all | solution.py:235
  112.7 16.9 %all-to-all-done.3 = f32[3,96,22]{2,0,1:T(4,128)S(1)} async-done(((f32[3,96,22]{2,0,1:T(4,128)}), f32[3,96,22]{2,0,1:T(4,128)S(1)}, u32[]{:S(2)}, u32[]{:S(2)}) %all-to-all-start.3) | async-done | bytes 25376 | tf_op jit(solution)/shard_map/all_to_all | solution.py:235
  129.8 3.2 %fusion = f32[12,2048]{1,0:T(8,128)S(1)} fusion(s32[2112]{0:T(1024)S(1)} %eq.85, bf16[4,2112]{1,0:T(4,128)(2,1)S(1)} %get-tuple-element.12, bf16[4,2112]{1,0:T(4,128)(2,1)S(1)} %get-tuple-element.11, bf16[4,2112]{1,0:T(4,128)(2,1)S(1)} %get-tuple-element.10), kind=kOutput, calls=%fused_computation.1 | convolution fusion | flops 108286464 | bytes 157440 | tf_op jit(solution)/shard_map/dot_general | solution.py:168
  133.1 0.6 slice_divide_fusion
  (39 shorter events, 3.8 us)
Async XLA Ops:
  5.0 35.4 %all-to-all-start = ((s32[96,1,22]{2,1,0:T(1,128)}), s32[96,1,22]{2,1,0:T(1,128)S(1)}, u32[]{:S(2)}, u32[]{:S(2)}) async-start(s32[96,1,22]{2,1,0:T(1,128)} %bitcast.6), calls=%async_computation | async-start | bytes 98304 | tf_op jit(solution)/shard_map/all_to_all | solution.py:201
  46.0 22.6 %all-to-all-start.1 = ((f32[3,96,22]{2,0,1:T(4,128)}), f32[3,96,22]{2,0,1:T(4,128)S(1)}, u32[]{:S(2)}, u32[]{:S(2)}) async-start(f32[3,96,22]{2,0,1:T(4,128)} %copy.16), calls=%async_computation.1 | async-start | bytes 393216 | tf_op jit(solution)/shard_map/all_to_all | solution.py:209
  68.8 1.6 %copy-start = (f32[162,8,128]{2,1,0:T(8,128)S(1)}, f32[162,8,128]{2,1,0:T(8,128)}, u32[]{:S(2)}) copy-start(f32[162,8,128]{2,1,0:T(8,128)} %energy_ref.1) | copy-start | bytes 1990660
  70.4 6.8 %copy-start.3 = (s32[8,128]{1,0:T(8,128)S(1)}, s32[8,128]{1,0:T(8,128)}, u32[]{:S(2)}) copy-start(s32[8,128]{1,0:T(8,128)} %param.13) | copy-start | bytes 12292
  70.6 9.1 %collective-permute-start.1 = (f32[165,4,128]{2,1,0:T(4,128)S(1)}, f32[165,4,128]{2,1,0:T(4,128)S(1)}, u32[]{:S(2)}, u32[]{:S(2)}) collective-permute-start(f32[165,4,128]{2,1,0:T(4,128)S(1)} %get-tuple-element.8), channel_id=1, source_target_pairs={{1,0},{2,1},{3,2},{4,3},{5,4},{6,5},{7,6},{8,7},{9,8},{10,9},{11,1... | collective-permute-start | bytes 1013768 | tf_op jit(solution)/shard_map/ppermute | solution.py:156
  73.7 9.1 %collective-permute-start = (f32[165,4,128]{2,1,0:T(4,128)S(1)}, f32[165,4,128]{2,1,0:T(4,128)S(1)}, u32[]{:S(2)}, u32[]{:S(2)}) collective-permute-start(f32[165,4,128]{2,1,0:T(4,128)S(1)} %get-tuple-element.9), channel_id=1, source_target_pairs={{0,1},{1,2},{2,3},{3,4},{4,5},{5,6},{6,7},{7,8},{8,9},{9,10},{10,1... | collective-permute-start | bytes 1013768 | tf_op jit(solution)/shard_map/ppermute | solution.py:156
  79.6 3.1 %copy-start.1 = (f32[165,4,128]{2,1,0:T(4,128)}, f32[165,4,128]{2,1,0:T(4,128)S(1)}, u32[]{:S(2)}) copy-start(f32[165,4,128]{2,1,0:T(4,128)S(1)} %collective-permute-done.1.after_ref.flow_after_ref) | copy-start | bytes 1013764
  82.8 0.7 copy-start.2
  90.9 10.1 %all-to-all-start.2 = ((f32[8,3,8,128]{3,2,1,0:T(8,128)}), f32[8,3,8,128]{3,2,1,0:T(8,128)S(1)}, u32[]{:S(2)}, u32[]{:S(2)}) async-start(f32[8,3,8,128]{3,2,1,0:T(8,128)} %get-tuple-element.5), calls=%async_computation.2 | async-start | bytes 196608 | tf_op jit(solution)/shard_map/all_to_all | solution.py:229
  103.6 26.0 %all-to-all-start.3 = ((f32[3,96,22]{2,0,1:T(4,128)}), f32[3,96,22]{2,0,1:T(4,128)S(1)}, u32[]{:S(2)}, u32[]{:S(2)}) async-start(f32[3,96,22]{2,0,1:T(4,128)} %copy.18), calls=%async_computation.3 | async-start | bytes 393216 | tf_op jit(solution)/shard_map/all_to_all | solution.py:235

commit v15 on v14

--- a/solution.py
+++ b/solution.py
@@ -191,8 +191,10 @@
     sin_dir = jnp.sin(angles)
     owners = owner_tile[:, 0]
     cell_ids = jnp.arange(owners.shape[0], dtype=jnp.int32)
-    same_before = (owners[None, :] == owners[:, None]) & (cell_ids[None, :] < cell_ids[:, None])
-    rank_in = jnp.sum(same_before.astype(jnp.int32), 1)
+    earlier = (cell_ids[None, :] < cell_ids[:, None]).astype(jnp.bfloat16)
+    owner_pick = owners[:, None] == jnp.arange(tile_count, dtype=jnp.int32)[None, :]
+    seen = jnp.dot(earlier, owner_pick.astype(jnp.bfloat16), preferred_element_type=jnp.float32)
+    rank_in = jnp.sum(jnp.where(owner_pick, seen, 0.0), 1).astype(jnp.int32)
     position = owners * capacity + rank_in
     slot_ids = jnp.arange(tile_count * capacity, dtype=jnp.int32)
     requests = (

time: 134 us -> 133 us (level)
  other arithmetic: 10.8 us -> 5.38 us
  waiting for transfers between devices: 53.2 us -> 55.9 us
    all_to_all x1, waiting for transfers between devices: 9.96 us -> 12.7 us  [local(): lax.all_to_all(requests.reshape(tile_count, capacity), 'tile', split_axis...]
    add x2, other arithmetic: 1.39 us -> 0.02 us  [local(): position = owners * capacity + rank_in]
  transfers between devices with their start and end apart: 6 -> 6, of which waited for: 6 -> 6; matrix products, arithmetic and copies ran while one was open for 4% -> 2% of each run, Pallas kernels for 0% -> 0%
where the time goes in v15:
time: 133 us; the launch traced here: 132 us
  waiting for transfers between devices  55.9 us (42%)
  starting transfers between devices  47.3 us (36%)
  matrix products  10.8 us (8%)
  Pallas kernels  7.44 us (6%)
  other arithmetic  5.38 us (4%)
  local copies, waits for them, and re-layouts  4.64 us (3%)
    all_to_all x1, starting transfers between devices, local(): lax.all_to_all(requests.reshape(tile_count, capacity), 'tile', split_axis...  21.8 us
    all_to_all x1, waiting for transfers between devices, local(): lax.all_to_all(packed.reshape(3, tile_count, capacity), 'tile', split_axi...  16.9 us
    all_to_all x1, waiting for transfers between devices, local(): lax.all_to_all(answer, 'tile', split_axis=1, concat_axis=1, tiled=True)  15.6 us
    all_to_all x1, waiting for transfers between devices, local(): lax.all_to_all(requests.reshape(tile_count, capacity), 'tile', split_axis...  12.7 us
    dot_general x4, matrix products, pick_matmul(): product = jnp.dot(stacked, pick, preferred_element_type=jnp.float32)  9.47 us
    all_to_all x1, starting transfers between devices, local(): lax.all_to_all(packed.reshape(3, tile_count, capacity), 'tile', split_axi...  8.82 us
    pallas_call x1, Pallas kernels, propagate(): pl.pallas_call(kernel, grid=(bins // block,), in_specs=[pl.BlockSpec(memo...  7.44 us
    all_to_all x1, starting transfers between devices, local(): lax.all_to_all(answer, 'tile', split_axis=1, concat_axis=1, tiled=True)  6.35 us
  transfers between devices with their start and end apart: 6, of which 6 were waited for; matrix products, arithmetic and copies ran while one was open for 2% of the time, Pallas kernels for 0%

profile of v15, /device:TPU:8, one launch (start us, length us, event | category | flops | bytes accessed | tf_op | source)
XLA Modules:
  0.0 132.5 jit_solution(7396634920352314642)
XLA Ops:
  0.7 1.3 %fusion.10 = f32[1024]{0:T(1024)S(1)} fusion(s32[1024]{0:T(1024)} %bitcast.29), kind=kOutput, calls=%fused_computation.15 | convolution fusion | flops 202767360 | bytes 8192 | tf_op jit(solution)/shard_map/dot_general | solution.py:196
  2.1 1.0 select_reduce_fusion
  3.1 0.8 sub.48
  3.8 21.8 %all-to-all-start = ((s32[96,1,22]{2,1,0:T(1,128)}), s32[96,1,22]{2,1,0:T(1,128)S(1)}, u32[]{:S(2)}, u32[]{:S(2)}) async-start(s32[96,1,22]{2,1,0:T(1,128)} %bitcast.6), calls=%async_computation | async-start | bytes 98304 | tf_op jit(solution)/shard_map/all_to_all | solution.py:203
  25.9 0.6 maximum_multiply_fusion.weight_ref
  26.5 12.7 %all-to-all-done = s32[96,1,22]{2,1,0:T(1,128)S(1)} async-done(((s32[96,1,22]{2,1,0:T(1,128)}), s32[96,1,22]{2,1,0:T(1,128)S(1)}, u32[]{:S(2)}, u32[]{:S(2)}) %all-to-all-start) | async-done | bytes 8480 | tf_op jit(solution)/shard_map/all_to_all | solution.py:203
  39.2 0.5 broadcast.341
  39.7 0.8 reduce.7
  40.6 3.2 %fusion.1 = f32[9,2112]{1,0:T(8,128)S(1)} fusion(s32[2112]{0:T(1024)S(1)} %eq.85, bf16[3,2048]{1,0:T(4,128)(2,1)S(1)} %get-tuple-element.17, bf16[3,2048]{1,0:T(4,128)(2,1)S(1)} %get-tuple-element.18, bf16[3,2048]{1,0:T(4,128)(2,1)S(1)} %get-tuple-element.16), kind=kOutput, calls=%fused_computation.2 | convolution fusion | flops 82292736 | bytes 121344 | tf_op jit(solution)/shard_map/dot_general | solution.py:168
  43.8 0.2 reshape.212
  44.0 0.8 copy.16
  44.8 6.3 %all-to-all-start.1 = ((f32[3,96,22]{2,0,1:T(4,128)}), f32[3,96,22]{2,0,1:T(4,128)S(1)}, u32[]{:S(2)}, u32[]{:S(2)}) async-start(f32[3,96,22]{2,0,1:T(4,128)} %copy.16), calls=%async_computation.1 | async-start | bytes 393216 | tf_op jit(solution)/shard_map/all_to_all | solution.py:211
  51.1 0.6 pad_maximum_fusion.4.speed_ref
  51.7 15.6 %all-to-all-done.1 = f32[3,96,22]{2,0,1:T(4,128)S(1)} async-done(((f32[3,96,22]{2,0,1:T(4,128)}), f32[3,96,22]{2,0,1:T(4,128)S(1)}, u32[]{:S(2)}, u32[]{:S(2)}) %all-to-all-start.1) | async-done | bytes 25376 | tf_op jit(solution)/shard_map/all_to_all | solution.py:211
  67.6 1.6 %fusion.5 = f32[9,1024]{1,0:T(8,128)S(1)} fusion(s32[1024]{0:T(1024)S(1)} %multiply_add_fusion, bf16[3,2112]{1,0:T(4,128)(2,1)S(1)} %get-tuple-element.14, bf16[3,2112]{1,0:T(4,128)(2,1)S(1)} %get-tuple-element.15, bf16[3,2112]{1,0:T(4,128)(2,1)S(1)} %get-tuple-element.13), kind=kOutput, calls=%fused_computation.7 | convolution fusion | flops 41205120 | bytes 78976 | tf_op jit(solution)/shard_map/dot_general | solution.py:168
  69.4 3.1 %collective-permute-start.1 = (f32[165,4,128]{2,1,0:T(4,128)S(1)}, f32[165,4,128]{2,1,0:T(4,128)S(1)}, u32[]{:S(2)}, u32[]{:S(2)}) collective-permute-start(f32[165,4,128]{2,1,0:T(4,128)S(1)} %get-tuple-element.8), channel_id=1, source_target_pairs={{1,0},{2,1},{3,2},{4,3},{5,4},{6,5},{7,6},{8,7},{9,8},{10,9},{11,1... | collective-permute-start | bytes 1013768 | tf_op jit(solution)/shard_map/ppermute | solution.py:156
  72.5 2.9 %collective-permute-start = (f32[165,4,128]{2,1,0:T(4,128)S(1)}, f32[165,4,128]{2,1,0:T(4,128)S(1)}, u32[]{:S(2)}, u32[]{:S(2)}) collective-permute-start(f32[165,4,128]{2,1,0:T(4,128)S(1)} %get-tuple-element.9), channel_id=1, source_target_pairs={{0,1},{1,2},{2,3},{3,4},{4,5},{5,6},{6,7},{7,8},{8,9},{9,10},{10,1... | collective-permute-start | bytes 1013768 | tf_op jit(solution)/shard_map/ppermute | solution.py:156
  75.4 0.6 pad_maximum_fusion.3.flow_ref
  76.0 0.6 convert_multiply_fusion.factor_ref
  76.6 1.8 %collective-permute-done.1.after_ref.flow_after_ref = f32[165,4,128]{2,1,0:T(4,128)S(1)} collective-permute-done((f32[165,4,128]{2,1,0:T(4,128)S(1)}, f32[165,4,128]{2,1,0:T(4,128)S(1)}, u32[]{:S(2)}, u32[]{:S(2)}) %collective-permute-start.1) | collective-permute-done | bytes 337952 | tf_op jit(solution)/shard_map/ppermute | solution.py:156
  78.4 3.1 %collective-permute-done.before_ref.flow_before_ref = f32[165,4,128]{2,1,0:T(4,128)S(1)} collective-permute-done((f32[165,4,128]{2,1,0:T(4,128)S(1)}, f32[165,4,128]{2,1,0:T(4,128)S(1)}, u32[]{:S(2)}, u32[]{:S(2)}) %collective-permute-start) | collective-permute-done | bytes 337952 | tf_op jit(solution)/shard_map/ppermute | solution.py:156
  81.6 0.7 copy-done.2
  82.3 7.4 %shard_map.95 = (f32[162,8,128]{2,1,0:T(8,128)}, f32[8,3,8,128]{3,2,1,0:T(8,128)}) custom-call(f32[2,162]{1,0:T(2,128)} %pad_maximum_fusion.4.speed_ref, f32[3,162]{1,0:T(4,128)} %maximum_multiply_fusion.weight_ref, f32[162,8,128]{2,1,0:T(8,128)} %energy_ref.1, f32[3,8,128]{2,1,0:T(8,128)} %pad_maximum_fusion.3.flow_ref, f32[165,4,128]{2,1,0:T(4,128)} %copy-done.2, ...), custom_call_target="tpu_custom_call" | custom-call | tf_op jit(solution)/shard_map/pallas_call | solution.py:121
  89.7 4.3 %all-to-all-start.2 = ((f32[8,3,8,128]{3,2,1,0:T(8,128)}), f32[8,3,8,128]{3,2,1,0:T(8,128)S(1)}, u32[]{:S(2)}, u32[]{:S(2)}) async-start(f32[8,3,8,128]{3,2,1,0:T(8,128)} %get-tuple-element.5), calls=%async_computation.2 | async-start | bytes 196608 | tf_op jit(solution)/shard_map/all_to_all | solution.py:231
  94.0 5.8 %all-to-all-done.2 = f32[8,3,8,128]{3,2,1,0:T(8,128)S(1)} async-done(((f32[8,3,8,128]{3,2,1,0:T(8,128)}), f32[8,3,8,128]{3,2,1,0:T(8,128)S(1)}, u32[]{:S(2)}, u32[]{:S(2)}) %all-to-all-start.2) | async-done | bytes 98336 | tf_op jit(solution)/shard_map/all_to_all | solution.py:231
  99.9 1.5 %fusion.4 = f32[9,2112]{1,0:T(8,128)S(1)} fusion(s32[1024]{0:T(1024)S(1)} %multiply_add_fusion, bf16[3,1024]{1,0:T(4,128)(2,1)S(1)} %get-tuple-element.20, bf16[3,1024]{1,0:T(4,128)(2,1)S(1)} %get-tuple-element.21, bf16[3,1024]{1,0:T(4,128)(2,1)S(1)} %get-tuple-element.19), kind=kOutput, calls=%fused_computation.6 | convolution fusion | flops 41146368 | bytes 98560 | tf_op jit(solution)/shard_map/dot_general | solution.py:168
  101.4 0.2 reshape.215
  101.6 0.8 copy.18
  102.4 8.8 %all-to-all-start.3 = ((f32[3,96,22]{2,0,1:T(4,128)}), f32[3,96,22]{2,0,1:T(4,128)S(1)}, u32[]{:S(2)}, u32[]{:S(2)}) async-start(f32[3,96,22]{2,0,1:T(4,128)} %copy.18), calls=%async_computation.3 | async-start | bytes 393216 | tf_op jit(solution)/shard_map/all_to_all | solution.py:237
  111.5 16.9 %all-to-all-done.3 = f32[3,96,22]{2,0,1:T(4,128)S(1)} async-done(((f32[3,96,22]{2,0,1:T(4,128)}), f32[3,96,22]{2,0,1:T(4,128)S(1)}, u32[]{:S(2)}, u32[]{:S(2)}) %all-to-all-start.3) | async-done | bytes 25376 | tf_op jit(solution)/shard_map/all_to_all | solution.py:237
  128.6 3.2 %fusion = f32[12,2048]{1,0:T(8,128)S(1)} fusion(s32[2112]{0:T(1024)S(1)} %eq.85, bf16[4,2112]{1,0:T(4,128)(2,1)S(1)} %get-tuple-element.12, bf16[4,2112]{1,0:T(4,128)(2,1)S(1)} %get-tuple-element.11, bf16[4,2112]{1,0:T(4,128)(2,1)S(1)} %get-tuple-element.10), kind=kOutput, calls=%fused_computation.1 | convolution fusion | flops 108286464 | bytes 157440 | tf_op jit(solution)/shard_map/dot_general | solution.py:168
  131.9 0.6 slice_divide_fusion
  (52 shorter events, 1.4 us)
Async XLA Ops:
  0.6 1.4 %copy-start.3 = (s32[1024,1]{0,1:T(1,128)S(1)}, s32[1024,1]{0,1:T(1,128)}, u32[]{:S(2)}) copy-start(s32[1024,1]{0,1:T(1,128)} %param.14) | copy-start | bytes 12292
  0.6 1.4 %copy-start.7 = (s32[1024]{0:T(1024)S(1)}, s32[1024]{0:T(1024)}, u32[]{:S(2)}) copy-start(s32[1024]{0:T(1024)} %param.15) | copy-start | bytes 12292
  0.7 25.0 %copy-start.4 = (s32[8,128]{1,0:T(8,128)S(1)}, s32[8,128]{1,0:T(8,128)}, u32[]{:S(2)}) copy-start(s32[8,128]{1,0:T(8,128)} %param.13) | copy-start | bytes 12292
  0.7 25.0 %copy-start.8 = (f32[36]{0:T(128)S(1)}, f32[36]{0:T(128)}, u32[]{:S(2)}) copy-start(f32[36]{0:T(128)} %param.10) | copy-start | bytes 436
  0.7 25.0 %copy-start.9 = (f32[36]{0:T(128)S(1)}, f32[36]{0:T(128)}, u32[]{:S(2)}) copy-start(f32[36]{0:T(128)} %param.9) | copy-start | bytes 436
  0.7 25.2 %copy-start.5 = (f32[2,2048]{1,0:T(2,128)S(1)}, f32[2,2048]{1,0:T(2,128)}, u32[]{:S(2)}) copy-start(f32[2,2048]{1,0:T(2,128)} %param.11) | copy-start | bytes 49156
  0.7 25.2 %copy-start.6 = (f32[2048]{0:T(1024)S(1)}, f32[2048]{0:T(1024)}, u32[]{:S(2)}) copy-start(f32[2048]{0:T(1024)} %param.12) | copy-start | bytes 24580
  3.8 35.4 %all-to-all-start = ((s32[96,1,22]{2,1,0:T(1,128)}), s32[96,1,22]{2,1,0:T(1,128)S(1)}, u32[]{:S(2)}, u32[]{:S(2)}) async-start(s32[96,1,22]{2,1,0:T(1,128)} %bitcast.6), calls=%async_computation | async-start | bytes 98304 | tf_op jit(solution)/shard_map/all_to_all | solution.py:203
  44.8 22.6 %all-to-all-start.1 = ((f32[3,96,22]{2,0,1:T(4,128)}), f32[3,96,22]{2,0,1:T(4,128)S(1)}, u32[]{:S(2)}, u32[]{:S(2)}) async-start(f32[3,96,22]{2,0,1:T(4,128)} %copy.16), calls=%async_computation.1 | async-start | bytes 393216 | tf_op jit(solution)/shard_map/all_to_all | solution.py:211
  67.6 1.6 %copy-start = (f32[162,8,128]{2,1,0:T(8,128)S(1)}, f32[162,8,128]{2,1,0:T(8,128)}, u32[]{:S(2)}) copy-start(f32[162,8,128]{2,1,0:T(8,128)} %energy_ref.1) | copy-start | bytes 1990660
  69.4 9.1 %collective-permute-start.1 = (f32[165,4,128]{2,1,0:T(4,128)S(1)}, f32[165,4,128]{2,1,0:T(4,128)S(1)}, u32[]{:S(2)}, u32[]{:S(2)}) collective-permute-start(f32[165,4,128]{2,1,0:T(4,128)S(1)} %get-tuple-element.8), channel_id=1, source_target_pairs={{1,0},{2,1},{3,2},{4,3},{5,4},{6,5},{7,6},{8,7},{9,8},{10,9},{11,1... | collective-permute-start | bytes 1013768 | tf_op jit(solution)/shard_map/ppermute | solution.py:156
  72.5 9.1 %collective-permute-start = (f32[165,4,128]{2,1,0:T(4,128)S(1)}, f32[165,4,128]{2,1,0:T(4,128)S(1)}, u32[]{:S(2)}, u32[]{:S(2)}) collective-permute-start(f32[165,4,128]{2,1,0:T(4,128)S(1)} %get-tuple-element.9), channel_id=1, source_target_pairs={{0,1},{1,2},{2,3},{3,4},{4,5},{5,6},{6,7},{7,8},{8,9},{9,10},{10,1... | collective-permute-start | bytes 1013768 | tf_op jit(solution)/shard_map/ppermute | solution.py:156
  78.4 3.1 %copy-start.1 = (f32[165,4,128]{2,1,0:T(4,128)}, f32[165,4,128]{2,1,0:T(4,128)S(1)}, u32[]{:S(2)}) copy-start(f32[165,4,128]{2,1,0:T(4,128)S(1)} %collective-permute-done.1.after_ref.flow_after_ref) | copy-start | bytes 1013764
  81.6 0.7 copy-start.2
  89.7 10.1 %all-to-all-start.2 = ((f32[8,3,8,128]{3,2,1,0:T(8,128)}), f32[8,3,8,128]{3,2,1,0:T(8,128)S(1)}, u32[]{:S(2)}, u32[]{:S(2)}) async-start(f32[8,3,8,128]{3,2,1,0:T(8,128)} %get-tuple-element.5), calls=%async_computation.2 | async-start | bytes 196608 | tf_op jit(solution)/shard_map/all_to_all | solution.py:231
  102.4 26.0 %all-to-all-start.3 = ((f32[3,96,22]{2,0,1:T(4,128)}), f32[3,96,22]{2,0,1:T(4,128)S(1)}, u32[]{:S(2)}, u32[]{:S(2)}) async-start(f32[3,96,22]{2,0,1:T(4,128)} %copy.18), calls=%async_computation.3 | async-start | bytes 393216 | tf_op jit(solution)/shard_map/all_to_all | solution.py:237

commit v16 on v15

--- a/solution.py
+++ b/solution.py
@@ -197,8 +197,8 @@
     rank_in = jnp.sum(jnp.where(owner_pick, seen, 0.0), 1).astype(jnp.int32)
     position = owners * capacity + rank_in
     slot_ids = jnp.arange(tile_count * capacity, dtype=jnp.int32)
-    requests = (
-        jnp.sum(jnp.where(position[:, None] == slot_ids[None, :], ocean_slot[:, None] + 1, 0), 0) - 1
+    requests = jnp.max(
+        jnp.where(position[:, None] == slot_ids[None, :], ocean_slot[:, None], -1), 0
     )
     asked_slots = lax.all_to_all(
         requests.reshape(tile_count, capacity), "tile", split_axis=0, concat_axis=0, tiled=True

time: 133 us -> 133 us (level)
  no operation moved by 1% of the time
where the time goes in v16:
time: 133 us
  waiting for transfers between devices  55.9 us (42%)
  starting transfers between devices  47.3 us (36%)
  matrix products  10.8 us (8%)
  Pallas kernels  7.44 us (6%)
  other arithmetic  5.65 us (4%)
  local copies, waits for them, and re-layouts  4.64 us (3%)
    all_to_all x1, starting transfers between devices, local(): lax.all_to_all(requests.reshape(tile_count, capacity), 'tile', split_axis...  21.8 us
    all_to_all x1, waiting for transfers between devices, local(): lax.all_to_all(packed.reshape(3, tile_count, capacity), 'tile', split_axi...  16.9 us
    all_to_all x1, waiting for transfers between devices, local(): lax.all_to_all(answer, 'tile', split_axis=1, concat_axis=1, tiled=True)  15.6 us
    all_to_all x1, waiting for transfers between devices, local(): lax.all_to_all(requests.reshape(tile_count, capacity), 'tile', split_axis...  12.7 us
    dot_general x4, matrix products, pick_matmul(): product = jnp.dot(stacked, pick, preferred_element_type=jnp.float32)  9.47 us
    all_to_all x1, starting transfers between devices, local(): lax.all_to_all(packed.reshape(3, tile_count, capacity), 'tile', split_axi...  8.82 us
    pallas_call x1, Pallas kernels, propagate(): pl.pallas_call(kernel, grid=(bins // block,), in_specs=[pl.BlockSpec(memo...  7.44 us
    all_to_all x1, starting transfers between devices, local(): lax.all_to_all(answer, 'tile', split_axis=1, concat_axis=1, tiled=True)  6.35 us
  transfers between devices with their start and end apart: 6, of which 6 were waited for; matrix products, arithmetic and copies ran while one was open for 2% of the time, Pallas kernels for 0%

profile of v16, /device:TPU:8, one launch (start us, length us, event | category | flops | bytes accessed | tf_op | source)
XLA Modules:
  0.0 132.7 jit_solution(14099546351051680097)
XLA Ops:
  0.7 1.3 %fusion.10 = f32[1024]{0:T(1024)S(1)} fusion(s32[1024]{0:T(1024)} %bitcast.29), kind=kOutput, calls=%fused_computation.15 | convolution fusion | flops 202767360 | bytes 8192 | tf_op jit(solution)/shard_map/dot_general | solution.py:196
  2.1 1.2 select_reduce_fusion
  3.3 0.8 all_to_all.15
  4.1 21.8 %all-to-all-start = ((s32[96,1,22]{2,1,0:T(1,128)}), s32[96,1,22]{2,1,0:T(1,128)S(1)}, u32[]{:S(2)}, u32[]{:S(2)}) async-start(s32[96,1,22]{2,1,0:T(1,128)} %bitcast.6), calls=%async_computation | async-start | bytes 98304 | tf_op jit(solution)/shard_map/all_to_all | solution.py:203
  26.2 0.6 maximum_multiply_fusion.weight_ref
  26.8 12.7 %all-to-all-done = s32[96,1,22]{2,1,0:T(1,128)S(1)} async-done(((s32[96,1,22]{2,1,0:T(1,128)}), s32[96,1,22]{2,1,0:T(1,128)S(1)}, u32[]{:S(2)}, u32[]{:S(2)}) %all-to-all-start) | async-done | bytes 8480 | tf_op jit(solution)/shard_map/all_to_all | solution.py:203
  39.4 0.5 broadcast.305
  40.0 0.8 reduce.7
  40.9 3.2 %fusion.1 = f32[9,2112]{1,0:T(8,128)S(1)} fusion(s32[2112]{0:T(1024)S(1)} %eq.85, bf16[3,2048]{1,0:T(4,128)(2,1)S(1)} %get-tuple-element.17, bf16[3,2048]{1,0:T(4,128)(2,1)S(1)} %get-tuple-element.18, bf16[3,2048]{1,0:T(4,128)(2,1)S(1)} %get-tuple-element.16), kind=kOutput, calls=%fused_computation.2 | convolution fusion | flops 82292736 | bytes 121344 | tf_op jit(solution)/shard_map/dot_general | solution.py:168
  44.1 0.2 reshape.199
  44.2 0.8 copy.16
  45.0 6.3 %all-to-all-start.1 = ((f32[3,96,22]{2,0,1:T(4,128)}), f32[3,96,22]{2,0,1:T(4,128)S(1)}, u32[]{:S(2)}, u32[]{:S(2)}) async-start(f32[3,96,22]{2,0,1:T(4,128)} %copy.16), calls=%async_computation.1 | async-start | bytes 393216 | tf_op jit(solution)/shard_map/all_to_all | solution.py:211
  51.4 0.6 pad_maximum_fusion.4.speed_ref
  52.0 15.6 %all-to-all-done.1 = f32[3,96,22]{2,0,1:T(4,128)S(1)} async-done(((f32[3,96,22]{2,0,1:T(4,128)}), f32[3,96,22]{2,0,1:T(4,128)S(1)}, u32[]{:S(2)}, u32[]{:S(2)}) %all-to-all-start.1) | async-done | bytes 25376 | tf_op jit(solution)/shard_map/all_to_all | solution.py:211
  67.8 1.6 %fusion.5 = f32[9,1024]{1,0:T(8,128)S(1)} fusion(s32[1024]{0:T(1024)S(1)} %multiply_add_fusion, bf16[3,2112]{1,0:T(4,128)(2,1)S(1)} %get-tuple-element.14, bf16[3,2112]{1,0:T(4,128)(2,1)S(1)} %get-tuple-element.15, bf16[3,2112]{1,0:T(4,128)(2,1)S(1)} %get-tuple-element.13), kind=kOutput, calls=%fused_computation.7 | convolution fusion | flops 41205120 | bytes 78976 | tf_op jit(solution)/shard_map/dot_general | solution.py:168
  69.6 3.1 %collective-permute-start.1 = (f32[165,4,128]{2,1,0:T(4,128)S(1)}, f32[165,4,128]{2,1,0:T(4,128)S(1)}, u32[]{:S(2)}, u32[]{:S(2)}) collective-permute-start(f32[165,4,128]{2,1,0:T(4,128)S(1)} %get-tuple-element.8), channel_id=1, source_target_pairs={{1,0},{2,1},{3,2},{4,3},{5,4},{6,5},{7,6},{8,7},{9,8},{10,9},{11,1... | collective-permute-start | bytes 1013768 | tf_op jit(solution)/shard_map/ppermute | solution.py:156
  72.7 2.9 %collective-permute-start = (f32[165,4,128]{2,1,0:T(4,128)S(1)}, f32[165,4,128]{2,1,0:T(4,128)S(1)}, u32[]{:S(2)}, u32[]{:S(2)}) collective-permute-start(f32[165,4,128]{2,1,0:T(4,128)S(1)} %get-tuple-element.9), channel_id=1, source_target_pairs={{0,1},{1,2},{2,3},{3,4},{4,5},{5,6},{6,7},{7,8},{8,9},{9,10},{10,1... | collective-permute-start | bytes 1013768 | tf_op jit(solution)/shard_map/ppermute | solution.py:156
  75.7 0.6 pad_maximum_fusion.3.flow_ref
  76.3 0.6 convert_multiply_fusion.factor_ref
  76.9 1.8 %collective-permute-done.1.after_ref.flow_after_ref = f32[165,4,128]{2,1,0:T(4,128)S(1)} collective-permute-done((f32[165,4,128]{2,1,0:T(4,128)S(1)}, f32[165,4,128]{2,1,0:T(4,128)S(1)}, u32[]{:S(2)}, u32[]{:S(2)}) %collective-permute-start.1) | collective-permute-done | bytes 337952 | tf_op jit(solution)/shard_map/ppermute | solution.py:156
  78.7 3.1 %collective-permute-done.before_ref.flow_before_ref = f32[165,4,128]{2,1,0:T(4,128)S(1)} collective-permute-done((f32[165,4,128]{2,1,0:T(4,128)S(1)}, f32[165,4,128]{2,1,0:T(4,128)S(1)}, u32[]{:S(2)}, u32[]{:S(2)}) %collective-permute-start) | collective-permute-done | bytes 337952 | tf_op jit(solution)/shard_map/ppermute | solution.py:156
  81.8 0.7 copy-done.2
  82.5 7.4 %shard_map.95 = (f32[162,8,128]{2,1,0:T(8,128)}, f32[8,3,8,128]{3,2,1,0:T(8,128)}) custom-call(f32[2,162]{1,0:T(2,128)} %pad_maximum_fusion.4.speed_ref, f32[3,162]{1,0:T(4,128)} %maximum_multiply_fusion.weight_ref, f32[162,8,128]{2,1,0:T(8,128)} %energy_ref.1, f32[3,8,128]{2,1,0:T(8,128)} %pad_maximum_fusion.3.flow_ref, f32[165,4,128]{2,1,0:T(4,128)} %copy-done.2, ...), custom_call_target="tpu_custom_call" | custom-call | tf_op jit(solution)/shard_map/pallas_call | solution.py:121
  90.0 4.3 %all-to-all-start.2 = ((f32[8,3,8,128]{3,2,1,0:T(8,128)}), f32[8,3,8,128]{3,2,1,0:T(8,128)S(1)}, u32[]{:S(2)}, u32[]{:S(2)}) async-start(f32[8,3,8,128]{3,2,1,0:T(8,128)} %get-tuple-element.5), calls=%async_computation.2 | async-start | bytes 196608 | tf_op jit(solution)/shard_map/all_to_all | solution.py:231
  94.3 5.8 %all-to-all-done.2 = f32[8,3,8,128]{3,2,1,0:T(8,128)S(1)} async-done(((f32[8,3,8,128]{3,2,1,0:T(8,128)}), f32[8,3,8,128]{3,2,1,0:T(8,128)S(1)}, u32[]{:S(2)}, u32[]{:S(2)}) %all-to-all-start.2) | async-done | bytes 98336 | tf_op jit(solution)/shard_map/all_to_all | solution.py:231
  100.1 1.5 %fusion.4 = f32[9,2112]{1,0:T(8,128)S(1)} fusion(s32[1024]{0:T(1024)S(1)} %multiply_add_fusion, bf16[3,1024]{1,0:T(4,128)(2,1)S(1)} %get-tuple-element.20, bf16[3,1024]{1,0:T(4,128)(2,1)S(1)} %get-tuple-element.21, bf16[3,1024]{1,0:T(4,128)(2,1)S(1)} %get-tuple-element.19), kind=kOutput, calls=%fused_computation.6 | convolution fusion | flops 41146368 | bytes 98560 | tf_op jit(solution)/shard_map/dot_general | solution.py:168
  101.7 0.2 reshape.202
  101.9 0.8 copy.18
  102.6 8.8 %all-to-all-start.3 = ((f32[3,96,22]{2,0,1:T(4,128)}), f32[3,96,22]{2,0,1:T(4,128)S(1)}, u32[]{:S(2)}, u32[]{:S(2)}) async-start(f32[3,96,22]{2,0,1:T(4,128)} %copy.18), calls=%async_computation.3 | async-start | bytes 393216 | tf_op jit(solution)/shard_map/all_to_all | solution.py:237
  111.8 16.9 %all-to-all-done.3 = f32[3,96,22]{2,0,1:T(4,128)S(1)} async-done(((f32[3,96,22]{2,0,1:T(4,128)}), f32[3,96,22]{2,0,1:T(4,128)S(1)}, u32[]{:S(2)}, u32[]{:S(2)}) %all-to-all-start.3) | async-done | bytes 25376 | tf_op jit(solution)/shard_map/all_to_all | solution.py:237
  128.9 3.2 %fusion = f32[12,2048]{1,0:T(8,128)S(1)} fusion(s32[2112]{0:T(1024)S(1)} %eq.85, bf16[4,2112]{1,0:T(4,128)(2,1)S(1)} %get-tuple-element.12, bf16[4,2112]{1,0:T(4,128)(2,1)S(1)} %get-tuple-element.11, bf16[4,2112]{1,0:T(4,128)(2,1)S(1)} %get-tuple-element.10), kind=kOutput, calls=%fused_computation.1 | convolution fusion | flops 108286464 | bytes 157440 | tf_op jit(solution)/shard_map/dot_general | solution.py:168
  132.1 0.6 slice_divide_fusion
  (50 shorter events, 1.4 us)
Async XLA Ops:
  0.6 1.4 %copy-start.3 = (s32[1024,1]{0,1:T(1,128)S(1)}, s32[1024,1]{0,1:T(1,128)}, u32[]{:S(2)}) copy-start(s32[1024,1]{0,1:T(1,128)} %param.14) | copy-start | bytes 12292
  0.6 1.4 %copy-start.9 = (s32[1024]{0:T(1024)S(1)}, s32[1024]{0:T(1024)}, u32[]{:S(2)}) copy-start(s32[1024]{0:T(1024)} %param.15) | copy-start | bytes 12292
  0.7 25.3 %copy-start.4 = (s32[8,128]{1,0:T(8,128)S(1)}, s32[8,128]{1,0:T(8,128)}, u32[]{:S(2)}) copy-start(s32[8,128]{1,0:T(8,128)} %param.13) | copy-start | bytes 12292
  0.7 25.3 %copy-start.7 = (f32[36]{0:T(128)S(1)}, f32[36]{0:T(128)}, u32[]{:S(2)}) copy-start(f32[36]{0:T(128)} %param.10) | copy-start | bytes 436
  0.7 25.3 %copy-start.8 = (f32[36]{0:T(128)S(1)}, f32[36]{0:T(128)}, u32[]{:S(2)}) copy-start(f32[36]{0:T(128)} %param.9) | copy-start | bytes 436
  0.7 25.4 %copy-start.5 = (f32[2,2048]{1,0:T(2,128)S(1)}, f32[2,2048]{1,0:T(2,128)}, u32[]{:S(2)}) copy-start(f32[2,2048]{1,0:T(2,128)} %param.11) | copy-start | bytes 49156
  0.7 25.4 %copy-start.6 = (f32[2048]{0:T(1024)S(1)}, f32[2048]{0:T(1024)}, u32[]{:S(2)}) copy-start(f32[2048]{0:T(1024)} %param.12) | copy-start | bytes 24580
  4.1 35.4 %all-to-all-start = ((s32[96,1,22]{2,1,0:T(1,128)}), s32[96,1,22]{2,1,0:T(1,128)S(1)}, u32[]{:S(2)}, u32[]{:S(2)}) async-start(s32[96,1,22]{2,1,0:T(1,128)} %bitcast.6), calls=%async_computation | async-start | bytes 98304 | tf_op jit(solution)/shard_map/all_to_all | solution.py:203
  45.0 22.6 %all-to-all-start.1 = ((f32[3,96,22]{2,0,1:T(4,128)}), f32[3,96,22]{2,0,1:T(4,128)S(1)}, u32[]{:S(2)}, u32[]{:S(2)}) async-start(f32[3,96,22]{2,0,1:T(4,128)} %copy.16), calls=%async_computation.1 | async-start | bytes 393216 | tf_op jit(solution)/shard_map/all_to_all | solution.py:211
  67.8 1.6 %copy-start = (f32[162,8,128]{2,1,0:T(8,128)S(1)}, f32[162,8,128]{2,1,0:T(8,128)}, u32[]{:S(2)}) copy-start(f32[162,8,128]{2,1,0:T(8,128)} %energy_ref.1) | copy-start | bytes 1990660
  69.6 9.1 %collective-permute-start.1 = (f32[165,4,128]{2,1,0:T(4,128)S(1)}, f32[165,4,128]{2,1,0:T(4,128)S(1)}, u32[]{:S(2)}, u32[]{:S(2)}) collective-permute-start(f32[165,4,128]{2,1,0:T(4,128)S(1)} %get-tuple-element.8), channel_id=1, source_target_pairs={{1,0},{2,1},{3,2},{4,3},{5,4},{6,5},{7,6},{8,7},{9,8},{10,9},{11,1... | collective-permute-start | bytes 1013768 | tf_op jit(solution)/shard_map/ppermute | solution.py:156
  72.7 9.1 %collective-permute-start = (f32[165,4,128]{2,1,0:T(4,128)S(1)}, f32[165,4,128]{2,1,0:T(4,128)S(1)}, u32[]{:S(2)}, u32[]{:S(2)}) collective-permute-start(f32[165,4,128]{2,1,0:T(4,128)S(1)} %get-tuple-element.9), channel_id=1, source_target_pairs={{0,1},{1,2},{2,3},{3,4},{4,5},{5,6},{6,7},{7,8},{8,9},{9,10},{10,1... | collective-permute-start | bytes 1013768 | tf_op jit(solution)/shard_map/ppermute | solution.py:156
  78.7 3.1 %copy-start.1 = (f32[165,4,128]{2,1,0:T(4,128)}, f32[165,4,128]{2,1,0:T(4,128)S(1)}, u32[]{:S(2)}) copy-start(f32[165,4,128]{2,1,0:T(4,128)S(1)} %collective-permute-done.1.after_ref.flow_after_ref) | copy-start | bytes 1013764
  81.8 0.7 copy-start.2
  90.0 10.1 %all-to-all-start.2 = ((f32[8,3,8,128]{3,2,1,0:T(8,128)}), f32[8,3,8,128]{3,2,1,0:T(8,128)S(1)}, u32[]{:S(2)}, u32[]{:S(2)}) async-start(f32[8,3,8,128]{3,2,1,0:T(8,128)} %get-tuple-element.5), calls=%async_computation.2 | async-start | bytes 196608 | tf_op jit(solution)/shard_map/all_to_all | solution.py:231
  102.6 26.0 %all-to-all-start.3 = ((f32[3,96,22]{2,0,1:T(4,128)}), f32[3,96,22]{2,0,1:T(4,128)S(1)}, u32[]{:S(2)}, u32[]{:S(2)}) async-start(f32[3,96,22]{2,0,1:T(4,128)} %copy.18), calls=%async_computation.3 | async-start | bytes 393216 | tf_op jit(solution)/shard_map/all_to_all | solution.py:237

commit v17 on v16

--- a/solution.py
+++ b/solution.py
@@ -237,9 +237,9 @@
     arrived = lax.all_to_all(
         packed.reshape(3, tile_count, capacity), "tile", split_axis=1, concat_axis=1, tiled=True
     )
-    weight = is_valid.reshape(-1).astype(jnp.float32)
     summed = pick_matmul(
-        jnp.concatenate([arrived.reshape(3, -1) * weight[None], weight[None]], 0), slot_pick.T
+        jnp.concatenate([arrived.reshape(3, -1), jnp.ones_like(arrived.reshape(3, -1)[:1])], 0),
+        slot_pick.T,
     )
     return (energy, summed[:3] / jnp.maximum(summed[3], 1.0)[None])
 

time: 133 us -> 132 us (level)
  blocking collectives: 0 us -> 35.9 us
  waiting for transfers between devices: 55.9 us -> 33.3 us
  starting transfers between devices: 47.3 us -> 34.1 us
    all_to_all x0 -> x2, blocking collectives: none -> 35.9 us  [the longest x1 25.8 us: local(): lax.all_to_all(packed.reshape(3, tile_count, capacity), 'tile', split_axi...]
    all_to_all x2 -> x0, waiting for transfers between devices: 22.7 us -> none  [the longest x1 16.9 us: local(): lax.all_to_all(packed.reshape(3, tile_count, capacity), 'tile', split_axi...]
    all_to_all x2 -> x0, starting transfers between devices: 13.1 us -> none  [the longest x1 8.82 us: local(): lax.all_to_all(packed.reshape(3, tile_count, capacity), 'tile', split_axi...]
  transfers between devices with their start and end apart: 6 -> 4, of which waited for: 6 -> 4; matrix products, arithmetic and copies ran while one was open for 2% -> 2% of each run, Pallas kernels for 0% -> 0%
where the time goes in v17:
time: 132 us
  blocking collectives  35.9 us (27%)
  starting transfers between devices  34.1 us (26%)
  waiting for transfers between devices  33.3 us (25%)
  matrix products  10.8 us (8%)
  Pallas kernels  7.44 us (6%)
  other arithmetic  5.46 us (4%)
  local copies, waits for them, and re-layouts  3.83 us (3%)
    all_to_all x1, blocking collectives, local(): lax.all_to_all(packed.reshape(3, tile_count, capacity), 'tile', split_axi...  25.8 us
    all_to_all x1, starting transfers between devices, local(): lax.all_to_all(requests.reshape(tile_count, capacity), 'tile', split_axis...  21.8 us
    all_to_all x1, waiting for transfers between devices, local(): lax.all_to_all(answer, 'tile', split_axis=1, concat_axis=1, tiled=True)  15.7 us
    all_to_all x1, waiting for transfers between devices, local(): lax.all_to_all(requests.reshape(tile_count, capacity), 'tile', split_axis...  12.7 us
    all_to_all x1, blocking collectives, local(): every_part = lax.all_to_all(partial_copies, 'sect', 0, 0, tiled=True)  10.1 us
    dot_general x4, matrix products, pick_matmul(): product = jnp.dot(stacked, pick, preferred_element_type=jnp.float32)  9.46 us
    pallas_call x1, Pallas kernels, propagate(): pl.pallas_call(kernel, grid=(bins // block,), in_specs=[pl.BlockSpec(memo...  7.44 us
    all_to_all x1, starting transfers between devices, local(): lax.all_to_all(answer, 'tile', split_axis=1, concat_axis=1, tiled=True)  6.35 us
  transfers between devices with their start and end apart: 4, of which 4 were waited for; matrix products, arithmetic and copies ran while one was open for 2% of the time, Pallas kernels for 0%

profile of v17, /device:TPU:8, one launch (start us, length us, event | category | flops | bytes accessed | tf_op | source)
XLA Modules:
  0.0 131.8 jit_solution(1380523413796248317)
XLA Ops:
  0.7 1.3 %fusion.10 = f32[1024]{0:T(1024)S(1)} fusion(s32[1024]{0:T(1024)} %bitcast.29), kind=kOutput, calls=%fused_computation.15 | convolution fusion | flops 202767360 | bytes 8192 | tf_op jit(solution)/shard_map/dot_general | solution.py:196
  2.1 1.2 select_reduce_fusion
  3.3 0.8 all_to_all.15
  4.1 21.8 %all-to-all-start = ((s32[96,1,22]{2,1,0:T(1,128)}), s32[96,1,22]{2,1,0:T(1,128)S(1)}, u32[]{:S(2)}, u32[]{:S(2)}) async-start(s32[96,1,22]{2,1,0:T(1,128)} %bitcast.6), calls=%async_computation | async-start | bytes 98304 | tf_op jit(solution)/shard_map/all_to_all | solution.py:203
  26.2 0.6 maximum_multiply_fusion.weight_ref
  26.8 12.7 %all-to-all-done = s32[96,1,22]{2,1,0:T(1,128)S(1)} async-done(((s32[96,1,22]{2,1,0:T(1,128)}), s32[96,1,22]{2,1,0:T(1,128)S(1)}, u32[]{:S(2)}, u32[]{:S(2)}) %all-to-all-start) | async-done | bytes 8480 | tf_op jit(solution)/shard_map/all_to_all | solution.py:203
  39.4 0.5 broadcast.293
  40.0 0.8 reduce.3
  40.7 0.1 eq.85
  40.9 3.2 %fusion.1 = f32[9,2112]{1,0:T(8,128)S(1)} fusion(s32[2112]{0:T(1024)S(1)} %eq.85, bf16[3,2048]{1,0:T(4,128)(2,1)S(1)} %get-tuple-element.17, bf16[3,2048]{1,0:T(4,128)(2,1)S(1)} %get-tuple-element.18, bf16[3,2048]{1,0:T(4,128)(2,1)S(1)} %get-tuple-element.16), kind=kOutput, calls=%fused_computation.2 | convolution fusion | flops 82292736 | bytes 121344 | tf_op jit(solution)/shard_map/dot_general | solution.py:168
  44.1 0.2 reshape.179
  44.2 0.8 copy.16
  45.0 6.3 %all-to-all-start.1 = ((f32[3,96,22]{2,0,1:T(4,128)}), f32[3,96,22]{2,0,1:T(4,128)S(1)}, u32[]{:S(2)}, u32[]{:S(2)}) async-start(f32[3,96,22]{2,0,1:T(4,128)} %copy.16), calls=%async_computation.1 | async-start | bytes 393216 | tf_op jit(solution)/shard_map/all_to_all | solution.py:211
  51.4 0.6 pad_maximum_fusion.3.speed_ref
  52.0 15.7 %all-to-all-done.1 = f32[3,96,22]{2,0,1:T(4,128)S(1)} async-done(((f32[3,96,22]{2,0,1:T(4,128)}), f32[3,96,22]{2,0,1:T(4,128)S(1)}, u32[]{:S(2)}, u32[]{:S(2)}) %all-to-all-start.1) | async-done | bytes 25376 | tf_op jit(solution)/shard_map/all_to_all | solution.py:211
  67.6 0.2 reshape.180
  67.8 1.6 %fusion.5 = f32[9,1024]{1,0:T(8,128)S(1)} fusion(s32[1024]{0:T(1024)S(1)} %multiply_add_fusion, bf16[3,2112]{1,0:T(4,128)(2,1)S(1)} %get-tuple-element.14, bf16[3,2112]{1,0:T(4,128)(2,1)S(1)} %get-tuple-element.15, bf16[3,2112]{1,0:T(4,128)(2,1)S(1)} %get-tuple-element.13), kind=kOutput, calls=%fused_computation.7 | convolution fusion | flops 41205120 | bytes 78976 | tf_op jit(solution)/shard_map/dot_general | solution.py:168
  69.6 3.1 %collective-permute-start.1 = (f32[165,4,128]{2,1,0:T(4,128)S(1)}, f32[165,4,128]{2,1,0:T(4,128)S(1)}, u32[]{:S(2)}, u32[]{:S(2)}) collective-permute-start(f32[165,4,128]{2,1,0:T(4,128)S(1)} %get-tuple-element.8), channel_id=1, source_target_pairs={{1,0},{2,1},{3,2},{4,3},{5,4},{6,5},{7,6},{8,7},{9,8},{10,9},{11,1... | collective-permute-start | bytes 1013768 | tf_op jit(solution)/shard_map/ppermute | solution.py:156
  72.7 2.9 %collective-permute-start = (f32[165,4,128]{2,1,0:T(4,128)S(1)}, f32[165,4,128]{2,1,0:T(4,128)S(1)}, u32[]{:S(2)}, u32[]{:S(2)}) collective-permute-start(f32[165,4,128]{2,1,0:T(4,128)S(1)} %get-tuple-element.9), channel_id=1, source_target_pairs={{0,1},{1,2},{2,3},{3,4},{4,5},{5,6},{6,7},{7,8},{8,9},{9,10},{10,1... | collective-permute-start | bytes 1013768 | tf_op jit(solution)/shard_map/ppermute | solution.py:156
  75.7 0.6 pad_maximum_fusion.2.flow_ref
  76.3 0.6 convert_multiply_fusion.factor_ref
  76.9 1.8 %collective-permute-done.1.after_ref.flow_after_ref = f32[165,4,128]{2,1,0:T(4,128)S(1)} collective-permute-done((f32[165,4,128]{2,1,0:T(4,128)S(1)}, f32[165,4,128]{2,1,0:T(4,128)S(1)}, u32[]{:S(2)}, u32[]{:S(2)}) %collective-permute-start.1) | collective-permute-done | bytes 337952 | tf_op jit(solution)/shard_map/ppermute | solution.py:156
  78.7 3.1 %collective-permute-done.before_ref.flow_before_ref = f32[165,4,128]{2,1,0:T(4,128)S(1)} collective-permute-done((f32[165,4,128]{2,1,0:T(4,128)S(1)}, f32[165,4,128]{2,1,0:T(4,128)S(1)}, u32[]{:S(2)}, u32[]{:S(2)}) %collective-permute-start) | collective-permute-done | bytes 337952 | tf_op jit(solution)/shard_map/ppermute | solution.py:156
  81.8 0.7 copy-done.2
  82.6 7.4 %shard_map.95 = (f32[162,8,128]{2,1,0:T(8,128)}, f32[8,3,8,128]{3,2,1,0:T(8,128)}) custom-call(f32[2,162]{1,0:T(2,128)} %pad_maximum_fusion.3.speed_ref, f32[3,162]{1,0:T(4,128)} %maximum_multiply_fusion.weight_ref, f32[162,8,128]{2,1,0:T(8,128)} %energy_ref.1, f32[3,8,128]{2,1,0:T(8,128)} %pad_maximum_fusion.2.flow_ref, f32[165,4,128]{2,1,0:T(4,128)} %copy-done.2, ...), custom_call_target="tpu_custom_call" | custom-call | tf_op jit(solution)/shard_map/pallas_call | solution.py:121
  90.0 10.1 %all_to_all.24 = f32[8,3,8,128]{3,2,1,0:T(8,128)S(1)} all-to-all(f32[8,3,8,128]{3,2,1,0:T(8,128)} %get-tuple-element.5), channel_id=1, replica_groups=mesh['sect'=8,'tile'=96] {'sect'}, dimensions={0} | all-to-all | bytes 196608 | tf_op jit(solution)/shard_map/all_to_all | solution.py:231
  100.1 1.5 %fusion.4 = f32[9,2112]{1,0:T(8,128)S(1)} fusion(s32[1024]{0:T(1024)S(1)} %multiply_add_fusion, bf16[3,1024]{1,0:T(4,128)(2,1)S(1)} %get-tuple-element.20, bf16[3,1024]{1,0:T(4,128)(2,1)S(1)} %get-tuple-element.21, bf16[3,1024]{1,0:T(4,128)(2,1)S(1)} %get-tuple-element.19), kind=kOutput, calls=%fused_computation.6 | convolution fusion | flops 41146368 | bytes 98560 | tf_op jit(solution)/shard_map/dot_general | solution.py:168
  101.7 0.2 reshape.182
  102.0 25.8 %all_to_all.25 = f32[3,96,22]{2,0,1:T(4,128)S(1)} all-to-all(f32[3,96,22]{2,0,1:T(4,128)S(1)} %copy.18), channel_id=1, replica_groups=mesh['sect'=8,'tile'=96] {'tile'}, dimensions={1} | all-to-all | bytes 50688 | tf_op jit(solution)/shard_map/all_to_all | solution.py:237
  127.8 0.2 reshape.183
  128.0 3.2 %fusion = f32[12,2048]{1,0:T(8,128)S(1)} fusion(s32[2112]{0:T(1024)S(1)} %eq.85, bf16[4,2112]{1,0:T(4,128)(2,1)S(1)} %get-tuple-element.11, bf16[4,2112]{1,0:T(4,128)(2,1)S(1)} %get-tuple-element.12, bf16[4,2112]{1,0:T(4,128)(2,1)S(1)} %get-tuple-element.10), kind=kOutput, calls=%fused_computation.1 | convolution fusion | flops 108286464 | bytes 157440 | tf_op jit(solution)/shard_map/dot_general | solution.py:168
  131.2 0.6 slice_divide_fusion
  (44 shorter events, 0.7 us)
Async XLA Ops:
  0.6 1.4 %copy-start.3 = (s32[1024,1]{0,1:T(1,128)S(1)}, s32[1024,1]{0,1:T(1,128)}, u32[]{:S(2)}) copy-start(s32[1024,1]{0,1:T(1,128)} %param.14) | copy-start | bytes 12292
  0.6 1.4 %copy-start.9 = (s32[1024]{0:T(1024)S(1)}, s32[1024]{0:T(1024)}, u32[]{:S(2)}) copy-start(s32[1024]{0:T(1024)} %param.15) | copy-start | bytes 12292
  0.7 25.3 %copy-start.4 = (s32[8,128]{1,0:T(8,128)S(1)}, s32[8,128]{1,0:T(8,128)}, u32[]{:S(2)}) copy-start(s32[8,128]{1,0:T(8,128)} %param.13) | copy-start | bytes 12292
  0.7 25.3 %copy-start.7 = (f32[36]{0:T(128)S(1)}, f32[36]{0:T(128)}, u32[]{:S(2)}) copy-start(f32[36]{0:T(128)} %param.10) | copy-start | bytes 436
  0.7 25.3 %copy-start.8 = (f32[36]{0:T(128)S(1)}, f32[36]{0:T(128)}, u32[]{:S(2)}) copy-start(f32[36]{0:T(128)} %param.9) | copy-start | bytes 436
  0.7 25.4 %copy-start.5 = (f32[2,2048]{1,0:T(2,128)S(1)}, f32[2,2048]{1,0:T(2,128)}, u32[]{:S(2)}) copy-start(f32[2,2048]{1,0:T(2,128)} %param.11) | copy-start | bytes 49156
  0.7 25.4 %copy-start.6 = (f32[2048]{0:T(1024)S(1)}, f32[2048]{0:T(1024)}, u32[]{:S(2)}) copy-start(f32[2048]{0:T(1024)} %param.12) | copy-start | bytes 24580
  4.1 35.4 %all-to-all-start = ((s32[96,1,22]{2,1,0:T(1,128)}), s32[96,1,22]{2,1,0:T(1,128)S(1)}, u32[]{:S(2)}, u32[]{:S(2)}) async-start(s32[96,1,22]{2,1,0:T(1,128)} %bitcast.6), calls=%async_computation | async-start | bytes 98304 | tf_op jit(solution)/shard_map/all_to_all | solution.py:203
  45.0 22.6 %all-to-all-start.1 = ((f32[3,96,22]{2,0,1:T(4,128)}), f32[3,96,22]{2,0,1:T(4,128)S(1)}, u32[]{:S(2)}, u32[]{:S(2)}) async-start(f32[3,96,22]{2,0,1:T(4,128)} %copy.16), calls=%async_computation.1 | async-start | bytes 393216 | tf_op jit(solution)/shard_map/all_to_all | solution.py:211
  67.8 1.6 %copy-start = (f32[162,8,128]{2,1,0:T(8,128)S(1)}, f32[162,8,128]{2,1,0:T(8,128)}, u32[]{:S(2)}) copy-start(f32[162,8,128]{2,1,0:T(8,128)} %energy_ref.1) | copy-start | bytes 1990660
  69.6 9.1 %collective-permute-start.1 = (f32[165,4,128]{2,1,0:T(4,128)S(1)}, f32[165,4,128]{2,1,0:T(4,128)S(1)}, u32[]{:S(2)}, u32[]{:S(2)}) collective-permute-start(f32[165,4,128]{2,1,0:T(4,128)S(1)} %get-tuple-element.8), channel_id=1, source_target_pairs={{1,0},{2,1},{3,2},{4,3},{5,4},{6,5},{7,6},{8,7},{9,8},{10,9},{11,1... | collective-permute-start | bytes 1013768 | tf_op jit(solution)/shard_map/ppermute | solution.py:156
  72.7 9.1 %collective-permute-start = (f32[165,4,128]{2,1,0:T(4,128)S(1)}, f32[165,4,128]{2,1,0:T(4,128)S(1)}, u32[]{:S(2)}, u32[]{:S(2)}) collective-permute-start(f32[165,4,128]{2,1,0:T(4,128)S(1)} %get-tuple-element.9), channel_id=1, source_target_pairs={{0,1},{1,2},{2,3},{3,4},{4,5},{5,6},{6,7},{7,8},{8,9},{9,10},{10,1... | collective-permute-start | bytes 1013768 | tf_op jit(solution)/shard_map/ppermute | solution.py:156
  78.7 3.1 %copy-start.1 = (f32[165,4,128]{2,1,0:T(4,128)}, f32[165,4,128]{2,1,0:T(4,128)S(1)}, u32[]{:S(2)}) copy-start(f32[165,4,128]{2,1,0:T(4,128)S(1)} %collective-permute-done.1.after_ref.flow_after_ref) | copy-start | bytes 1013764
  81.8 0.7 copy-start.2
